TPU v7x, 512 devices: a whole 4x4x16 slice. The times are simulated.
512 devices in a mesh: team: 128 (over x_lo, y, z), rep: 4 (over x_hi, core).
Axes of the slice: x: 4 (x_hi: 2, x_lo: 2; x = x_hi * 2 + x_lo), y: 4, z: 16, core: 2. Of those that a mesh axis runs over, the one named last changes fastest.
Arguments:
- features: bfloat16 [131072, 128], P('team'), may hold values from -6 to 6
- weight: bfloat16 [128, 128], replicated, may hold values from -0.5 to 0.5
- out_grad: bfloat16 [131072, 128], P(('team', 'rep')), may hold values from -6 to 6
- tiles: bfloat16 [1024, 5, 8, 128, 128], P(('team', 'rep')), may hold values from -0.125 to 0.125
- coords: int32 [1024, 5, 8], P(('team', 'rep')), may hold values from 0 to 7, as said below
- counts: int32 [1024, 5], P(('team', 'rep')), may hold values from 1 to 8, as said below
Outputs:
- activated: bfloat16 [131072, 128], P(('team', 'rep'))
- grad_weight: float32 [128, 128], replicated
- grad_features: bfloat16 [131072, 128], P(('team', 'rep'))
Inputs may be any that keep to these rules, and one draw needn't show every extreme that they name: `coords`: the live and dead slots of one panel and section name distinct column tiles. `counts`: in every draw all panels of some team have 8 live slots for every section.
All inputs are finite; a program needn't handle non-finite values.
Results may differ from a plain program's by a relative error of at most 0.013.
Values may be sent and summed in bfloat16 or wider, within the bound.
No kernel may reach another device: no remote copies, remote signals or barrier semaphores. Data moves between devices by JAX's collectives and lax.ppermute only.
A program may use at most 64 MiB of HBM per device.

v0:
```python
import math

import jax
import jax.numpy as jnp
from jax import lax
from jax.sharding import PartitionSpec as P


def from_behind(block, axis, distance):
    devices = range(lax.axis_size(axis))
    route = [((i - distance) % len(devices), i) for i in devices]
    return lax.ppermute(block, axis, route)


def neighbour_blocks(features, reach_size):
    blocks = {0: features}
    ahead_block = features
    behind_block = features
    for offset in range(1, reach_size + 1):
        ahead_block = from_behind(ahead_block, "team", -1)
        behind_block = from_behind(behind_block, "team", 1)
        blocks[offset] = ahead_block
        blocks[-offset] = behind_block
    return blocks


def deliver(pieces, reach_size):
    combined = pieces[0]
    upward = pieces[reach_size]
    downward = pieces[-reach_size]
    for step_index in range(reach_size):
        upward = from_behind(upward.astype(jnp.bfloat16), "team", 1).astype(upward.dtype)
        downward = from_behind(downward.astype(jnp.bfloat16), "team", -1).astype(downward.dtype)
        if step_index < reach_size - 1:
            upward = upward + pieces[reach_size - 1 - step_index]
            downward = downward + pieces[-(reach_size - 1 - step_index)]
    combined = combined + upward + downward
    return combined


def aggregate(running, source_tiles, section_tiles, section_coords, section_live, slot_bound):

    def aggregate_add_slot(slot_index, partial_rows):
        column_tile = lax.dynamic_index_in_dim(section_coords, slot_index, 1, keepdims=False)
        picked = jnp.take(source_tiles, column_tile, axis=0)
        current = lax.dynamic_index_in_dim(section_tiles, slot_index, 1, keepdims=False)
        keep_mask = lax.dynamic_index_in_dim(section_live, slot_index, 1, keepdims=False)
        current = jnp.where(keep_mask[:, None, None], current, jnp.zeros_like(current))
        return partial_rows + jnp.einsum(
            "pab,pbf->paf", current, picked, preferred_element_type=jnp.float32
        )

    return lax.fori_loop(0, slot_bound, aggregate_add_slot, running)


def spread(back_tiles, section_tiles, section_coords, section_live, slot_bound, column_count):
    panel_dev, _, tile_size, _ = section_tiles.shape
    feature_width = back_tiles.shape[2]

    def spread_add_slot(slot_index, partial_sums):
        column_tile = lax.dynamic_index_in_dim(section_coords, slot_index, 1, keepdims=False)
        current = lax.dynamic_index_in_dim(section_tiles, slot_index, 1, keepdims=False)
        keep_mask = lax.dynamic_index_in_dim(section_live, slot_index, 1, keepdims=False)
        current = jnp.where(keep_mask[:, None, None], current, jnp.zeros_like(current))
        contrib = jnp.einsum(
            "pab,paf->pbf", current, back_tiles, preferred_element_type=jnp.float32
        )
        return partial_sums.at[column_tile].add(contrib)

    initial = jnp.zeros((column_count, tile_size, feature_width), jnp.float32)
    return lax.fori_loop(0, slot_bound, spread_add_slot, initial)


def body(features, weight, out_grad, tiles, coords, counts):
    panel_dev, section_count, slot_count, tile_size, _ = tiles.shape
    team_rows, feature_width = features.shape
    column_count = team_rows // tile_size
    reach_size = (section_count - 1) // 2
    nodes_total = team_rows * lax.axis_size("team")
    live_slots = lax.broadcasted_iota(jnp.int32, coords.shape, 2) < counts[:, :, None]
    slot_bounds = jnp.max(counts, axis=0)
    blocks = neighbour_blocks(features, reach_size)
    running = jnp.zeros((panel_dev, tile_size, feature_width), jnp.float32)
    for section_index in range(section_count):
        source_tiles = blocks[section_index - reach_size].reshape(
            column_count, tile_size, feature_width
        )
        running = aggregate(
            running,
            source_tiles,
            tiles[:, section_index],
            coords[:, section_index],
            live_slots[:, section_index],
            slot_bounds[section_index],
        )
    aggregated = running.reshape(-1, feature_width).astype(jnp.bfloat16)
    pre_act = jnp.dot(aggregated, weight, preferred_element_type=jnp.float32)
    sigmoid_value = jax.nn.sigmoid(pre_act)
    activated = (pre_act * sigmoid_value).astype(jnp.bfloat16)
    gate_grad = (
        out_grad.astype(jnp.float32) * sigmoid_value * (1.0 + pre_act * (1.0 - sigmoid_value))
    ).astype(jnp.bfloat16)
    local_weight_grad = lax.dot_general(
        aggregated, gate_grad, (((0,), (0,)), ((), ())), preferred_element_type=jnp.float32
    )
    grad_weight = lax.psum(local_weight_grad, ("team", "rep")) * (1.0 / math.sqrt(nodes_total))
    back_rows = lax.dot_general(
        gate_grad, weight, (((1,), (1,)), ((), ())), preferred_element_type=jnp.float32
    ).astype(jnp.bfloat16)
    back_tiles = back_rows.reshape(panel_dev, tile_size, feature_width)
    partial_list = []
    for section_index in range(section_count):
        section_sums = spread(
            back_tiles,
            tiles[:, section_index],
            coords[:, section_index],
            live_slots[:, section_index],
            slot_bounds[section_index],
            column_count,
        )
        partial_list.append(section_sums.reshape(team_rows, feature_width))
    pieces = {}
    for section_index in range(section_count):
        pieces[section_index - reach_size] = partial_list[section_index]
    team_total = deliver(pieces, reach_size)
    gradient_share = lax.psum_scatter(
        team_total.astype(jnp.bfloat16), "rep", scatter_dimension=0, tiled=True
    )
    return (activated, grad_weight, gradient_share)


def solution(mesh):
    placed = (
        P("team", None),
        P(),
        P(("team", "rep"), None),
        P(("team", "rep"), None, None, None, None),
        P(("team", "rep"), None, None),
        P(("team", "rep"), None),
    )
    return jax.shard_map(
        body,
        mesh=mesh,
        in_specs=placed,
        out_specs=(P(("team", "rep"), None), P(), P(("team", "rep"), None)),
        check_vma=False,
    )
```

profile of v0, /device:TPU:1, one launch (start us, length us, event | category | flops | bytes accessed | tf_op | source)
XLA Modules:
  0.0 590.6 jit_solution(17013438232153228950)
XLA Ops:
  8.1 4.4 collective-permute-start
  12.4 12.9 %collective-permute-start.2 = (bf16[1024,128]{1,0:T(8,128)(2,1)}, bf16[1024,128]{1,0:T(8,128)(2,1)}, u32[]{:S(2)}, u32[]{:S(2)}) collective-permute-start(bf16[1024,128]{1,0:T(8,128)(2,1)} %param.28), channel_id=1, source_target_pairs={{4,0},{8,4},{12,8},{16,12},{20,16},{24,20},{28,24},{32,28},{36,32}... | collective-permute-start | bytes 786440 | tf_op jit(solution)/shard_map/ppermute | solution.py:12
  27.0 2.0 fusion.79
  29.7 1.9 collective-permute-start.1
  34.3 7.6 %collective-permute-start.3 = (bf16[1024,128]{1,0:T(8,128)(2,1)}, bf16[1024,128]{1,0:T(8,128)(2,1)S(1)}, u32[]{:S(2)}, u32[]{:S(2)}) collective-permute-start(bf16[1024,128]{1,0:T(8,128)(2,1)} %collective-permute-done.2), channel_id=1, source_target_pairs={{4,0},{8,4},{12,8},{16,12},{20,16},{24,20},{28,24},{32,28},{36,32}... | collective-permute-start | bytes 786440 | tf_op jit(solution)/shard_map/ppermute | solution.py:12
  42.7 10.8 %while.100 = (s32[]{:T(128)}, f32[2,128,128]{2,1,0:T(8,128)S(1)}, s32[]{:T(128)}, pred[2,8]{0,1:T(8,128)(4,1)S(1)}, bf16[2,8,128,128]{2,3,0,1:T(8,128)(2,1)S(1)}...) while((s32[]{:T(128)}, f32[2,128,128]{2,1,0:T(8,128)S(1)}, ...), condition=%wide.region_2.0_spmd, body=%wide.region_1.3_spmd.sunk | while | flops 8487953 | bytes 790725 | solution.py:53
  53.5 11.0 %while.101 = (s32[]{:T(128)}, f32[2,128,128]{2,1,0:T(8,128)S(1)}, s32[]{:T(128)}, pred[2,8]{0,1:T(8,128)(4,1)S(1)}, bf16[2,8,128,128]{2,3,0,1:T(8,128)(2,1)S(1)}...) while((s32[]{:T(128)}, f32[2,128,128]{2,1,0:T(8,128)S(1)}, ...), condition=%wide.region_4.6_spmd, body=%wide.region_3.5_spmd.sunk | while | flops 8487953 | bytes 790725 | solution.py:53
  64.6 11.4 %while.102 = (s32[]{:T(128)}, f32[2,128,128]{2,1,0:T(8,128)S(1)}, s32[]{:T(128)}, pred[2,8]{0,1:T(8,128)(4,1)S(1)}, bf16[2,8,128,128]{2,3,0,1:T(8,128)(2,1)S(1)}...) while((s32[]{:T(128)}, f32[2,128,128]{2,1,0:T(8,128)S(1)}, ...), condition=%wide.region_6.8_spmd, body=%wide.region_5.7_spmd.sunk | while | flops 8487953 | bytes 790725 | solution.py:53
  65.5 1.5 gather_fusion.2
  68.1 1.5 gather_fusion.2
  70.8 1.5 gather_fusion.2
  76.0 11.4 %while.103 = (s32[]{:T(128)}, f32[2,128,128]{2,1,0:T(8,128)S(1)}, s32[]{:T(128)}, pred[2,8]{0,1:T(8,128)(4,1)S(1)}, bf16[2,8,128,128]{2,3,0,1:T(8,128)(2,1)S(1)}...) while((s32[]{:T(128)}, f32[2,128,128]{2,1,0:T(8,128)S(1)}, ...), condition=%wide.region_8.10_spmd, body=%wide.region_7.9_spmd.sunk | while | flops 8487953 | bytes 790725 | solution.py:53
  87.4 5.7 while.104
  95.1 6.7 %while.109 = (s32[]{:T(128)}, f32[8,128,128]{2,1,0:T(8,128)S(1)}, s32[]{:T(128)}, s32[2,8]{0,1:T(8,128)S(1)}, pred[2,8]{0,1:T(8,128)(4,1)S(1)}, /*index=5*/bf16[...) while((s32[]{:T(128)}, f32[8,128,128]{2,1,0:T(8,128)S(1)}, ...), condition=%wide.region_26.28_spmd, body=%wide.region_24.27_spmd.sunk | while | flops 8454155 | bytes 656055 | solution.py:71
  101.9 6.5 %while.108 = (s32[]{:T(128)}, f32[8,128,128]{2,1,0:T(8,128)S(1)}, s32[]{:T(128)}, s32[2,8]{0,1:T(8,128)S(1)}, pred[2,8]{0,1:T(8,128)(4,1)S(1)}, /*index=5*/bf16[...) while((s32[]{:T(128)}, f32[8,128,128]{2,1,0:T(8,128)S(1)}, ...), condition=%wide.region_23.25_spmd, body=%wide.region_21.24_spmd.sunk | while | flops 8454155 | bytes 656055 | solution.py:71
  108.4 10.0 %collective-permute-start.6 = (bf16[1024,128]{1,0:T(8,128)(2,1)S(1)}, bf16[1024,128]{1,0:T(8,128)(2,1)S(1)}, u32[]{:S(2)}, u32[]{:S(2)}) collective-permute-start(bf16[1024,128]{1,0:T(8,128)(2,1)S(1)} %bitcast.222), channel_id=1, source_target_pairs={{4,0},{8,4},{12,8},{16,12},{20,16},{24,20},{28,24},{32,28},{36,32}... | collective-permute-start | bytes 786440 | tf_op jit(solution)/shard_map/ppermute | solution.py:12
  118.4 5.3 while.106
  123.8 29.7 %collective-permute-start.4 = (bf16[1024,128]{1,0:T(8,128)(2,1)S(1)}, bf16[1024,128]{1,0:T(8,128)(2,1)S(1)}, u32[]{:S(2)}, u32[]{:S(2)}) collective-permute-start(bf16[1024,128]{1,0:T(8,128)(2,1)S(1)} %bitcast.223), channel_id=1, source_target_pairs={{508,0},{0,4},{4,8},{8,12},{12,16},{16,20},{20,24},{24,28},{28,32}... | collective-permute-start | bytes 786440 | tf_op jit(solution)/shard_map/ppermute | solution.py:12
  153.5 7.1 %while.107 = (s32[]{:T(128)}, f32[8,128,128]{2,1,0:T(8,128)S(1)}, s32[]{:T(128)}, s32[2,8]{0,1:T(8,128)S(1)}, pred[2,8]{0,1:T(8,128)(4,1)S(1)}, /*index=5*/bf16[...) while((s32[]{:T(128)}, f32[8,128,128]{2,1,0:T(8,128)S(1)}, ...), condition=%wide.region_20.22_spmd, body=%wide.region_18.21_spmd.sunk | while | flops 8454155 | bytes 656055 | solution.py:71
  160.7 1.9 collective-permute-start.7
  162.7 5.1 collective-permute-start.5
  167.9 7.1 %while.105 = (s32[]{:T(128)}, f32[8,128,128]{2,1,0:T(8,128)S(1)}, s32[]{:T(128)}, s32[2,8]{0,1:T(8,128)S(1)}, pred[2,8]{0,1:T(8,128)(4,1)S(1)}, /*index=5*/bf16[...) while((s32[]{:T(128)}, f32[8,128,128]{2,1,0:T(8,128)S(1)}, ...), condition=%wide.region_14.16_spmd, body=%wide.region_12.15_spmd.sunk | while | flops 8454155 | bytes 656055 | solution.py:71
  175.0 10.4 %collective-permute-done.5 = bf16[1024,128]{1,0:T(8,128)(2,1)S(1)} collective-permute-done((bf16[1024,128]{1,0:T(8,128)(2,1)S(1)}, bf16[1024,128]{1,0:T(8,128)(2,1)S(1)}, u32[]{:S(2)}, u32[]{:S(2)}) %collective-permute-start.5) | collective-permute-done | bytes 262176 | tf_op jit(solution)/shard_map/ppermute | solution.py:12
  186.2 395.4 %all-reduce.2.cloned.1.call-done = f32[128,128]{1,0:T(8,128)} async-done(((f32[128,128]{1,0:T(8,128)}), f32[128,128]{1,0:T(8,128)}) %all-reduce.2.cloned.1.call-update) | async-done | bytes 65552 | tf_op jit(solution)/shard_map/psum | solution.py:106
  (261 shorter events, 56.1 us)
Async XLA Ops:
  8.0 85.1 %copy-start = (bf16[128,128]{1,0:T(8,128)(2,1)S(1)}, bf16[128,128]{1,0:T(8,128)(2,1)}, u32[]{:S(2)}) copy-start(bf16[128,128]{1,0:T(8,128)(2,1)} %param.29) | copy-start | bytes 98308
  8.0 573.6 %all-reduce.2.cloned.1.call-start = ((), (), s32[]{:S(2)}) async-start(), calls=%async_computation.1 | async-start | bytes 131072 | tf_op jit(solution)/shard_map/psum | solution.py:106
  8.1 21.6 %collective-permute-start = (bf16[1024,128]{1,0:T(8,128)(2,1)}, bf16[1024,128]{1,0:T(8,128)(2,1)}, u32[]{:S(2)}, u32[]{:S(2)}) collective-permute-start(bf16[1024,128]{1,0:T(8,128)(2,1)} %param.28), channel_id=1, source_target_pairs={{508,0},{0,4},{4,8},{8,12},{12,16},{16,20},{20,24},{24,28},{28,32}... | collective-permute-start | bytes 786440 | tf_op jit(solution)/shard_map/ppermute | solution.py:12
  12.4 21.8 %collective-permute-start.2 = (bf16[1024,128]{1,0:T(8,128)(2,1)}, bf16[1024,128]{1,0:T(8,128)(2,1)}, u32[]{:S(2)}, u32[]{:S(2)}) collective-permute-start(bf16[1024,128]{1,0:T(8,128)(2,1)} %param.28), channel_id=1, source_target_pairs={{4,0},{8,4},{12,8},{16,12},{20,16},{24,20},{28,24},{32,28},{36,32}... | collective-permute-start | bytes 786440 | tf_op jit(solution)/shard_map/ppermute | solution.py:12
  27.0 4.7 copy-start.1
  29.7 13.0 %collective-permute-start.1 = (bf16[1024,128]{1,0:T(8,128)(2,1)}, bf16[1024,128]{1,0:T(8,128)(2,1)}, u32[]{:S(2)}, u32[]{:S(2)}) collective-permute-start(bf16[1024,128]{1,0:T(8,128)(2,1)} %collective-permute-done), channel_id=1, source_target_pairs={{508,0},{0,4},{4,8},{8,12},{12,16},{16,20},{20,24},{24,28},{28,32}... | collective-permute-start | bytes 786440 | tf_op jit(solution)/shard_map/ppermute | solution.py:12
  34.3 53.1 %collective-permute-start.3 = (bf16[1024,128]{1,0:T(8,128)(2,1)}, bf16[1024,128]{1,0:T(8,128)(2,1)S(1)}, u32[]{:S(2)}, u32[]{:S(2)}) collective-permute-start(bf16[1024,128]{1,0:T(8,128)(2,1)} %collective-permute-done.2), channel_id=1, source_target_pairs={{4,0},{8,4},{12,8},{16,12},{20,16},{24,20},{28,24},{32,28},{36,32}... | collective-permute-start | bytes 786440 | tf_op jit(solution)/shard_map/ppermute | solution.py:12
  87.4 5.7 copy-start.2
  95.0 488.1 %reduce-scatter.2.cloned.1.call-start = ((), (), s32[]{:S(2)}) async-start(), calls=%async_computation.2 | async-start | bytes 327680 | tf_op jit(solution)/shard_map/reduce_scatter | solution.py:126
  108.4 52.2 %collective-permute-start.6 = (bf16[1024,128]{1,0:T(8,128)(2,1)S(1)}, bf16[1024,128]{1,0:T(8,128)(2,1)S(1)}, u32[]{:S(2)}, u32[]{:S(2)}) collective-permute-start(bf16[1024,128]{1,0:T(8,128)(2,1)S(1)} %bitcast.222), channel_id=1, source_target_pairs={{4,0},{8,4},{12,8},{16,12},{20,16},{24,20},{28,24},{32,28},{36,32}... | collective-permute-start | bytes 786440 | tf_op jit(solution)/shard_map/ppermute | solution.py:12
  123.8 38.9 %collective-permute-start.4 = (bf16[1024,128]{1,0:T(8,128)(2,1)S(1)}, bf16[1024,128]{1,0:T(8,128)(2,1)S(1)}, u32[]{:S(2)}, u32[]{:S(2)}) collective-permute-start(bf16[1024,128]{1,0:T(8,128)(2,1)S(1)} %bitcast.223), channel_id=1, source_target_pairs={{508,0},{0,4},{4,8},{8,12},{12,16},{16,20},{20,24},{24,28},{28,32}... | collective-permute-start | bytes 786440 | tf_op jit(solution)/shard_map/ppermute | solution.py:12
  160.7 14.3 %collective-permute-start.7 = (bf16[1024,128]{1,0:T(8,128)(2,1)S(1)}, bf16[1024,128]{1,0:T(8,128)(2,1)S(1)}, u32[]{:S(2)}, u32[]{:S(2)}) collective-permute-start(bf16[1024,128]{1,0:T(8,128)(2,1)S(1)} %fusion.75), channel_id=1, source_target_pairs={{4,0},{8,4},{12,8},{16,12},{20,16},{24,20},{28,24},{32,28},{36,32}... | collective-permute-start | bytes 786440 | tf_op jit(solution)/shard_map/ppermute | solution.py:12
  162.7 22.7 %collective-permute-start.5 = (bf16[1024,128]{1,0:T(8,128)(2,1)S(1)}, bf16[1024,128]{1,0:T(8,128)(2,1)S(1)}, u32[]{:S(2)}, u32[]{:S(2)}) collective-permute-start(bf16[1024,128]{1,0:T(8,128)(2,1)S(1)} %fusion.76), channel_id=1, source_target_pairs={{508,0},{0,4},{4,8},{8,12},{12,16},{16,20},{20,24},{24,28},{28,32}... | collective-permute-start | bytes 786440 | tf_op jit(solution)/shard_map/ppermute | solution.py:12
Sparse Core Ops, SparseCore 0:
  95.1 486.4 all-reduce.1
Sparse Core Ops, SparseCore 1:
  186.3 62.8 reduce-scatter.1
where the time goes:
time: 593 us; the launch traced here: 591 us
  waiting for transfers between devices  407 us (69%)
  starting transfers between devices  73.5 us (12%)
  local copies, waits for them, and re-layouts  34.8 us (6%)
  loops' own time  32.8 us (6%)
  other arithmetic  16 us (3%)
  between operations  15.8 us (3%)
  matrix products  10.4 us (2%)
    psum x1, waiting for transfers between devices, body(): lax.psum(local_weight_grad, ('team', 'rep'))  395 us
    ppermute x8, starting transfers between devices, from_behind(): return lax.ppermute(block, axis, route)  73.5 us
    gather x19, local copies, waits for them, and re-layouts, aggregate_add_slot(): picked = jnp.take(source_tiles, column_tile, axis=0)  25.9 us
    another operation x5, loops' own time, aggregate(): return lax.fori_loop(0, slot_bound, aggregate_add_slot, running)  16.6 us
    another operation x5, loops' own time, spread(): return lax.fori_loop(0, slot_bound, spread_add_slot, initial)  16.1 us
    scatter-add x19, other arithmetic, spread_add_slot(): return partial_sums.at[column_tile].add(contrib)  12.2 us
  transfers between devices with their start and end apart: 10, of which 4 were waited for; matrix products, arithmetic and copies ran while one was open for 10% of the time, Pallas kernels for 0%

commit v1 on v0

--- a/solution.py
+++ b/solution.py
@@ -10,6 +10,20 @@
     devices = range(lax.axis_size(axis))
     route = [((i - distance) % len(devices), i) for i in devices]
     return lax.ppermute(block, axis, route)
+
+
+def butterfly_sum(block, axes):
+    for axis in axes:
+        size = lax.axis_size(axis)
+        if size & (size - 1):
+            block = lax.psum(block, axis)
+            continue
+        distance = 1
+        while distance < size:
+            route = [(i, i ^ distance) for i in range(size)]
+            block = block + lax.ppermute(block, axis, route)
+            distance *= 2
+    return block
 
 
 def neighbour_blocks(features, reach_size):
@@ -103,7 +117,7 @@
     local_weight_grad = lax.dot_general(
         aggregated, gate_grad, (((0,), (0,)), ((), ())), preferred_element_type=jnp.float32
     )
-    grad_weight = lax.psum(local_weight_grad, ("team", "rep")) * (1.0 / math.sqrt(nodes_total))
+    grad_weight = butterfly_sum(local_weight_grad, ("rep", "team")) * (1.0 / math.sqrt(nodes_total))
     back_rows = lax.dot_general(
         gate_grad, weight, (((1,), (1,)), ((), ())), preferred_element_type=jnp.float32
     ).astype(jnp.bfloat16)

time: 593 us -> 280 us (0.47)
  waiting for transfers between devices: 407 us -> 28.4 us
  starting transfers between devices: 73.5 us -> 121 us
  loops' own time: 32.8 us -> 40.4 us
  local copies, waits for them, and re-layouts: 34.8 us -> 42.1 us
    psum x1 -> x0, waiting for transfers between devices: 395 us -> none  [body(): lax.psum(local_weight_grad, ('team', 'rep'))]
    ppermute x0 -> x9, starting transfers between devices: none -> 73.1 us  [butterfly_sum(): block = block + lax.ppermute(block, axis, route)]
    ppermute x8, starting transfers between devices: 73.5 us -> 47.7 us  [from_behind(): return lax.ppermute(block, axis, route)]
    ppermute x0 -> x9, waiting for transfers between devices: none -> 11.5 us  [butterfly_sum(): block = block + lax.ppermute(block, axis, route)]
    reduce_scatter x1, waiting for transfers between devices: 0.01 us -> 11.2 us  [body(): lax.psum_scatter(team_total.astype(jnp.bfloat16), 'rep', scatter_dimensio...]
    gather x19 -> x24, local copies, waits for them, and re-layouts: 25.9 us -> 32.5 us  [aggregate_add_slot(): picked = jnp.take(source_tiles, column_tile, axis=0)]
    ppermute x8, waiting for transfers between devices: 11.7 us -> 5.69 us  [from_behind(): return lax.ppermute(block, axis, route)]
    scatter-add x19 -> x24, other arithmetic: 12.2 us -> 15.4 us  [spread_add_slot(): return partial_sums.at[column_tile].add(contrib)]
  transfers between devices with their start and end apart: 10 -> 18, of which waited for: 4 -> 9; matrix products, arithmetic and copies ran while one was open for 10% -> 25% of each run, Pallas kernels for 0% -> 0%
where the time goes in v1:
time: 280 us; the launch traced here: 278 us
  starting transfers between devices  121 us (43%)
  local copies, waits for them, and re-layouts  42.1 us (15%)
  loops' own time  40.4 us (14%)
  waiting for transfers between devices  28.4 us (10%)
  other arithmetic  19.6 us (7%)
  between operations  14.5 us (5%)
  matrix products  12 us (4%)
    ppermute x9, starting transfers between devices, butterfly_sum(): block = block + lax.ppermute(block, axis, route)  73.1 us
    ppermute x8, starting transfers between devices, from_behind(): return lax.ppermute(block, axis, route)  47.7 us
    gather x24, local copies, waits for them, and re-layouts, aggregate_add_slot(): picked = jnp.take(source_tiles, column_tile, axis=0)  32.5 us
    another operation x5, loops' own time, aggregate(): return lax.fori_loop(0, slot_bound, aggregate_add_slot, running)  20.5 us
    another operation x5, loops' own time, spread(): return lax.fori_loop(0, slot_bound, spread_add_slot, initial)  19.9 us
    scatter-add x24, other arithmetic, spread_add_slot(): return partial_sums.at[column_tile].add(contrib)  15.4 us
    ppermute x9, waiting for transfers between devices, butterfly_sum(): block = block + lax.ppermute(block, axis, route)  11.5 us
    reduce_scatter x1, waiting for transfers between devices, body(): lax.psum_scatter(team_total.astype(jnp.bfloat16), 'rep', scatter_dimensio...  11.2 us
  transfers between devices with their start and end apart: 18, of which 9 were waited for; matrix products, arithmetic and copies ran while one was open for 25% of the time, Pallas kernels for 0%

profile of v1, /device:TPU:1, one launch (start us, length us, event | category | flops | bytes accessed | tf_op | source)
XLA Modules:
  0.0 277.8 jit_solution(17309447382010295771)
XLA Ops:
  7.2 4.4 %collective-permute-start = (bf16[1024,128]{1,0:T(8,128)(2,1)}, bf16[1024,128]{1,0:T(8,128)(2,1)}, u32[]{:S(2)}, u32[]{:S(2)}) collective-permute-start(bf16[1024,128]{1,0:T(8,128)(2,1)} %param.28), channel_id=1, source_target_pairs={{508,0},{0,4},{4,8},{8,12},{12,16},{16,20},{20,24},{24,28},{28,32}... | collective-permute-start | bytes 786440 | tf_op jit(solution)/shard_map/ppermute | solution.py:12
  11.6 12.9 %collective-permute-start.2 = (bf16[1024,128]{1,0:T(8,128)(2,1)}, bf16[1024,128]{1,0:T(8,128)(2,1)}, u32[]{:S(2)}, u32[]{:S(2)}) collective-permute-start(bf16[1024,128]{1,0:T(8,128)(2,1)} %param.28), channel_id=1, source_target_pairs={{4,0},{8,4},{12,8},{16,12},{20,16},{24,20},{28,24},{32,28},{36,32}... | collective-permute-start | bytes 786440 | tf_op jit(solution)/shard_map/ppermute | solution.py:12
  33.4 7.6 %collective-permute-start.3 = (bf16[1024,128]{1,0:T(8,128)(2,1)}, bf16[1024,128]{1,0:T(8,128)(2,1)S(1)}, u32[]{:S(2)}, u32[]{:S(2)}) collective-permute-start(bf16[1024,128]{1,0:T(8,128)(2,1)} %collective-permute-done.2), channel_id=1, source_target_pairs={{4,0},{8,4},{12,8},{16,12},{20,16},{24,20},{28,24},{32,28},{36,32}... | collective-permute-start | bytes 786440 | tf_op jit(solution)/shard_map/ppermute | solution.py:12
  41.9 16.7 %while.100 = (s32[]{:T(128)}, f32[2,128,128]{2,1,0:T(8,128)S(1)}, s32[]{:T(128)}, pred[2,8]{0,1:T(8,128)(4,1)S(1)}, bf16[2,8,128,128]{2,3,0,1:T(8,128)(2,1)S(1)}...) while((s32[]{:T(128)}, f32[2,128,128]{2,1,0:T(8,128)S(1)}, ...), condition=%wide.region_2.0_spmd, body=%wide.region_1.3_spmd.sunk | while | flops 8487953 | bytes 790725 | solution.py:67
  58.6 14.1 %while.101 = (s32[]{:T(128)}, f32[2,128,128]{2,1,0:T(8,128)S(1)}, s32[]{:T(128)}, pred[2,8]{0,1:T(8,128)(4,1)S(1)}, bf16[2,8,128,128]{2,3,0,1:T(8,128)(2,1)S(1)}...) while((s32[]{:T(128)}, f32[2,128,128]{2,1,0:T(8,128)S(1)}, ...), condition=%wide.region_4.6_spmd, body=%wide.region_3.5_spmd.sunk | while | flops 8487953 | bytes 790725 | solution.py:67
  72.7 8.4 %while.102 = (s32[]{:T(128)}, f32[2,128,128]{2,1,0:T(8,128)S(1)}, s32[]{:T(128)}, pred[2,8]{0,1:T(8,128)(4,1)S(1)}, bf16[2,8,128,128]{2,3,0,1:T(8,128)(2,1)S(1)}...) while((s32[]{:T(128)}, f32[2,128,128]{2,1,0:T(8,128)S(1)}, ...), condition=%wide.region_6.8_spmd, body=%wide.region_5.7_spmd.sunk | while | flops 8487953 | bytes 790725 | solution.py:67
  81.1 16.2 %while.103 = (s32[]{:T(128)}, f32[2,128,128]{2,1,0:T(8,128)S(1)}, s32[]{:T(128)}, pred[2,8]{0,1:T(8,128)(4,1)S(1)}, bf16[2,8,128,128]{2,3,0,1:T(8,128)(2,1)S(1)}...) while((s32[]{:T(128)}, f32[2,128,128]{2,1,0:T(8,128)S(1)}, ...), condition=%wide.region_8.10_spmd, body=%wide.region_7.9_spmd.sunk | while | flops 8487953 | bytes 790725 | solution.py:67
  97.4 7.3 %while.104 = (s32[]{:T(128)}, f32[2,128,128]{2,1,0:T(8,128)S(1)}, s32[]{:T(128)}, pred[2,8]{0,1:T(8,128)(4,1)S(1)}, bf16[2,8,128,128]{2,3,0,1:T(8,128)(2,1)S(1)}...) while((s32[]{:T(128)}, f32[2,128,128]{2,1,0:T(8,128)S(1)}, ...), condition=%wide.region_10.12_spmd, body=%wide.region_9.11_spmd.sunk | while | flops 8487953 | bytes 790725 | solution.py:67
  106.0 4.6 %collective-permute-start.4 = (f32[128,128]{1,0:T(8,128)S(1)}, f32[128,128]{1,0:T(8,128)S(1)}, u32[]{:S(2)}, u32[]{:S(2)}) collective-permute-start(f32[128,128]{1,0:T(8,128)S(1)} %fusion.81), channel_id=1, source_target_pairs={{0,1},{1,0},{2,3},{3,2},{4,5},{5,4},{6,7},{7,6},{8,9},{9,8},{10,11... | collective-permute-start | bytes 196616 | tf_op jit(solution)/shard_map/ppermute | solution.py:24
  110.7 8.7 %while.109 = (s32[]{:T(128)}, f32[8,128,128]{2,1,0:T(8,128)S(1)}, s32[]{:T(128)}, s32[2,8]{0,1:T(8,128)S(1)}, pred[2,8]{0,1:T(8,128)(4,1)S(1)}, /*index=5*/bf16[...) while((s32[]{:T(128)}, f32[8,128,128]{2,1,0:T(8,128)S(1)}, ...), condition=%wide.region_25.27_spmd, body=%wide.region_23.26_spmd.sunk | while | flops 8454155 | bytes 656055 | solution.py:85
  119.4 10.3 %while.108 = (s32[]{:T(128)}, f32[8,128,128]{2,1,0:T(8,128)S(1)}, s32[]{:T(128)}, s32[2,8]{0,1:T(8,128)S(1)}, pred[2,8]{0,1:T(8,128)(4,1)S(1)}, /*index=5*/bf16[...) while((s32[]{:T(128)}, f32[8,128,128]{2,1,0:T(8,128)S(1)}, ...), condition=%wide.region_22.24_spmd, body=%wide.region_20.23_spmd.sunk | while | flops 8454155 | bytes 656055 | solution.py:85
  133.7 6.8 %while.106 = (s32[]{:T(128)}, f32[8,128,128]{2,1,0:T(8,128)S(1)}, s32[]{:T(128)}, s32[2,8]{0,1:T(8,128)S(1)}, pred[2,8]{0,1:T(8,128)(4,1)S(1)}, /*index=5*/bf16[...) while((s32[]{:T(128)}, f32[8,128,128]{2,1,0:T(8,128)S(1)}, ...), condition=%wide.region_16.18_spmd, body=%wide.region_14.17_spmd.sunk | while | flops 8454155 | bytes 656055 | solution.py:85
  140.5 4.9 %collective-permute-start.13 = (bf16[1024,128]{1,0:T(8,128)(2,1)S(1)}, bf16[1024,128]{1,0:T(8,128)(2,1)S(1)}, u32[]{:S(2)}, u32[]{:S(2)}) collective-permute-start(bf16[1024,128]{1,0:T(8,128)(2,1)S(1)} %bitcast.223), channel_id=1, source_target_pairs={{508,0},{0,4},{4,8},{8,12},{12,16},{16,20},{20,24},{24,28},{28,32}... | collective-permute-start | bytes 786440 | tf_op jit(solution)/shard_map/ppermute | solution.py:12
  145.5 14.7 %collective-permute-start.6 = (f32[128,128]{1,0:T(8,128)S(1)}, f32[128,128]{1,0:T(8,128)S(1)}, u32[]{:S(2)}, u32[]{:S(2)}) collective-permute-start(f32[128,128]{1,0:T(8,128)S(1)} %add.181), channel_id=1, source_target_pairs={{0,4},{4,0},{8,12},{12,8},{16,20},{20,16},{24,28},{28,24},{32,36},... | collective-permute-start | bytes 196616 | tf_op jit(solution)/shard_map/ppermute | solution.py:24
  160.2 9.8 %while.107 = (s32[]{:T(128)}, f32[8,128,128]{2,1,0:T(8,128)S(1)}, s32[]{:T(128)}, s32[2,8]{0,1:T(8,128)S(1)}, pred[2,8]{0,1:T(8,128)(4,1)S(1)}, /*index=5*/bf16[...) while((s32[]{:T(128)}, f32[8,128,128]{2,1,0:T(8,128)S(1)}, ...), condition=%wide.region_19.21_spmd, body=%wide.region_17.20_spmd.sunk | while | flops 8454155 | bytes 656055 | solution.py:85
  170.0 3.2 %collective-permute-start.7 = (f32[128,128]{1,0:T(8,128)S(1)}, f32[128,128]{1,0:T(8,128)S(1)}, u32[]{:S(2)}, u32[]{:S(2)}) collective-permute-start(f32[128,128]{1,0:T(8,128)S(1)} %add.182), channel_id=1, source_target_pairs={{0,8},{4,12},{8,0},{12,4},{16,24},{20,28},{24,16},{28,20},{32,40},... | collective-permute-start | bytes 196616 | tf_op jit(solution)/shard_map/ppermute | solution.py:24
  174.3 12.2 %collective-permute-start.16 = (bf16[1024,128]{1,0:T(8,128)(2,1)S(1)}, bf16[1024,128]{1,0:T(8,128)(2,1)S(1)}, u32[]{:S(2)}, u32[]{:S(2)}) collective-permute-start(bf16[1024,128]{1,0:T(8,128)(2,1)S(1)} %fusion.75), channel_id=1, source_target_pairs={{4,0},{8,4},{12,8},{16,12},{20,16},{24,20},{28,24},{32,28},{36,32}... | collective-permute-start | bytes 786440 | tf_op jit(solution)/shard_map/ppermute | solution.py:12
  188.6 5.2 %while.105 = (s32[]{:T(128)}, f32[8,128,128]{2,1,0:T(8,128)S(1)}, s32[]{:T(128)}, s32[2,8]{0,1:T(8,128)S(1)}, pred[2,8]{0,1:T(8,128)(4,1)S(1)}, /*index=5*/bf16[...) while((s32[]{:T(128)}, f32[8,128,128]{2,1,0:T(8,128)S(1)}, ...), condition=%wide.region_13.15_spmd, body=%wide.region_11.14_spmd.sunk | while | flops 8454155 | bytes 656055 | solution.py:85
  195.7 4.2 %collective-permute-done.14 = bf16[1024,128]{1,0:T(8,128)(2,1)S(1)} collective-permute-done((bf16[1024,128]{1,0:T(8,128)(2,1)S(1)}, bf16[1024,128]{1,0:T(8,128)(2,1)S(1)}, u32[]{:S(2)}, u32[]{:S(2)}) %collective-permute-start.14) | collective-permute-done | bytes 262176 | tf_op jit(solution)/shard_map/ppermute | solution.py:12
  202.7 17.2 %collective-permute-start.9 = (f32[128,128]{1,0:T(8,128)S(1)}, f32[128,128]{1,0:T(8,128)S(1)}, u32[]{:S(2)}, u32[]{:S(2)}) collective-permute-start(f32[128,128]{1,0:T(8,128)S(1)} %add.184), channel_id=1, source_target_pairs={{0,32},{4,36},{8,40},{12,44},{16,48},{20,52},{24,56},{28,60},{32,0... | collective-permute-start | bytes 196616 | tf_op jit(solution)/shard_map/ppermute | solution.py:24
  221.6 22.4 %collective-permute-start.10 = (f32[128,128]{1,0:T(8,128)S(1)}, f32[128,128]{1,0:T(8,128)S(1)}, u32[]{:S(2)}, u32[]{:S(2)}) collective-permute-start(f32[128,128]{1,0:T(8,128)S(1)} %add.185), channel_id=1, source_target_pairs={{0,64},{4,68},{8,72},{12,76},{16,80},{20,84},{24,88},{28,92},{32,9... | collective-permute-start | bytes 196616 | tf_op jit(solution)/shard_map/ppermute | solution.py:24
  247.6 4.6 %collective-permute-done.11 = f32[128,128]{1,0:T(8,128)S(1)} collective-permute-done((f32[128,128]{1,0:T(8,128)S(1)}, f32[128,128]{1,0:T(8,128)S(1)}, u32[]{:S(2)}, u32[]{:S(2)}) %collective-permute-start.11) | collective-permute-done | bytes 65568 | tf_op jit(solution)/shard_map/ppermute | solution.py:24
  252.2 5.3 %collective-permute-start.12 = (f32[128,128]{1,0:T(8,128)S(1)}, f32[128,128]{1,0:T(8,128)S(1)}, u32[]{:S(2)}, u32[]{:S(2)}) collective-permute-start(f32[128,128]{1,0:T(8,128)S(1)} %add.187), channel_id=1, source_target_pairs={{0,256},{4,260},{8,264},{12,268},{16,272},{20,276},{24,280},{28,28... | collective-permute-start | bytes 196616 | tf_op jit(solution)/shard_map/ppermute | solution.py:24
  259.8 11.2 %reduce-scatter.2.cloned.1.call-done = bf16[256,128]{1,0:T(8,128)(2,1)} async-done(((bf16[1024,128]{1,0:T(8,128)(2,1)}), bf16[256,128]{1,0:T(8,128)(2,1)}) %reduce-scatter.2.cloned.1.call-update) | async-done | bytes 65552 | tf_op jit(solution)/shard_map/reduce_scatter | solution.py:140
  (339 shorter events, 93.6 us)
Async XLA Ops:
  7.2 97.6 %copy-start = (bf16[128,128]{1,0:T(8,128)(2,1)S(1)}, bf16[128,128]{1,0:T(8,128)(2,1)}, u32[]{:S(2)}) copy-start(bf16[128,128]{1,0:T(8,128)(2,1)} %param.29) | copy-start | bytes 98308
  7.2 263.8 %reduce-scatter.2.cloned.1.call-start = ((), (), s32[]{:S(2)}) async-start(), calls=%async_computation.1 | async-start | bytes 327680 | tf_op jit(solution)/shard_map/reduce_scatter | solution.py:140
  7.2 21.6 %collective-permute-start = (bf16[1024,128]{1,0:T(8,128)(2,1)}, bf16[1024,128]{1,0:T(8,128)(2,1)}, u32[]{:S(2)}, u32[]{:S(2)}) collective-permute-start(bf16[1024,128]{1,0:T(8,128)(2,1)} %param.28), channel_id=1, source_target_pairs={{508,0},{0,4},{4,8},{8,12},{12,16},{16,20},{20,24},{24,28},{28,32}... | collective-permute-start | bytes 786440 | tf_op jit(solution)/shard_map/ppermute | solution.py:12
  11.6 21.8 %collective-permute-start.2 = (bf16[1024,128]{1,0:T(8,128)(2,1)}, bf16[1024,128]{1,0:T(8,128)(2,1)}, u32[]{:S(2)}, u32[]{:S(2)}) collective-permute-start(bf16[1024,128]{1,0:T(8,128)(2,1)} %param.28), channel_id=1, source_target_pairs={{4,0},{8,4},{12,8},{16,12},{20,16},{24,20},{28,24},{32,28},{36,32}... | collective-permute-start | bytes 786440 | tf_op jit(solution)/shard_map/ppermute | solution.py:12
  26.1 4.7 %copy-start.1 = (s32[2,5,8]{2,0,1:T(2,128)S(1)}, s32[2,5,8]{2,0,1:T(2,128)}, u32[]{:S(2)}) copy-start(s32[2,5,8]{2,0,1:T(2,128)} %param.32) | copy-start | bytes 964
  28.9 13.0 %collective-permute-start.1 = (bf16[1024,128]{1,0:T(8,128)(2,1)}, bf16[1024,128]{1,0:T(8,128)(2,1)}, u32[]{:S(2)}, u32[]{:S(2)}) collective-permute-start(bf16[1024,128]{1,0:T(8,128)(2,1)} %collective-permute-done), channel_id=1, source_target_pairs={{508,0},{0,4},{4,8},{8,12},{12,16},{16,20},{20,24},{24,28},{28,32}... | collective-permute-start | bytes 786440 | tf_op jit(solution)/shard_map/ppermute | solution.py:12
  33.4 64.0 %collective-permute-start.3 = (bf16[1024,128]{1,0:T(8,128)(2,1)}, bf16[1024,128]{1,0:T(8,128)(2,1)S(1)}, u32[]{:S(2)}, u32[]{:S(2)}) collective-permute-start(bf16[1024,128]{1,0:T(8,128)(2,1)} %collective-permute-done.2), channel_id=1, source_target_pairs={{4,0},{8,4},{12,8},{16,12},{20,16},{24,20},{28,24},{32,28},{36,32}... | collective-permute-start | bytes 786440 | tf_op jit(solution)/shard_map/ppermute | solution.py:12
  97.4 7.4 %copy-start.2 = (bf16[256,128]{1,0:T(8,128)(2,1)S(1)}, bf16[256,128]{1,0:T(8,128)(2,1)}, u32[]{:S(2)}) copy-start(bf16[256,128]{1,0:T(8,128)(2,1)} %param.30) | copy-start | bytes 196612
  106.0 25.7 %collective-permute-start.4 = (f32[128,128]{1,0:T(8,128)S(1)}, f32[128,128]{1,0:T(8,128)S(1)}, u32[]{:S(2)}, u32[]{:S(2)}) collective-permute-start(f32[128,128]{1,0:T(8,128)S(1)} %fusion.81), channel_id=1, source_target_pairs={{0,1},{1,0},{2,3},{3,2},{4,5},{5,4},{6,7},{7,6},{8,9},{9,8},{10,11... | collective-permute-start | bytes 196616 | tf_op jit(solution)/shard_map/ppermute | solution.py:24
  129.7 43.5 %collective-permute-start.15 = (bf16[1024,128]{1,0:T(8,128)(2,1)S(1)}, bf16[1024,128]{1,0:T(8,128)(2,1)}, u32[]{:S(2)}, u32[]{:S(2)}) collective-permute-start(bf16[1024,128]{1,0:T(8,128)(2,1)S(1)} %bitcast.222), channel_id=1, source_target_pairs={{4,0},{8,4},{12,8},{16,12},{20,16},{24,20},{28,24},{32,28},{36,32}... | collective-permute-start | bytes 786440 | tf_op jit(solution)/shard_map/ppermute | solution.py:12
  131.7 13.8 %collective-permute-start.5 = (f32[128,128]{1,0:T(8,128)S(1)}, f32[128,128]{1,0:T(8,128)S(1)}, u32[]{:S(2)}, u32[]{:S(2)}) collective-permute-start(f32[128,128]{1,0:T(8,128)S(1)} %add.180), channel_id=1, source_target_pairs={{0,2},{1,3},{2,0},{3,1},{4,6},{5,7},{6,4},{7,5},{8,10},{9,11},{10,... | collective-permute-start | bytes 196616 | tf_op jit(solution)/shard_map/ppermute | solution.py:24
  140.5 46.0 %collective-permute-start.13 = (bf16[1024,128]{1,0:T(8,128)(2,1)S(1)}, bf16[1024,128]{1,0:T(8,128)(2,1)S(1)}, u32[]{:S(2)}, u32[]{:S(2)}) collective-permute-start(bf16[1024,128]{1,0:T(8,128)(2,1)S(1)} %bitcast.223), channel_id=1, source_target_pairs={{508,0},{0,4},{4,8},{8,12},{12,16},{16,20},{20,24},{24,28},{28,32}... | collective-permute-start | bytes 786440 | tf_op jit(solution)/shard_map/ppermute | solution.py:12
  145.5 24.5 %collective-permute-start.6 = (f32[128,128]{1,0:T(8,128)S(1)}, f32[128,128]{1,0:T(8,128)S(1)}, u32[]{:S(2)}, u32[]{:S(2)}) collective-permute-start(f32[128,128]{1,0:T(8,128)S(1)} %add.181), channel_id=1, source_target_pairs={{0,4},{4,0},{8,12},{12,8},{16,20},{20,16},{24,28},{28,24},{32,36},... | collective-permute-start | bytes 196616 | tf_op jit(solution)/shard_map/ppermute | solution.py:24
  170.0 23.7 %collective-permute-start.7 = (f32[128,128]{1,0:T(8,128)S(1)}, f32[128,128]{1,0:T(8,128)S(1)}, u32[]{:S(2)}, u32[]{:S(2)}) collective-permute-start(f32[128,128]{1,0:T(8,128)S(1)} %add.182), channel_id=1, source_target_pairs={{0,8},{4,12},{8,0},{12,4},{16,24},{20,28},{24,16},{28,20},{32,40},... | collective-permute-start | bytes 196616 | tf_op jit(solution)/shard_map/ppermute | solution.py:24
  174.3 21.4 %collective-permute-start.16 = (bf16[1024,128]{1,0:T(8,128)(2,1)S(1)}, bf16[1024,128]{1,0:T(8,128)(2,1)S(1)}, u32[]{:S(2)}, u32[]{:S(2)}) collective-permute-start(bf16[1024,128]{1,0:T(8,128)(2,1)S(1)} %fusion.75), channel_id=1, source_target_pairs={{4,0},{8,4},{12,8},{16,12},{20,16},{24,20},{28,24},{32,28},{36,32}... | collective-permute-start | bytes 786440 | tf_op jit(solution)/shard_map/ppermute | solution.py:12
  186.6 13.4 %collective-permute-start.14 = (bf16[1024,128]{1,0:T(8,128)(2,1)S(1)}, bf16[1024,128]{1,0:T(8,128)(2,1)S(1)}, u32[]{:S(2)}, u32[]{:S(2)}) collective-permute-start(bf16[1024,128]{1,0:T(8,128)(2,1)S(1)} %fusion.76), channel_id=1, source_target_pairs={{508,0},{0,4},{4,8},{8,12},{12,16},{16,20},{20,24},{24,28},{28,32}... | collective-permute-start | bytes 786440 | tf_op jit(solution)/shard_map/ppermute | solution.py:12
  193.8 8.9 %collective-permute-start.8 = (f32[128,128]{1,0:T(8,128)S(1)}, f32[128,128]{1,0:T(8,128)S(1)}, u32[]{:S(2)}, u32[]{:S(2)}) collective-permute-start(f32[128,128]{1,0:T(8,128)S(1)} %add.183), channel_id=1, source_target_pairs={{0,16},{4,20},{8,24},{12,28},{16,0},{20,4},{24,8},{28,12},{32,48},... | collective-permute-start | bytes 196616 | tf_op jit(solution)/shard_map/ppermute | solution.py:24
  202.7 18.9 %collective-permute-start.9 = (f32[128,128]{1,0:T(8,128)S(1)}, f32[128,128]{1,0:T(8,128)S(1)}, u32[]{:S(2)}, u32[]{:S(2)}) collective-permute-start(f32[128,128]{1,0:T(8,128)S(1)} %add.184), channel_id=1, source_target_pairs={{0,32},{4,36},{8,40},{12,44},{16,48},{20,52},{24,56},{28,60},{32,0... | collective-permute-start | bytes 196616 | tf_op jit(solution)/shard_map/ppermute | solution.py:24
  221.6 24.0 %collective-permute-start.10 = (f32[128,128]{1,0:T(8,128)S(1)}, f32[128,128]{1,0:T(8,128)S(1)}, u32[]{:S(2)}, u32[]{:S(2)}) collective-permute-start(f32[128,128]{1,0:T(8,128)S(1)} %add.185), channel_id=1, source_target_pairs={{0,64},{4,68},{8,72},{12,76},{16,80},{20,84},{24,88},{28,92},{32,9... | collective-permute-start | bytes 196616 | tf_op jit(solution)/shard_map/ppermute | solution.py:24
  245.7 6.5 %collective-permute-start.11 = (f32[128,128]{1,0:T(8,128)S(1)}, f32[128,128]{1,0:T(8,128)S(1)}, u32[]{:S(2)}, u32[]{:S(2)}) collective-permute-start(f32[128,128]{1,0:T(8,128)S(1)} %add.186), channel_id=1, source_target_pairs={{0,128},{4,132},{8,136},{12,140},{16,144},{20,148},{24,152},{28,15... | collective-permute-start | bytes 196616 | tf_op jit(solution)/shard_map/ppermute | solution.py:24
  252.2 6.9 %collective-permute-start.12 = (f32[128,128]{1,0:T(8,128)S(1)}, f32[128,128]{1,0:T(8,128)S(1)}, u32[]{:S(2)}, u32[]{:S(2)}) collective-permute-start(f32[128,128]{1,0:T(8,128)S(1)} %add.187), channel_id=1, source_target_pairs={{0,256},{4,260},{8,264},{12,268},{16,272},{20,276},{24,280},{28,28... | collective-permute-start | bytes 196616 | tf_op jit(solution)/shard_map/ppermute | solution.py:24
Sparse Core Ops, SparseCore 0:
  200.9 70.0 reduce-scatter.1

commit v2 on v1

v2 whole, which is shorter than its diff:
```python
import functools
import math

import jax
import jax.numpy as jnp
from jax import lax
from jax.experimental import pallas as pl
from jax.experimental.pallas import tpu as pltpu
from jax.sharding import PartitionSpec as P


def from_behind(block, axis, distance):
    devices = range(lax.axis_size(axis))
    route = [((i - distance) % len(devices), i) for i in devices]
    return lax.ppermute(block, axis, route)


def butterfly_sum(block, axes):
    for axis in axes:
        size = lax.axis_size(axis)
        if size & (size - 1):
            block = lax.psum(block, axis)
            continue
        distance = 1
        while distance < size:
            route = [(i, i ^ distance) for i in range(size)]
            block = block + lax.ppermute(block, axis, route)
            distance *= 2
    return block


def neighbour_blocks(features, reach_size):
    blocks = {0: features}
    ahead_block = features
    behind_block = features
    for offset in range(1, reach_size + 1):
        ahead_block = from_behind(ahead_block, "team", -1)
        behind_block = from_behind(behind_block, "team", 1)
        blocks[offset] = ahead_block
        blocks[-offset] = behind_block
    return blocks


def layer_kernel(coords_ref, counts_ref, *refs, section_count, slot_count, panel_dev, tile_size):
    feature_refs = refs[:section_count]
    tiles_ref, out_grad_ref, weight_ref, act_ref, wgrad_ref, sums_ref = refs[section_count:]
    weight = weight_ref[...]
    column_count = feature_refs[0].shape[0] // tile_size
    direct_first = slot_count == column_count

    def slot_entry(g, s, k):
        base = (g * section_count + s) * slot_count + k
        column = jnp.clip(coords_ref[base], 0, column_count - 1)
        live = k < counts_ref[g * section_count + s]
        return column, live

    aggregated_rows = []
    gate_rows = []
    for g in range(panel_dev):
        total = jnp.zeros((tile_size, weight.shape[1]), jnp.float32)
        for s in range(section_count):
            for k in range(slot_count):
                column, live = slot_entry(g, s, k)
                start = pl.multiple_of(column * tile_size, tile_size)
                picked = feature_refs[s][pl.ds(start, tile_size), :]
                product = jnp.dot(tiles_ref[g, s, k], picked, preferred_element_type=jnp.float32)
                total = total + jnp.where(live, product, 0.0)
        aggregated = total.astype(jnp.bfloat16)
        pre_act = jnp.dot(aggregated, weight, preferred_element_type=jnp.float32)
        sigmoid_value = jax.nn.sigmoid(pre_act)
        rows = pl.ds(g * tile_size, tile_size)
        act_ref[rows, :] = (pre_act * sigmoid_value).astype(act_ref.dtype)
        out_grad = out_grad_ref[rows, :].astype(jnp.float32)
        gate = (out_grad * sigmoid_value * (1.0 + pre_act * (1.0 - sigmoid_value))).astype(jnp.bfloat16)
        aggregated_rows.append(aggregated)
        gate_rows.append(gate)

    aggregated_all = jnp.concatenate(aggregated_rows, axis=0)
    gate_all = jnp.concatenate(gate_rows, axis=0)
    wgrad_ref[...] = lax.dot_general(
        aggregated_all, gate_all, (((0,), (0,)), ((), ())), preferred_element_type=jnp.float32
    )
    if not direct_first:
        sums_ref[...] = jnp.zeros(sums_ref.shape, sums_ref.dtype)
    for g in range(panel_dev):
        back = lax.dot_general(
            gate_rows[g], weight, (((1,), (1,)), ((), ())), preferred_element_type=jnp.float32
        ).astype(jnp.bfloat16)
        for s in range(section_count):
            for k in range(slot_count):
                column, live = slot_entry(g, s, k)
                start = pl.multiple_of(column * tile_size, tile_size)
                contrib = lax.dot_general(
                    tiles_ref[g, s, k], back, (((0,), (0,)), ((), ())),
                    preferred_element_type=jnp.float32,
                )
                contrib = jnp.where(live, contrib, 0.0)
                if g == 0 and direct_first:
                    sums_ref[s, pl.ds(start, tile_size), :] = contrib
                else:
                    sums_ref[s, pl.ds(start, tile_size), :] += contrib


def layer_call(source_blocks, tiles, out_grad, weight, coords, counts):
    panel_dev, section_count, slot_count, tile_size, _ = tiles.shape
    team_rows, feature_width = source_blocks[0].shape
    kernel = functools.partial(
        layer_kernel,
        section_count=section_count,
        slot_count=slot_count,
        panel_dev=panel_dev,
        tile_size=tile_size,
    )
    smem = pl.BlockSpec(memory_space=pltpu.SMEM)
    vmem = pl.BlockSpec(memory_space=pltpu.VMEM)
    matmuls = 2 * panel_dev * section_count * slot_count + 4 * panel_dev
    return pl.pallas_call(
        kernel,
        out_shape=(
            jax.ShapeDtypeStruct(out_grad.shape, jnp.bfloat16),
            jax.ShapeDtypeStruct((feature_width, feature_width), jnp.float32),
            jax.ShapeDtypeStruct((section_count, team_rows, feature_width), jnp.float32),
        ),
        in_specs=[smem, smem] + [vmem] * (section_count + 3),
        out_specs=(vmem, vmem, vmem),
        compiler_params=pltpu.CompilerParams(vmem_limit_bytes=48 * 1024 * 1024),
        cost_estimate=pl.CostEstimate(
            flops=2 * matmuls * tile_size * tile_size * feature_width,
            transcendentals=panel_dev * tile_size * feature_width,
            bytes_accessed=tiles.size * 2 + section_count * team_rows * feature_width * 6,
        ),
    )(coords.reshape(-1), counts.reshape(-1), *source_blocks, tiles, out_grad, weight)


def split_pick(block, index, axis):
    kept = lax.dynamic_index_in_dim(block, index, axis, keepdims=False)
    sent = lax.dynamic_index_in_dim(block, 1 - index, axis, keepdims=False)
    return kept, sent


def swap_with(block, axis, mask):
    size = lax.axis_size(axis)
    route = [(i, i ^ mask) for i in range(size)]
    return lax.ppermute(block, axis, route)


def body(features, weight, out_grad, tiles, coords, counts):
    panel_dev, section_count, slot_count, tile_size, _ = tiles.shape
    team_rows, feature_width = features.shape
    reach_size = (section_count - 1) // 2
    nodes_total = team_rows * lax.axis_size("team")
    rep_size = lax.axis_size("rep")
    blocks = neighbour_blocks(features, reach_size)
    source_blocks = [blocks[s - reach_size] for s in range(section_count)]
    activated, local_weight_grad, sums = layer_call(
        source_blocks, tiles, out_grad, weight, coords, counts
    )
    grad_weight = butterfly_sum(local_weight_grad, ("rep", "team")) * (1.0 / math.sqrt(nodes_total))

    rep_index = lax.axis_index("rep")
    if rep_size == 4:
        quarter = team_rows // 4
        staged = sums.reshape(section_count, 2, 2, quarter, feature_width)
        kept, sent = split_pick(staged, rep_index % 2, 2)
        kept = kept + swap_with(sent.astype(jnp.bfloat16), "rep", 1).astype(jnp.float32)
        kept, sent = split_pick(kept, rep_index // 2, 1)
        share = kept + swap_with(sent.astype(jnp.bfloat16), "rep", 2).astype(jnp.float32)
    else:
        share = lax.psum_scatter(sums, "rep", scatter_dimension=1, tiled=True)

    total = share[reach_size]
    for s in range(section_count):
        if s == reach_size:
            continue
        shift = s - reach_size
        arrived = from_behind(share[s].astype(jnp.bfloat16), "team", shift)
        total = total + arrived.astype(jnp.float32)
    gradient_share = total.astype(jnp.bfloat16)
    return (activated, grad_weight, gradient_share)


def solution(mesh):
    placed = (
        P("team", None),
        P(),
        P(("team", "rep"), None),
        P(("team", "rep"), None, None, None, None),
        P(("team", "rep"), None, None),
        P(("team", "rep"), None),
    )
    return jax.shard_map(
        body,
        mesh=mesh,
        in_specs=placed,
        out_specs=(P(("team", "rep"), None), P(), P(("team", "rep"), None)),
        check_vma=False,
    )
```

time: 280 us -> 142 us (0.51)
  the two profiles are of different devices: /device:TPU:1 before, /device:TPU:2 now
where the time goes in v2:
time: 142 us; the launch traced here: 141 us
  starting transfers between devices  80.6 us (57%)
  waiting for transfers between devices  44 us (31%)
  local copies, waits for them, and re-layouts  6.96 us (5%)
  Pallas kernels  4.47 us (3%)
  other arithmetic  3.79 us (3%)
    ppermute x8, starting transfers between devices, from_behind(): return lax.ppermute(block, axis, route)  46 us
    ppermute x9, waiting for transfers between devices, butterfly_sum(): block = block + lax.ppermute(block, axis, route)  35.1 us
    ppermute x9, starting transfers between devices, butterfly_sum(): block = block + lax.ppermute(block, axis, route)  28.3 us
    ppermute x8, waiting for transfers between devices, from_behind(): return lax.ppermute(block, axis, route)  8.94 us
    ppermute x2, starting transfers between devices, swap_with(): return lax.ppermute(block, axis, route)  6.25 us
    unnamed x13, local copies, waits for them, and re-layouts  5.94 us
    pallas_call x1, Pallas kernels, layer_call(): pl.pallas_call(kernel, out_shape=(jax.ShapeDtypeStruct(out_grad.shape, jn...  4.47 us
  transfers between devices with their start and end apart: 19, of which 11 were waited for; matrix products, arithmetic and copies ran while one was open for 3% of the time, Pallas kernels for 0%

profile of v2, /device:TPU:2, one launch (start us, length us, event | category | flops | bytes accessed | tf_op | source)
XLA Modules:
  0.0 140.8 jit_solution(7547482256792227555)
XLA Ops:
  0.6 3.8 %collective-permute-start = (bf16[1024,128]{1,0:T(8,128)(2,1)}, bf16[1024,128]{1,0:T(8,128)(2,1)S(1)}, u32[]{:S(2)}, u32[]{:S(2)}) collective-permute-start(bf16[1024,128]{1,0:T(8,128)(2,1)} %refs_2_.1), channel_id=1, source_target_pairs={{508,0},{0,4},{4,8},{8,12},{12,16},{16,20},{20,24},{24,28},{28,32}... | collective-permute-start | bytes 786440 | tf_op jit(solution)/shard_map/ppermute | solution.py:15
  4.5 11.9 %collective-permute-start.2 = (bf16[1024,128]{1,0:T(8,128)(2,1)}, bf16[1024,128]{1,0:T(8,128)(2,1)S(1)}, u32[]{:S(2)}, u32[]{:S(2)}) collective-permute-start(bf16[1024,128]{1,0:T(8,128)(2,1)} %refs_2_.1), channel_id=1, source_target_pairs={{4,0},{8,4},{12,8},{16,12},{20,16},{24,20},{28,24},{32,28},{36,32}... | collective-permute-start | bytes 786440 | tf_op jit(solution)/shard_map/ppermute | solution.py:15
  16.4 4.6 %collective-permute-done.refs_1_ = bf16[1024,128]{1,0:T(8,128)(2,1)S(1)} collective-permute-done((bf16[1024,128]{1,0:T(8,128)(2,1)}, bf16[1024,128]{1,0:T(8,128)(2,1)S(1)}, u32[]{:S(2)}, u32[]{:S(2)}) %collective-permute-start) | collective-permute-done | bytes 262176 | tf_op jit(solution)/shard_map/ppermute | solution.py:15
  22.9 8.1 %collective-permute-start.3 = (bf16[1024,128]{1,0:T(8,128)(2,1)S(1)}, bf16[1024,128]{1,0:T(8,128)(2,1)S(1)}, u32[]{:S(2)}, u32[]{:S(2)}) collective-permute-start(bf16[1024,128]{1,0:T(8,128)(2,1)S(1)} %collective-permute-done.2.refs_3_), channel_id=1, source_target_pairs={{4,0},{8,4},{12,8},{16,12},{20,16},{24,20},{28,24},{32,28},{36,32}... | collective-permute-start | bytes 786440 | tf_op jit(solution)/shard_map/ppermute | solution.py:15
  32.6 1.9 %collective-permute-done.1.refs_0_ = bf16[1024,128]{1,0:T(8,128)(2,1)S(1)} collective-permute-done((bf16[1024,128]{1,0:T(8,128)(2,1)S(1)}, bf16[1024,128]{1,0:T(8,128)(2,1)S(1)}, u32[]{:S(2)}, u32[]{:S(2)}) %collective-permute-start.1) | collective-permute-done | bytes 262176 | tf_op jit(solution)/shard_map/ppermute | solution.py:15
  39.9 4.5 %shard_map.85 = (bf16[256,128]{1,0:T(8,128)(2,1)}, f32[128,128]{1,0:T(8,128)S(1)}, f32[5,1024,128]{2,1,0:T(8,128)S(1)}) custom-call(s32[80]{0:T(128)S(1)} %reshape.21.coords_ref, s32[10]{0:T(128)S(1)} %reshape.22.counts_ref, bf16[1024,128]{1,0:T(8,128)(2,1)S(1)} %collective-permute-done.1.refs_0_, bf16[1024,128]{1,0:T(8,128)(2,1)S(1)} %collective-permute-done.refs_1_, ...), custom_call_target="tpu_custom_call" | custom-call | flops 704643072 | bytes 6553600 | tf_op jit(solution)/shard_map/pallas_call | solution.py:117
  44.5 1.9 %collective-permute-start.13 = (bf16[5,2,256,128]{3,2,0,1:T(8,128)(2,1)S(1)}, bf16[5,2,256,128]{3,2,0,1:T(8,128)(2,1)}, u32[]{:S(2)}, u32[]{:S(2)}) collective-permute-start(bf16[5,2,256,128]{3,2,0,1:T(8,128)(2,1)S(1)} %fusion), channel_id=1, source_target_pairs={{0,1},{1,0},{2,3},{3,2},{4,5},{5,4},{6,7},{7,6},{8,9},{9,8},{10,11... | collective-permute-start | bytes 1966088 | tf_op jit(solution)/shard_map/ppermute | solution.py:144
  46.4 2.4 %collective-permute-start.4 = (f32[128,128]{1,0:T(8,128)S(1)}, f32[128,128]{1,0:T(8,128)S(1)}, u32[]{:S(2)}, u32[]{:S(2)}) collective-permute-start(f32[128,128]{1,0:T(8,128)S(1)} %get-tuple-element.7), channel_id=1, source_target_pairs={{0,1},{1,0},{2,3},{3,2},{4,5},{5,4},{6,7},{7,6},{8,9},{9,8},{10,11... | collective-permute-start | bytes 196616 | tf_op jit(solution)/shard_map/ppermute | solution.py:27
  49.8 4.3 %collective-permute-start.5 = (f32[128,128]{1,0:T(8,128)S(1)}, f32[128,128]{1,0:T(8,128)S(1)}, u32[]{:S(2)}, u32[]{:S(2)}) collective-permute-start(f32[128,128]{1,0:T(8,128)S(1)} %add.66), channel_id=1, source_target_pairs={{0,2},{1,3},{2,0},{3,1},{4,6},{5,7},{6,4},{7,5},{8,10},{9,11},{10,... | collective-permute-start | bytes 196616 | tf_op jit(solution)/shard_map/ppermute | solution.py:27
  54.1 3.4 %collective-permute-done.5 = f32[128,128]{1,0:T(8,128)S(1)} collective-permute-done((f32[128,128]{1,0:T(8,128)S(1)}, f32[128,128]{1,0:T(8,128)S(1)}, u32[]{:S(2)}, u32[]{:S(2)}) %collective-permute-start.5) | collective-permute-done | bytes 65568 | tf_op jit(solution)/shard_map/ppermute | solution.py:27
  57.5 1.9 %collective-permute-start.6 = (f32[128,128]{1,0:T(8,128)S(1)}, f32[128,128]{1,0:T(8,128)S(1)}, u32[]{:S(2)}, u32[]{:S(2)}) collective-permute-start(f32[128,128]{1,0:T(8,128)S(1)} %add.67), channel_id=1, source_target_pairs={{0,4},{4,0},{8,12},{12,8},{16,20},{20,16},{24,28},{28,24},{32,36},... | collective-permute-start | bytes 196616 | tf_op jit(solution)/shard_map/ppermute | solution.py:27
  59.5 4.2 %collective-permute-done.6 = f32[128,128]{1,0:T(8,128)S(1)} collective-permute-done((f32[128,128]{1,0:T(8,128)S(1)}, f32[128,128]{1,0:T(8,128)S(1)}, u32[]{:S(2)}, u32[]{:S(2)}) %collective-permute-start.6) | collective-permute-done | bytes 65568 | tf_op jit(solution)/shard_map/ppermute | solution.py:27
  63.7 1.9 %collective-permute-start.7 = (f32[128,128]{1,0:T(8,128)S(1)}, f32[128,128]{1,0:T(8,128)S(1)}, u32[]{:S(2)}, u32[]{:S(2)}) collective-permute-start(f32[128,128]{1,0:T(8,128)S(1)} %add.68), channel_id=1, source_target_pairs={{0,8},{4,12},{8,0},{12,4},{16,24},{20,28},{24,16},{28,20},{32,40},... | collective-permute-start | bytes 196616 | tf_op jit(solution)/shard_map/ppermute | solution.py:27
  68.0 4.3 %collective-permute-start.14 = (bf16[5,256,128]{2,1,0:T(8,128)(2,1)S(1)}, bf16[5,256,128]{2,1,0:T(8,128)(2,1)S(1)}, u32[]{:S(2)}, u32[]{:S(2)}) collective-permute-start(bf16[5,256,128]{2,1,0:T(8,128)(2,1)S(1)} %fusion.1), channel_id=1, source_target_pairs={{0,2},{1,3},{2,0},{3,1},{4,6},{5,7},{6,4},{7,5},{8,10},{9,11},{10,... | collective-permute-start | bytes 983048 | tf_op jit(solution)/shard_map/ppermute | solution.py:144
  72.3 3.3 %collective-permute-start.8 = (f32[128,128]{1,0:T(8,128)S(1)}, f32[128,128]{1,0:T(8,128)S(1)}, u32[]{:S(2)}, u32[]{:S(2)}) collective-permute-start(f32[128,128]{1,0:T(8,128)S(1)} %add.69), channel_id=1, source_target_pairs={{0,16},{4,20},{8,24},{12,28},{16,0},{20,4},{24,8},{28,12},{32,48},... | collective-permute-start | bytes 196616 | tf_op jit(solution)/shard_map/ppermute | solution.py:27
  75.6 7.8 %collective-permute-done.8 = f32[128,128]{1,0:T(8,128)S(1)} collective-permute-done((f32[128,128]{1,0:T(8,128)S(1)}, f32[128,128]{1,0:T(8,128)S(1)}, u32[]{:S(2)}, u32[]{:S(2)}) %collective-permute-start.8) | collective-permute-done | bytes 65568 | tf_op jit(solution)/shard_map/ppermute | solution.py:27
  83.4 6.2 %collective-permute-start.9 = (f32[128,128]{1,0:T(8,128)S(1)}, f32[128,128]{1,0:T(8,128)S(1)}, u32[]{:S(2)}, u32[]{:S(2)}) collective-permute-start(f32[128,128]{1,0:T(8,128)S(1)} %add.70), channel_id=1, source_target_pairs={{0,32},{4,36},{8,40},{12,44},{16,48},{20,52},{24,56},{28,60},{32,0... | collective-permute-start | bytes 196616 | tf_op jit(solution)/shard_map/ppermute | solution.py:27
  89.6 8.9 %collective-permute-done.9 = f32[128,128]{1,0:T(8,128)S(1)} collective-permute-done((f32[128,128]{1,0:T(8,128)S(1)}, f32[128,128]{1,0:T(8,128)S(1)}, u32[]{:S(2)}, u32[]{:S(2)}) %collective-permute-start.9) | collective-permute-done | bytes 65568 | tf_op jit(solution)/shard_map/ppermute | solution.py:27
  100.4 4.2 %collective-permute-done.10 = f32[128,128]{1,0:T(8,128)S(1)} collective-permute-done((f32[128,128]{1,0:T(8,128)S(1)}, f32[128,128]{1,0:T(8,128)S(1)}, u32[]{:S(2)}, u32[]{:S(2)}) %collective-permute-start.10) | collective-permute-done | bytes 65568 | tf_op jit(solution)/shard_map/ppermute | solution.py:27
  106.6 5.7 %collective-permute-done.11 = f32[128,128]{1,0:T(8,128)S(1)} collective-permute-done((f32[128,128]{1,0:T(8,128)S(1)}, f32[128,128]{1,0:T(8,128)S(1)}, u32[]{:S(2)}, u32[]{:S(2)}) %collective-permute-start.11) | collective-permute-done | bytes 65568 | tf_op jit(solution)/shard_map/ppermute | solution.py:27
  112.4 4.3 %collective-permute-start.12 = (f32[128,128]{1,0:T(8,128)S(1)}, f32[128,128]{1,0:T(8,128)S(1)}, u32[]{:S(2)}, u32[]{:S(2)}) collective-permute-start(f32[128,128]{1,0:T(8,128)S(1)} %add.73), channel_id=1, source_target_pairs={{0,256},{4,260},{8,264},{12,268},{16,272},{20,276},{24,280},{28,28... | collective-permute-start | bytes 196616 | tf_op jit(solution)/shard_map/ppermute | solution.py:27
  117.9 7.1 %collective-permute-start.15 = (bf16[256,128]{1,0:T(8,128)(2,1)S(1)}, bf16[256,128]{1,0:T(8,128)(2,1)S(1)}, u32[]{:S(2)}, u32[]{:S(2)}) collective-permute-start(bf16[256,128]{1,0:T(8,128)(2,1)S(1)} %get-tuple-element.11), channel_id=1, source_target_pairs={{8,0},{12,4},{16,8},{20,12},{24,16},{28,20},{32,24},{36,28},{40,32... | collective-permute-start | bytes 196616 | tf_op jit(solution)/shard_map/ppermute | solution.py:15
  127.0 3.7 %collective-permute-start.17 = (bf16[256,128]{1,0:T(8,128)(2,1)S(1)}, bf16[256,128]{1,0:T(8,128)(2,1)S(1)}, u32[]{:S(2)}, u32[]{:S(2)}) collective-permute-start(bf16[256,128]{1,0:T(8,128)(2,1)S(1)} %get-tuple-element.13), channel_id=1, source_target_pairs={{508,0},{0,4},{4,8},{8,12},{12,16},{16,20},{20,24},{24,28},{28,32}... | collective-permute-start | bytes 196616 | tf_op jit(solution)/shard_map/ppermute | solution.py:15
  130.6 7.6 %collective-permute-start.16 = (bf16[256,128]{1,0:T(8,128)(2,1)S(1)}, bf16[256,128]{1,0:T(8,128)(2,1)S(1)}, u32[]{:S(2)}, u32[]{:S(2)}) collective-permute-start(bf16[256,128]{1,0:T(8,128)(2,1)S(1)} %get-tuple-element.14), channel_id=1, source_target_pairs={{4,0},{8,4},{12,8},{16,12},{20,16},{24,20},{28,24},{32,28},{36,32}... | collective-permute-start | bytes 196616 | tf_op jit(solution)/shard_map/ppermute | solution.py:15
  (45 shorter events, 21.7 us)
Async XLA Ops:
  0.6 20.3 %collective-permute-start = (bf16[1024,128]{1,0:T(8,128)(2,1)}, bf16[1024,128]{1,0:T(8,128)(2,1)S(1)}, u32[]{:S(2)}, u32[]{:S(2)}) collective-permute-start(bf16[1024,128]{1,0:T(8,128)(2,1)} %refs_2_.1), channel_id=1, source_target_pairs={{508,0},{0,4},{4,8},{8,12},{12,16},{16,20},{20,24},{24,28},{28,32}... | collective-permute-start | bytes 786440 | tf_op jit(solution)/shard_map/ppermute | solution.py:15
  4.5 18.4 %collective-permute-start.2 = (bf16[1024,128]{1,0:T(8,128)(2,1)}, bf16[1024,128]{1,0:T(8,128)(2,1)S(1)}, u32[]{:S(2)}, u32[]{:S(2)}) collective-permute-start(bf16[1024,128]{1,0:T(8,128)(2,1)} %refs_2_.1), channel_id=1, source_target_pairs={{4,0},{8,4},{12,8},{16,12},{20,16},{24,20},{28,24},{32,28},{36,32}... | collective-permute-start | bytes 786440 | tf_op jit(solution)/shard_map/ppermute | solution.py:15
  21.0 13.6 %collective-permute-start.1 = (bf16[1024,128]{1,0:T(8,128)(2,1)S(1)}, bf16[1024,128]{1,0:T(8,128)(2,1)S(1)}, u32[]{:S(2)}, u32[]{:S(2)}) collective-permute-start(bf16[1024,128]{1,0:T(8,128)(2,1)S(1)} %collective-permute-done.refs_1_), channel_id=1, source_target_pairs={{508,0},{0,4},{4,8},{8,12},{12,16},{16,20},{20,24},{24,28},{28,32}... | collective-permute-start | bytes 786440 | tf_op jit(solution)/shard_map/ppermute | solution.py:15
  22.9 12.8 %collective-permute-start.3 = (bf16[1024,128]{1,0:T(8,128)(2,1)S(1)}, bf16[1024,128]{1,0:T(8,128)(2,1)S(1)}, u32[]{:S(2)}, u32[]{:S(2)}) collective-permute-start(bf16[1024,128]{1,0:T(8,128)(2,1)S(1)} %collective-permute-done.2.refs_3_), channel_id=1, source_target_pairs={{4,0},{8,4},{12,8},{16,12},{20,16},{24,20},{28,24},{32,28},{36,32}... | collective-permute-start | bytes 786440 | tf_op jit(solution)/shard_map/ppermute | solution.py:15
  36.4 0.9 copy-start
  37.4 0.9 copy-start.2
  38.3 0.8 copy-start.3
  39.2 0.8 copy-start.4
  44.5 21.1 %collective-permute-start.13 = (bf16[5,2,256,128]{3,2,0,1:T(8,128)(2,1)S(1)}, bf16[5,2,256,128]{3,2,0,1:T(8,128)(2,1)}, u32[]{:S(2)}, u32[]{:S(2)}) collective-permute-start(bf16[5,2,256,128]{3,2,0,1:T(8,128)(2,1)S(1)} %fusion), channel_id=1, source_target_pairs={{0,1},{1,0},{2,3},{3,2},{4,5},{5,4},{6,7},{7,6},{8,9},{9,8},{10,11... | collective-permute-start | bytes 1966088 | tf_op jit(solution)/shard_map/ppermute | solution.py:144
  46.4 3.3 %collective-permute-start.4 = (f32[128,128]{1,0:T(8,128)S(1)}, f32[128,128]{1,0:T(8,128)S(1)}, u32[]{:S(2)}, u32[]{:S(2)}) collective-permute-start(f32[128,128]{1,0:T(8,128)S(1)} %get-tuple-element.7), channel_id=1, source_target_pairs={{0,1},{1,0},{2,3},{3,2},{4,5},{5,4},{6,7},{7,6},{8,9},{9,8},{10,11... | collective-permute-start | bytes 196616 | tf_op jit(solution)/shard_map/ppermute | solution.py:27
  49.8 7.7 %collective-permute-start.5 = (f32[128,128]{1,0:T(8,128)S(1)}, f32[128,128]{1,0:T(8,128)S(1)}, u32[]{:S(2)}, u32[]{:S(2)}) collective-permute-start(f32[128,128]{1,0:T(8,128)S(1)} %add.66), channel_id=1, source_target_pairs={{0,2},{1,3},{2,0},{3,1},{4,6},{5,7},{6,4},{7,5},{8,10},{9,11},{10,... | collective-permute-start | bytes 196616 | tf_op jit(solution)/shard_map/ppermute | solution.py:27
  57.5 6.2 %collective-permute-start.6 = (f32[128,128]{1,0:T(8,128)S(1)}, f32[128,128]{1,0:T(8,128)S(1)}, u32[]{:S(2)}, u32[]{:S(2)}) collective-permute-start(f32[128,128]{1,0:T(8,128)S(1)} %add.67), channel_id=1, source_target_pairs={{0,4},{4,0},{8,12},{12,8},{16,20},{20,16},{24,28},{28,24},{32,36},... | collective-permute-start | bytes 196616 | tf_op jit(solution)/shard_map/ppermute | solution.py:27
  63.7 8.6 %collective-permute-start.7 = (f32[128,128]{1,0:T(8,128)S(1)}, f32[128,128]{1,0:T(8,128)S(1)}, u32[]{:S(2)}, u32[]{:S(2)}) collective-permute-start(f32[128,128]{1,0:T(8,128)S(1)} %add.68), channel_id=1, source_target_pairs={{0,8},{4,12},{8,0},{12,4},{16,24},{20,28},{24,16},{28,20},{32,40},... | collective-permute-start | bytes 196616 | tf_op jit(solution)/shard_map/ppermute | solution.py:27
  66.8 1.1 copy-start.5
  68.0 48.7 %collective-permute-start.14 = (bf16[5,256,128]{2,1,0:T(8,128)(2,1)S(1)}, bf16[5,256,128]{2,1,0:T(8,128)(2,1)S(1)}, u32[]{:S(2)}, u32[]{:S(2)}) collective-permute-start(bf16[5,256,128]{2,1,0:T(8,128)(2,1)S(1)} %fusion.1), channel_id=1, source_target_pairs={{0,2},{1,3},{2,0},{3,1},{4,6},{5,7},{6,4},{7,5},{8,10},{9,11},{10,... | collective-permute-start | bytes 983048 | tf_op jit(solution)/shard_map/ppermute | solution.py:144
  72.3 11.1 %collective-permute-start.8 = (f32[128,128]{1,0:T(8,128)S(1)}, f32[128,128]{1,0:T(8,128)S(1)}, u32[]{:S(2)}, u32[]{:S(2)}) collective-permute-start(f32[128,128]{1,0:T(8,128)S(1)} %add.69), channel_id=1, source_target_pairs={{0,16},{4,20},{8,24},{12,28},{16,0},{20,4},{24,8},{28,12},{32,48},... | collective-permute-start | bytes 196616 | tf_op jit(solution)/shard_map/ppermute | solution.py:27
  83.4 15.1 %collective-permute-start.9 = (f32[128,128]{1,0:T(8,128)S(1)}, f32[128,128]{1,0:T(8,128)S(1)}, u32[]{:S(2)}, u32[]{:S(2)}) collective-permute-start(f32[128,128]{1,0:T(8,128)S(1)} %add.70), channel_id=1, source_target_pairs={{0,32},{4,36},{8,40},{12,44},{16,48},{20,52},{24,56},{28,60},{32,0... | collective-permute-start | bytes 196616 | tf_op jit(solution)/shard_map/ppermute | solution.py:27
  98.5 6.2 %collective-permute-start.10 = (f32[128,128]{1,0:T(8,128)S(1)}, f32[128,128]{1,0:T(8,128)S(1)}, u32[]{:S(2)}, u32[]{:S(2)}) collective-permute-start(f32[128,128]{1,0:T(8,128)S(1)} %add.71), channel_id=1, source_target_pairs={{0,64},{4,68},{8,72},{12,76},{16,80},{20,84},{24,88},{28,92},{32,9... | collective-permute-start | bytes 196616 | tf_op jit(solution)/shard_map/ppermute | solution.py:27
  104.7 7.7 %collective-permute-start.11 = (f32[128,128]{1,0:T(8,128)S(1)}, f32[128,128]{1,0:T(8,128)S(1)}, u32[]{:S(2)}, u32[]{:S(2)}) collective-permute-start(f32[128,128]{1,0:T(8,128)S(1)} %add.72), channel_id=1, source_target_pairs={{0,128},{4,132},{8,136},{12,140},{16,144},{20,148},{24,152},{28,15... | collective-permute-start | bytes 196616 | tf_op jit(solution)/shard_map/ppermute | solution.py:27
  112.4 25.9 %collective-permute-start.12 = (f32[128,128]{1,0:T(8,128)S(1)}, f32[128,128]{1,0:T(8,128)S(1)}, u32[]{:S(2)}, u32[]{:S(2)}) collective-permute-start(f32[128,128]{1,0:T(8,128)S(1)} %add.73), channel_id=1, source_target_pairs={{0,256},{4,260},{8,264},{12,268},{16,272},{20,276},{24,280},{28,28... | collective-permute-start | bytes 196616 | tf_op jit(solution)/shard_map/ppermute | solution.py:27
  117.9 20.9 %collective-permute-start.15 = (bf16[256,128]{1,0:T(8,128)(2,1)S(1)}, bf16[256,128]{1,0:T(8,128)(2,1)S(1)}, u32[]{:S(2)}, u32[]{:S(2)}) collective-permute-start(bf16[256,128]{1,0:T(8,128)(2,1)S(1)} %get-tuple-element.11), channel_id=1, source_target_pairs={{8,0},{12,4},{16,8},{20,12},{24,16},{28,20},{32,24},{36,28},{40,32... | collective-permute-start | bytes 196616 | tf_op jit(solution)/shard_map/ppermute | solution.py:15
  125.0 13.8 %collective-permute-start.18 = (bf16[256,128]{1,0:T(8,128)(2,1)S(1)}, bf16[256,128]{1,0:T(8,128)(2,1)S(1)}, u32[]{:S(2)}, u32[]{:S(2)}) collective-permute-start(bf16[256,128]{1,0:T(8,128)(2,1)S(1)} %get-tuple-element.12), channel_id=1, source_target_pairs={{504,0},{508,4},{0,8},{4,12},{8,16},{12,20},{16,24},{20,28},{24,32... | collective-permute-start | bytes 196616 | tf_op jit(solution)/shard_map/ppermute | solution.py:15
  127.0 11.9 %collective-permute-start.17 = (bf16[256,128]{1,0:T(8,128)(2,1)S(1)}, bf16[256,128]{1,0:T(8,128)(2,1)S(1)}, u32[]{:S(2)}, u32[]{:S(2)}) collective-permute-start(bf16[256,128]{1,0:T(8,128)(2,1)S(1)} %get-tuple-element.13), channel_id=1, source_target_pairs={{508,0},{0,4},{4,8},{8,12},{12,16},{16,20},{20,24},{24,28},{28,32}... | collective-permute-start | bytes 196616 | tf_op jit(solution)/shard_map/ppermute | solution.py:15
  130.6 9.5 %collective-permute-start.16 = (bf16[256,128]{1,0:T(8,128)(2,1)S(1)}, bf16[256,128]{1,0:T(8,128)(2,1)S(1)}, u32[]{:S(2)}, u32[]{:S(2)}) collective-permute-start(bf16[256,128]{1,0:T(8,128)(2,1)S(1)} %get-tuple-element.14), channel_id=1, source_target_pairs={{4,0},{8,4},{12,8},{16,12},{20,16},{24,20},{28,24},{32,28},{36,32}... | collective-permute-start | bytes 196616 | tf_op jit(solution)/shard_map/ppermute | solution.py:15
  (1 other events, 0.7 us)

commit v3 on v2

--- a/solution.py
+++ b/solution.py
@@ -132,16 +132,21 @@
     )(coords.reshape(-1), counts.reshape(-1), *source_blocks, tiles, out_grad, weight)
 
 
-def split_pick(block, index, axis):
-    kept = lax.dynamic_index_in_dim(block, index, axis, keepdims=False)
-    sent = lax.dynamic_index_in_dim(block, 1 - index, axis, keepdims=False)
-    return kept, sent
-
-
 def swap_with(block, axis, mask):
     size = lax.axis_size(axis)
     route = [(i, i ^ mask) for i in range(size)]
     return lax.ppermute(block, axis, route)
+
+
+def team_total_sum(block):
+    size = lax.axis_size("team")
+    rows = block.shape[0]
+    if rows % size:
+        return butterfly_sum(block, ("team",))
+    pieces = lax.all_to_all(block.reshape(size, rows // size, -1), "team", 0, 0, tiled=True)
+    own = jnp.sum(pieces, axis=0)
+    copies = jnp.broadcast_to(own[None], (size,) + own.shape)
+    return lax.all_to_all(copies, "team", 0, 0, tiled=True).reshape(block.shape)
 
 
 def body(features, weight, out_grad, tiles, coords, counts):
@@ -150,32 +155,53 @@
     reach_size = (section_count - 1) // 2
     nodes_total = team_rows * lax.axis_size("team")
     rep_size = lax.axis_size("rep")
-    blocks = neighbour_blocks(features, reach_size)
-    source_blocks = [blocks[s - reach_size] for s in range(section_count)]
+    source_blocks = [
+        features if s == reach_size else from_behind(features, "team", reach_size - s)
+        for s in range(section_count)
+    ]
     activated, local_weight_grad, sums = layer_call(
         source_blocks, tiles, out_grad, weight, coords, counts
     )
-    grad_weight = butterfly_sum(local_weight_grad, ("rep", "team")) * (1.0 / math.sqrt(nodes_total))
+    if rep_size != 4:
+        grad_weight = butterfly_sum(local_weight_grad, ("rep", "team"))
+        share = lax.psum_scatter(sums, "rep", scatter_dimension=1, tiled=True)
+        total = share[reach_size]
+        for s in range(section_count):
+            if s != reach_size:
+                arrived = from_behind(share[s].astype(jnp.bfloat16), "team", s - reach_size)
+                total = total + arrived.astype(jnp.float32)
+        return (activated, grad_weight * (1.0 / math.sqrt(nodes_total)), total.astype(jnp.bfloat16))
 
     rep_index = lax.axis_index("rep")
-    if rep_size == 4:
-        quarter = team_rows // 4
-        staged = sums.reshape(section_count, 2, 2, quarter, feature_width)
-        kept, sent = split_pick(staged, rep_index % 2, 2)
-        kept = kept + swap_with(sent.astype(jnp.bfloat16), "rep", 1).astype(jnp.float32)
-        kept, sent = split_pick(kept, rep_index // 2, 1)
-        share = kept + swap_with(sent.astype(jnp.bfloat16), "rep", 2).astype(jnp.float32)
-    else:
-        share = lax.psum_scatter(sums, "rep", scatter_dimension=1, tiled=True)
-
-    total = share[reach_size]
+    core_bit = rep_index % 2
+    chip_bit = rep_index // 2
+    quarter = team_rows // 4
+    half_rows = 2 * quarter
+    staged = sums.reshape(section_count, 2, 2, quarter, feature_width)
+    kept = lax.dynamic_index_in_dim(staged, core_bit, 2, keepdims=False)
+    sent = lax.dynamic_index_in_dim(staged, 1 - core_bit, 2, keepdims=False)
+    packet = jnp.concatenate(
+        [sent.reshape(section_count * half_rows, feature_width), local_weight_grad], axis=0
+    )
+    arrived = swap_with(packet, "rep", 1)
+    kept = kept.reshape(section_count, half_rows, feature_width) + arrived[
+        : section_count * half_rows
+    ].reshape(section_count, half_rows, feature_width)
+    weight_grad = local_weight_grad + arrived[section_count * half_rows :]
+
+    total = kept[reach_size]
     for s in range(section_count):
-        if s == reach_size:
-            continue
-        shift = s - reach_size
-        arrived = from_behind(share[s].astype(jnp.bfloat16), "team", shift)
-        total = total + arrived.astype(jnp.float32)
-    gradient_share = total.astype(jnp.bfloat16)
+        if s != reach_size:
+            moved = from_behind(kept[s].astype(jnp.bfloat16), "team", s - reach_size)
+            total = total + moved.astype(jnp.float32)
+
+    staged = total.reshape(2, quarter, feature_width)
+    kept = lax.dynamic_index_in_dim(staged, chip_bit, 0, keepdims=False)
+    sent = lax.dynamic_index_in_dim(staged, 1 - chip_bit, 0, keepdims=False)
+    arrived = swap_with(jnp.concatenate([sent, weight_grad], axis=0), "rep", 2)
+    gradient_share = (kept + arrived[:quarter]).astype(jnp.bfloat16)
+    weight_grad = weight_grad + arrived[quarter:]
+    grad_weight = team_total_sum(weight_grad) * (1.0 / math.sqrt(nodes_total))
     return (activated, grad_weight, gradient_share)
 
 

time: 142 us -> 137 us (0.965)
  the two profiles are of different devices: /device:TPU:2 before, /device:TPU:4 now
where the time goes in v3:
time: 137 us; the launch traced here: 136 us
  starting transfers between devices  59.2 us (43%)
  waiting for transfers between devices  37.6 us (27%)
  blocking collectives  23.5 us (17%)
  local copies, waits for them, and re-layouts  6.39 us (5%)
  Pallas kernels  4.49 us (3%)
  other arithmetic  3.85 us (3%)
    ppermute x8, starting transfers between devices, from_behind(): return lax.ppermute(block, axis, route)  48.7 us
    all_to_all x1, blocking collectives, team_total_sum(): lax.all_to_all(block.reshape(size, rows // size, -1), 'team', 0, 0, tiled...  23.5 us
    all_to_all x1, waiting for transfers between devices, team_total_sum(): return lax.all_to_all(copies, 'team', 0, 0, tiled=True).reshape(block.shape)  14.6 us
    ppermute x8, waiting for transfers between devices, from_behind(): return lax.ppermute(block, axis, route)  12.4 us
    ppermute x2, waiting for transfers between devices, swap_with(): return lax.ppermute(block, axis, route)  10.7 us
    all_to_all x1, starting transfers between devices, team_total_sum(): return lax.all_to_all(copies, 'team', 0, 0, tiled=True).reshape(block.shape)  6.15 us
    pallas_call x1, Pallas kernels, layer_call(): pl.pallas_call(kernel, out_shape=(jax.ShapeDtypeStruct(out_grad.shape, jn...  4.49 us
    ppermute x2, starting transfers between devices, swap_with(): return lax.ppermute(block, axis, route)  4.29 us
  transfers between devices with their start and end apart: 11, of which 7 were waited for; matrix products, arithmetic and copies ran while one was open for 2% of the time, Pallas kernels for 0%

profile of v3, /device:TPU:4, one launch (start us, length us, event | category | flops | bytes accessed | tf_op | source)
XLA Modules:
  0.0 135.8 jit_solution(10442170203663187638)
XLA Ops:
  0.6 14.5 %collective-permute-start.2 = (bf16[1024,128]{1,0:T(8,128)(2,1)}, bf16[1024,128]{1,0:T(8,128)(2,1)S(1)}, u32[]{:S(2)}, u32[]{:S(2)}) collective-permute-start(bf16[1024,128]{1,0:T(8,128)(2,1)} %refs_2_.1), channel_id=1, source_target_pairs={{4,0},{8,4},{12,8},{16,12},{20,16},{24,20},{28,24},{32,28},{36,32}... | collective-permute-start | bytes 786440 | tf_op jit(solution)/shard_map/ppermute | solution.py:15
  15.1 1.9 %collective-permute-start.1 = (bf16[1024,128]{1,0:T(8,128)(2,1)}, bf16[1024,128]{1,0:T(8,128)(2,1)S(1)}, u32[]{:S(2)}, u32[]{:S(2)}) collective-permute-start(bf16[1024,128]{1,0:T(8,128)(2,1)} %refs_2_.1), channel_id=1, source_target_pairs={{508,0},{0,4},{4,8},{8,12},{12,16},{16,20},{20,24},{24,28},{28,32}... | collective-permute-start | bytes 786440 | tf_op jit(solution)/shard_map/ppermute | solution.py:15
  17.1 1.9 %collective-permute-start = (bf16[1024,128]{1,0:T(8,128)(2,1)}, bf16[1024,128]{1,0:T(8,128)(2,1)S(1)}, u32[]{:S(2)}, u32[]{:S(2)}) collective-permute-start(bf16[1024,128]{1,0:T(8,128)(2,1)} %refs_2_.1), channel_id=1, source_target_pairs={{504,0},{508,4},{0,8},{4,12},{8,16},{12,20},{16,24},{20,28},{24,32... | collective-permute-start | bytes 786440 | tf_op jit(solution)/shard_map/ppermute | solution.py:15
  19.0 9.0 %collective-permute-start.3 = (bf16[1024,128]{1,0:T(8,128)(2,1)}, bf16[1024,128]{1,0:T(8,128)(2,1)S(1)}, u32[]{:S(2)}, u32[]{:S(2)}) collective-permute-start(bf16[1024,128]{1,0:T(8,128)(2,1)} %refs_2_.1), channel_id=1, source_target_pairs={{8,0},{12,4},{16,8},{20,12},{24,16},{28,20},{32,24},{36,28},{40,32... | collective-permute-start | bytes 786440 | tf_op jit(solution)/shard_map/ppermute | solution.py:15
  29.6 6.7 %collective-permute-done.1.refs_1_ = bf16[1024,128]{1,0:T(8,128)(2,1)S(1)} collective-permute-done((bf16[1024,128]{1,0:T(8,128)(2,1)}, bf16[1024,128]{1,0:T(8,128)(2,1)S(1)}, u32[]{:S(2)}, u32[]{:S(2)}) %collective-permute-start.1) | collective-permute-done | bytes 262176 | tf_op jit(solution)/shard_map/ppermute | solution.py:15
  36.2 2.7 %collective-permute-done.3.refs_4_ = bf16[1024,128]{1,0:T(8,128)(2,1)S(1)} collective-permute-done((bf16[1024,128]{1,0:T(8,128)(2,1)}, bf16[1024,128]{1,0:T(8,128)(2,1)S(1)}, u32[]{:S(2)}, u32[]{:S(2)}) %collective-permute-start.3) | collective-permute-done | bytes 262176 | tf_op jit(solution)/shard_map/ppermute | solution.py:15
  39.0 0.9 copy-done
  39.9 0.8 copy-done.1
  41.5 4.5 %shard_map.85 = (bf16[256,128]{1,0:T(8,128)(2,1)}, f32[128,128]{1,0:T(8,128)S(1)}, f32[5,1024,128]{2,1,0:T(8,128)S(1)}) custom-call(s32[80]{0:T(128)S(1)} %reshape.44.coords_ref, s32[10]{0:T(128)S(1)} %reshape.45.counts_ref, bf16[1024,128]{1,0:T(8,128)(2,1)S(1)} %collective-permute-done.refs_0_, bf16[1024,128]{1,0:T(8,128)(2,1)S(1)} %collective-permute-done.1.refs_1_, ...), custom_call_target="tpu_custom_call" | custom-call | flops 704643072 | bytes 6553600 | tf_op jit(solution)/shard_map/pallas_call | solution.py:117
  46.2 1.2 pad_maximum_fusion
  47.4 1.9 %collective-permute-start.4 = (f32[2688,128]{1,0:T(8,128)}, f32[2688,128]{1,0:T(8,128)}, u32[]{:S(2)}, u32[]{:S(2)}) collective-permute-start(f32[2688,128]{1,0:T(8,128)} %pad_maximum_fusion), channel_id=1, source_target_pairs={{0,1},{1,0},{2,3},{3,2},{4,5},{5,4},{6,7},{7,6},{8,9},{9,8},{10,11... | collective-permute-start | bytes 4128776 | tf_op jit(solution)/shard_map/ppermute | solution.py:138
  49.3 3.4 %collective-permute-done.4 = f32[2688,128]{1,0:T(8,128)} collective-permute-done((f32[2688,128]{1,0:T(8,128)}, f32[2688,128]{1,0:T(8,128)}, u32[]{:S(2)}, u32[]{:S(2)}) %collective-permute-start.4) | collective-permute-done | bytes 1376288 | tf_op jit(solution)/shard_map/ppermute | solution.py:138
  52.7 1.4 %slice.41 = f32[2560,128]{1,0:T(8,128)S(1)} slice(f32[2688,128]{1,0:T(8,128)} %collective-permute-done.4), slice={[0:2560], [0:128]} | slice | bytes 2621440 | tf_op jit(solution)/shard_map/slice | solution.py:187
  54.4 9.4 %collective-permute-start.5 = (bf16[512,128]{1,0:T(8,128)(2,1)S(1)}, bf16[512,128]{1,0:T(8,128)(2,1)S(1)}, u32[]{:S(2)}, u32[]{:S(2)}) collective-permute-start(bf16[512,128]{1,0:T(8,128)(2,1)S(1)} %get-tuple-element.13), channel_id=1, source_target_pairs={{8,0},{12,4},{16,8},{20,12},{24,16},{28,20},{32,24},{36,28},{40,32... | collective-permute-start | bytes 393224 | tf_op jit(solution)/shard_map/ppermute | solution.py:15
  63.8 1.9 %collective-permute-start.8 = (bf16[512,128]{1,0:T(8,128)(2,1)S(1)}, bf16[512,128]{1,0:T(8,128)(2,1)S(1)}, u32[]{:S(2)}, u32[]{:S(2)}) collective-permute-start(bf16[512,128]{1,0:T(8,128)(2,1)S(1)} %get-tuple-element.14), channel_id=1, source_target_pairs={{504,0},{508,4},{0,8},{4,12},{8,16},{12,20},{16,24},{20,28},{24,32... | collective-permute-start | bytes 393224 | tf_op jit(solution)/shard_map/ppermute | solution.py:15
  65.7 1.9 %collective-permute-start.7 = (bf16[512,128]{1,0:T(8,128)(2,1)S(1)}, bf16[512,128]{1,0:T(8,128)(2,1)S(1)}, u32[]{:S(2)}, u32[]{:S(2)}) collective-permute-start(bf16[512,128]{1,0:T(8,128)(2,1)S(1)} %get-tuple-element.15), channel_id=1, source_target_pairs={{508,0},{0,4},{4,8},{8,12},{12,16},{16,20},{20,24},{24,28},{28,32}... | collective-permute-start | bytes 393224 | tf_op jit(solution)/shard_map/ppermute | solution.py:15
  67.6 8.1 %collective-permute-start.6 = (bf16[512,128]{1,0:T(8,128)(2,1)S(1)}, bf16[512,128]{1,0:T(8,128)(2,1)S(1)}, u32[]{:S(2)}, u32[]{:S(2)}) collective-permute-start(bf16[512,128]{1,0:T(8,128)(2,1)S(1)} %get-tuple-element.16), channel_id=1, source_target_pairs={{4,0},{8,4},{12,8},{16,12},{20,16},{24,20},{28,24},{32,28},{36,32}... | collective-permute-start | bytes 393224 | tf_op jit(solution)/shard_map/ppermute | solution.py:15
  75.8 0.8 slice_add_fusion.2
  77.0 2.6 %collective-permute-done.7 = bf16[512,128]{1,0:T(8,128)(2,1)S(1)} collective-permute-done((bf16[512,128]{1,0:T(8,128)(2,1)S(1)}, bf16[512,128]{1,0:T(8,128)(2,1)S(1)}, u32[]{:S(2)}, u32[]{:S(2)}) %collective-permute-start.7) | collective-permute-done | bytes 131104 | tf_op jit(solution)/shard_map/ppermute | solution.py:15
  79.8 2.4 %collective-permute-start.9 = (f32[384,128]{1,0:T(8,128)S(1)}, f32[384,128]{1,0:T(8,128)S(1)}, u32[]{:S(2)}, u32[]{:S(2)}) collective-permute-start(f32[384,128]{1,0:T(8,128)S(1)} %pad_maximum_fusion.1), channel_id=1, source_target_pairs={{0,2},{1,3},{2,0},{3,1},{4,6},{5,7},{6,4},{7,5},{8,10},{9,11},{10,... | collective-permute-start | bytes 589832 | tf_op jit(solution)/shard_map/ppermute | solution.py:138
  82.2 7.2 %collective-permute-done.9 = f32[384,128]{1,0:T(8,128)S(1)} collective-permute-done((f32[384,128]{1,0:T(8,128)S(1)}, f32[384,128]{1,0:T(8,128)S(1)}, u32[]{:S(2)}, u32[]{:S(2)}) %collective-permute-start.9) | collective-permute-done | bytes 196640 | tf_op jit(solution)/shard_map/ppermute | solution.py:138
  89.4 23.5 %all_to_all.10 = f32[128,1,128]{2,1,0:T(1,128)S(1)} all-to-all(f32[128,1,128]{2,1,0:T(1,128)S(1)} %bitcast.38), channel_id=1, replica_groups=mesh['team'=128,'rep'=4] {'team'}, dimensions={0} | all-to-all | bytes 131072 | tf_op jit(solution)/shard_map/all_to_all | solution.py:146
  113.8 6.1 %all-to-all-start.1 = ((f32[128,1,128]{2,1,0:T(1,128)}), f32[128,1,128]{2,1,0:T(1,128)S(1)}, u32[]{:S(2)}, u32[]{:S(2)}) async-start(f32[128,1,128]{2,1,0:T(1,128)} %broadcast_in_dim.2), calls=%async_computation.1 | async-start | bytes 131072 | tf_op jit(solution)/shard_map/all_to_all | solution.py:149
  120.6 14.6 %all-to-all-done.1 = f32[128,1,128]{2,1,0:T(1,128)S(1)} async-done(((f32[128,1,128]{2,1,0:T(1,128)}), f32[128,1,128]{2,1,0:T(1,128)S(1)}, u32[]{:S(2)}, u32[]{:S(2)}) %all-to-all-start.1) | async-done | bytes 65568 | tf_op jit(solution)/shard_map/all_to_all | solution.py:149
  (23 shorter events, 5.4 us)
Async XLA Ops:
  0.6 29.0 %collective-permute-start.2 = (bf16[1024,128]{1,0:T(8,128)(2,1)}, bf16[1024,128]{1,0:T(8,128)(2,1)S(1)}, u32[]{:S(2)}, u32[]{:S(2)}) collective-permute-start(bf16[1024,128]{1,0:T(8,128)(2,1)} %refs_2_.1), channel_id=1, source_target_pairs={{4,0},{8,4},{12,8},{16,12},{20,16},{24,20},{28,24},{32,28},{36,32}... | collective-permute-start | bytes 786440 | tf_op jit(solution)/shard_map/ppermute | solution.py:15
  15.1 21.1 %collective-permute-start.1 = (bf16[1024,128]{1,0:T(8,128)(2,1)}, bf16[1024,128]{1,0:T(8,128)(2,1)S(1)}, u32[]{:S(2)}, u32[]{:S(2)}) collective-permute-start(bf16[1024,128]{1,0:T(8,128)(2,1)} %refs_2_.1), channel_id=1, source_target_pairs={{508,0},{0,4},{4,8},{8,12},{12,16},{16,20},{20,24},{24,28},{28,32}... | collective-permute-start | bytes 786440 | tf_op jit(solution)/shard_map/ppermute | solution.py:15
  17.1 19.2 %collective-permute-start = (bf16[1024,128]{1,0:T(8,128)(2,1)}, bf16[1024,128]{1,0:T(8,128)(2,1)S(1)}, u32[]{:S(2)}, u32[]{:S(2)}) collective-permute-start(bf16[1024,128]{1,0:T(8,128)(2,1)} %refs_2_.1), channel_id=1, source_target_pairs={{504,0},{508,4},{0,8},{4,12},{8,16},{12,20},{16,24},{20,28},{24,32... | collective-permute-start | bytes 786440 | tf_op jit(solution)/shard_map/ppermute | solution.py:15
  19.0 20.0 %collective-permute-start.3 = (bf16[1024,128]{1,0:T(8,128)(2,1)}, bf16[1024,128]{1,0:T(8,128)(2,1)S(1)}, u32[]{:S(2)}, u32[]{:S(2)}) collective-permute-start(bf16[1024,128]{1,0:T(8,128)(2,1)} %refs_2_.1), channel_id=1, source_target_pairs={{8,0},{12,4},{16,8},{20,12},{24,16},{28,20},{32,24},{36,28},{40,32... | collective-permute-start | bytes 786440 | tf_op jit(solution)/shard_map/ppermute | solution.py:15
  39.0 0.9 copy-start
  39.9 0.8 copy-start.1
  40.7 0.8 copy-start.2
  47.4 5.4 %collective-permute-start.4 = (f32[2688,128]{1,0:T(8,128)}, f32[2688,128]{1,0:T(8,128)}, u32[]{:S(2)}, u32[]{:S(2)}) collective-permute-start(f32[2688,128]{1,0:T(8,128)} %pad_maximum_fusion), channel_id=1, source_target_pairs={{0,1},{1,0},{2,3},{3,2},{4,5},{5,4},{6,7},{7,6},{8,9},{9,8},{10,11... | collective-permute-start | bytes 4128776 | tf_op jit(solution)/shard_map/ppermute | solution.py:138
  54.4 22.3 %collective-permute-start.5 = (bf16[512,128]{1,0:T(8,128)(2,1)S(1)}, bf16[512,128]{1,0:T(8,128)(2,1)S(1)}, u32[]{:S(2)}, u32[]{:S(2)}) collective-permute-start(bf16[512,128]{1,0:T(8,128)(2,1)S(1)} %get-tuple-element.13), channel_id=1, source_target_pairs={{8,0},{12,4},{16,8},{20,12},{24,16},{28,20},{32,24},{36,28},{40,32... | collective-permute-start | bytes 393224 | tf_op jit(solution)/shard_map/ppermute | solution.py:15
  63.8 13.2 %collective-permute-start.8 = (bf16[512,128]{1,0:T(8,128)(2,1)S(1)}, bf16[512,128]{1,0:T(8,128)(2,1)S(1)}, u32[]{:S(2)}, u32[]{:S(2)}) collective-permute-start(bf16[512,128]{1,0:T(8,128)(2,1)S(1)} %get-tuple-element.14), channel_id=1, source_target_pairs={{504,0},{508,4},{0,8},{4,12},{8,16},{12,20},{16,24},{20,28},{24,32... | collective-permute-start | bytes 393224 | tf_op jit(solution)/shard_map/ppermute | solution.py:15
  65.7 13.9 %collective-permute-start.7 = (bf16[512,128]{1,0:T(8,128)(2,1)S(1)}, bf16[512,128]{1,0:T(8,128)(2,1)S(1)}, u32[]{:S(2)}, u32[]{:S(2)}) collective-permute-start(bf16[512,128]{1,0:T(8,128)(2,1)S(1)} %get-tuple-element.15), channel_id=1, source_target_pairs={{508,0},{0,4},{4,8},{8,12},{12,16},{16,20},{20,24},{24,28},{28,32}... | collective-permute-start | bytes 393224 | tf_op jit(solution)/shard_map/ppermute | solution.py:15
  67.6 12.0 %collective-permute-start.6 = (bf16[512,128]{1,0:T(8,128)(2,1)S(1)}, bf16[512,128]{1,0:T(8,128)(2,1)S(1)}, u32[]{:S(2)}, u32[]{:S(2)}) collective-permute-start(bf16[512,128]{1,0:T(8,128)(2,1)S(1)} %get-tuple-element.16), channel_id=1, source_target_pairs={{4,0},{8,4},{12,8},{16,12},{20,16},{24,20},{28,24},{32,28},{36,32}... | collective-permute-start | bytes 393224 | tf_op jit(solution)/shard_map/ppermute | solution.py:15
  79.8 9.6 %collective-permute-start.9 = (f32[384,128]{1,0:T(8,128)S(1)}, f32[384,128]{1,0:T(8,128)S(1)}, u32[]{:S(2)}, u32[]{:S(2)}) collective-permute-start(f32[384,128]{1,0:T(8,128)S(1)} %pad_maximum_fusion.1), channel_id=1, source_target_pairs={{0,2},{1,3},{2,0},{3,1},{4,6},{5,7},{6,4},{7,5},{8,10},{9,11},{10,... | collective-permute-start | bytes 589832 | tf_op jit(solution)/shard_map/ppermute | solution.py:138
  113.8 21.4 %all-to-all-start.1 = ((f32[128,1,128]{2,1,0:T(1,128)}), f32[128,1,128]{2,1,0:T(1,128)S(1)}, u32[]{:S(2)}, u32[]{:S(2)}) async-start(f32[128,1,128]{2,1,0:T(1,128)} %broadcast_in_dim.2), calls=%async_computation.1 | async-start | bytes 131072 | tf_op jit(solution)/shard_map/all_to_all | solution.py:149

commit v4 on v3

--- a/solution.py
+++ b/solution.py
@@ -187,7 +187,7 @@
     kept = kept.reshape(section_count, half_rows, feature_width) + arrived[
         : section_count * half_rows
     ].reshape(section_count, half_rows, feature_width)
-    weight_grad = local_weight_grad + arrived[section_count * half_rows :]
+    weight_grad = team_total_sum(local_weight_grad + arrived[section_count * half_rows :])
 
     total = kept[reach_size]
     for s in range(section_count):
@@ -200,8 +200,7 @@
     sent = lax.dynamic_index_in_dim(staged, 1 - chip_bit, 0, keepdims=False)
     arrived = swap_with(jnp.concatenate([sent, weight_grad], axis=0), "rep", 2)
     gradient_share = (kept + arrived[:quarter]).astype(jnp.bfloat16)
-    weight_grad = weight_grad + arrived[quarter:]
-    grad_weight = team_total_sum(weight_grad) * (1.0 / math.sqrt(nodes_total))
+    grad_weight = (weight_grad + arrived[quarter:]) * (1.0 / math.sqrt(nodes_total))
     return (activated, grad_weight, gradient_share)
 
 

time: 137 us -> 122 us (0.89)
  blocking collectives: 23.5 us -> 0 us
  starting transfers between devices: 59.2 us -> 74 us
  waiting for transfers between devices: 37.6 us -> 34 us
  other arithmetic: 3.85 us -> 2.45 us
    all_to_all x1 -> x0, blocking collectives: 23.5 us -> none  [team_total_sum(): lax.all_to_all(block.reshape(size, rows // size, -1), 'team', 0, 0, tiled...]
    all_to_all x0 -> x1, starting transfers between devices: none -> 11 us  [team_total_sum(): lax.all_to_all(block.reshape(size, rows // size, -1), 'team', 0, 0, tiled...]
    all_to_all x1, starting transfers between devices: 6.15 us -> 10.2 us  [team_total_sum(): return lax.all_to_all(copies, 'team', 0, 0, tiled=True).reshape(block.shape)]
    ppermute x8, waiting for transfers between devices: 12.4 us -> 9.37 us  [from_behind(): return lax.ppermute(block, axis, route)]
  transfers between devices with their start and end apart: 11 -> 12, of which waited for: 7 -> 5; matrix products, arithmetic and copies ran while one was open for 2% -> 2% of each run, Pallas kernels for 0% -> 0%
where the time goes in v4:
time: 122 us; the launch traced here: 121 us
  starting transfers between devices  74 us (61%)
  waiting for transfers between devices  34 us (28%)
  local copies, waits for them, and re-layouts  5.07 us (4%)
  Pallas kernels  4.49 us (4%)
  other arithmetic  2.45 us (2%)
    ppermute x8, starting transfers between devices, from_behind(): return lax.ppermute(block, axis, route)  48.3 us
    all_to_all x1, waiting for transfers between devices, team_total_sum(): return lax.all_to_all(copies, 'team', 0, 0, tiled=True).reshape(block.shape)  15.1 us
    all_to_all x1, starting transfers between devices, team_total_sum(): lax.all_to_all(block.reshape(size, rows // size, -1), 'team', 0, 0, tiled...  11 us
    all_to_all x1, starting transfers between devices, team_total_sum(): return lax.all_to_all(copies, 'team', 0, 0, tiled=True).reshape(block.shape)  10.2 us
    ppermute x2, waiting for transfers between devices, swap_with(): return lax.ppermute(block, axis, route)  9.44 us
    ppermute x8, waiting for transfers between devices, from_behind(): return lax.ppermute(block, axis, route)  9.37 us
    ppermute x2, starting transfers between devices, swap_with(): return lax.ppermute(block, axis, route)  4.63 us
    pallas_call x1, Pallas kernels, layer_call(): pl.pallas_call(kernel, out_shape=(jax.ShapeDtypeStruct(out_grad.shape, jn...  4.49 us
  transfers between devices with their start and end apart: 12, of which 5 were waited for; matrix products, arithmetic and copies ran while one was open for 2% of the time, Pallas kernels for 0%

profile of v4, /device:TPU:4, one launch (start us, length us, event | category | flops | bytes accessed | tf_op | source)
XLA Modules:
  0.0 120.9 jit_solution(8904163178663672753)
XLA Ops:
  0.6 14.5 %collective-permute-start.2 = (bf16[1024,128]{1,0:T(8,128)(2,1)}, bf16[1024,128]{1,0:T(8,128)(2,1)S(1)}, u32[]{:S(2)}, u32[]{:S(2)}) collective-permute-start(bf16[1024,128]{1,0:T(8,128)(2,1)} %refs_2_.1), channel_id=1, source_target_pairs={{4,0},{8,4},{12,8},{16,12},{20,16},{24,20},{28,24},{32,28},{36,32}... | collective-permute-start | bytes 786440 | tf_op jit(solution)/shard_map/ppermute | solution.py:15
  15.1 1.9 %collective-permute-start.1 = (bf16[1024,128]{1,0:T(8,128)(2,1)}, bf16[1024,128]{1,0:T(8,128)(2,1)S(1)}, u32[]{:S(2)}, u32[]{:S(2)}) collective-permute-start(bf16[1024,128]{1,0:T(8,128)(2,1)} %refs_2_.1), channel_id=1, source_target_pairs={{508,0},{0,4},{4,8},{8,12},{12,16},{16,20},{20,24},{24,28},{28,32}... | collective-permute-start | bytes 786440 | tf_op jit(solution)/shard_map/ppermute | solution.py:15
  17.1 1.9 %collective-permute-start = (bf16[1024,128]{1,0:T(8,128)(2,1)}, bf16[1024,128]{1,0:T(8,128)(2,1)S(1)}, u32[]{:S(2)}, u32[]{:S(2)}) collective-permute-start(bf16[1024,128]{1,0:T(8,128)(2,1)} %refs_2_.1), channel_id=1, source_target_pairs={{504,0},{508,4},{0,8},{4,12},{8,16},{12,20},{16,24},{20,28},{24,32... | collective-permute-start | bytes 786440 | tf_op jit(solution)/shard_map/ppermute | solution.py:15
  19.0 9.0 %collective-permute-start.3 = (bf16[1024,128]{1,0:T(8,128)(2,1)}, bf16[1024,128]{1,0:T(8,128)(2,1)S(1)}, u32[]{:S(2)}, u32[]{:S(2)}) collective-permute-start(bf16[1024,128]{1,0:T(8,128)(2,1)} %refs_2_.1), channel_id=1, source_target_pairs={{8,0},{12,4},{16,8},{20,12},{24,16},{28,20},{32,24},{36,28},{40,32... | collective-permute-start | bytes 786440 | tf_op jit(solution)/shard_map/ppermute | solution.py:15
  28.1 0.8 reshape.45.counts_ref
  28.8 0.7 copy.11
  29.6 6.7 %collective-permute-done.1.refs_1_ = bf16[1024,128]{1,0:T(8,128)(2,1)S(1)} collective-permute-done((bf16[1024,128]{1,0:T(8,128)(2,1)}, bf16[1024,128]{1,0:T(8,128)(2,1)S(1)}, u32[]{:S(2)}, u32[]{:S(2)}) %collective-permute-start.1) | collective-permute-done | bytes 262176 | tf_op jit(solution)/shard_map/ppermute | solution.py:15
  36.2 2.7 %collective-permute-done.3.refs_4_ = bf16[1024,128]{1,0:T(8,128)(2,1)S(1)} collective-permute-done((bf16[1024,128]{1,0:T(8,128)(2,1)}, bf16[1024,128]{1,0:T(8,128)(2,1)S(1)}, u32[]{:S(2)}, u32[]{:S(2)}) %collective-permute-start.3) | collective-permute-done | bytes 262176 | tf_op jit(solution)/shard_map/ppermute | solution.py:15
  39.0 0.9 copy-done
  39.9 0.8 copy-done.1
  40.7 0.8 copy-done.2
  41.5 4.5 %shard_map.85 = (bf16[256,128]{1,0:T(8,128)(2,1)}, f32[128,128]{1,0:T(8,128)S(1)}, f32[5,1024,128]{2,1,0:T(8,128)S(1)}) custom-call(s32[80]{0:T(128)S(1)} %reshape.44.coords_ref, s32[10]{0:T(128)S(1)} %reshape.45.counts_ref, bf16[1024,128]{1,0:T(8,128)(2,1)S(1)} %collective-permute-done.refs_0_, bf16[1024,128]{1,0:T(8,128)(2,1)S(1)} %collective-permute-done.1.refs_1_, ...), custom_call_target="tpu_custom_call" | custom-call | flops 704643072 | bytes 6553600 | tf_op jit(solution)/shard_map/pallas_call | solution.py:117
  46.3 1.9 %collective-permute-start.4 = (f32[2688,128]{1,0:T(8,128)S(1)}, f32[2688,128]{1,0:T(8,128)S(1)}, u32[]{:S(2)}, u32[]{:S(2)}) collective-permute-start(f32[2688,128]{1,0:T(8,128)S(1)} %pad_maximum_fusion), channel_id=1, source_target_pairs={{0,1},{1,0},{2,3},{3,2},{4,5},{5,4},{6,7},{7,6},{8,9},{9,8},{10,11... | collective-permute-start | bytes 4128776 | tf_op jit(solution)/shard_map/ppermute | solution.py:138
  48.2 3.1 %collective-permute-done.4 = f32[2688,128]{1,0:T(8,128)S(1)} collective-permute-done((f32[2688,128]{1,0:T(8,128)S(1)}, f32[2688,128]{1,0:T(8,128)S(1)}, u32[]{:S(2)}, u32[]{:S(2)}) %collective-permute-start.4) | collective-permute-done | bytes 1376288 | tf_op jit(solution)/shard_map/ppermute | solution.py:138
  51.9 11.0 %all-to-all-start = ((f32[128,1,128]{2,1,0:T(1,128)}), f32[128,1,128]{2,1,0:T(1,128)S(1)}, u32[]{:S(2)}, u32[]{:S(2)}) async-start(f32[128,1,128]{2,1,0:T(1,128)} %bitcast.3), calls=%async_computation | async-start | bytes 131072 | tf_op jit(solution)/shard_map/all_to_all | solution.py:146
  63.3 8.9 %collective-permute-start.5 = (bf16[512,128]{1,0:T(8,128)(2,1)S(1)}, bf16[512,128]{1,0:T(8,128)(2,1)S(1)}, u32[]{:S(2)}, u32[]{:S(2)}) collective-permute-start(bf16[512,128]{1,0:T(8,128)(2,1)S(1)} %get-tuple-element.13), channel_id=1, source_target_pairs={{8,0},{12,4},{16,8},{20,12},{24,16},{28,20},{32,24},{36,28},{40,32... | collective-permute-start | bytes 393224 | tf_op jit(solution)/shard_map/ppermute | solution.py:15
  72.2 1.9 %collective-permute-start.8 = (bf16[512,128]{1,0:T(8,128)(2,1)S(1)}, bf16[512,128]{1,0:T(8,128)(2,1)S(1)}, u32[]{:S(2)}, u32[]{:S(2)}) collective-permute-start(bf16[512,128]{1,0:T(8,128)(2,1)S(1)} %get-tuple-element.14), channel_id=1, source_target_pairs={{504,0},{508,4},{0,8},{4,12},{8,16},{12,20},{16,24},{20,28},{24,32... | collective-permute-start | bytes 393224 | tf_op jit(solution)/shard_map/ppermute | solution.py:15
  74.1 2.5 %collective-permute-start.7 = (bf16[512,128]{1,0:T(8,128)(2,1)S(1)}, bf16[512,128]{1,0:T(8,128)(2,1)S(1)}, u32[]{:S(2)}, u32[]{:S(2)}) collective-permute-start(bf16[512,128]{1,0:T(8,128)(2,1)S(1)} %get-tuple-element.15), channel_id=1, source_target_pairs={{508,0},{0,4},{4,8},{8,12},{12,16},{16,20},{20,24},{24,28},{28,32}... | collective-permute-start | bytes 393224 | tf_op jit(solution)/shard_map/ppermute | solution.py:15
  76.6 7.6 %collective-permute-start.6 = (bf16[512,128]{1,0:T(8,128)(2,1)S(1)}, bf16[512,128]{1,0:T(8,128)(2,1)S(1)}, u32[]{:S(2)}, u32[]{:S(2)}) collective-permute-start(bf16[512,128]{1,0:T(8,128)(2,1)S(1)} %get-tuple-element.16), channel_id=1, source_target_pairs={{4,0},{8,4},{12,8},{16,12},{20,16},{24,20},{28,24},{32,28},{36,32}... | collective-permute-start | bytes 393224 | tf_op jit(solution)/shard_map/ppermute | solution.py:15
  84.4 0.7 broadcast_in_dim.2
  85.1 10.2 %all-to-all-start.1 = ((f32[128,1,128]{2,1,0:T(1,128)}), f32[128,1,128]{2,1,0:T(1,128)S(1)}, u32[]{:S(2)}, u32[]{:S(2)}) async-start(f32[128,1,128]{2,1,0:T(1,128)} %broadcast_in_dim.2), calls=%async_computation.1 | async-start | bytes 131072 | tf_op jit(solution)/shard_map/all_to_all | solution.py:149
  95.4 15.1 %all-to-all-done.1 = f32[128,1,128]{2,1,0:T(1,128)S(1)} async-done(((f32[128,1,128]{2,1,0:T(1,128)}), f32[128,1,128]{2,1,0:T(1,128)S(1)}, u32[]{:S(2)}, u32[]{:S(2)}) %all-to-all-start.1) | async-done | bytes 65568 | tf_op jit(solution)/shard_map/all_to_all | solution.py:149
  110.5 2.7 %collective-permute-start.9 = (f32[384,128]{1,0:T(8,128)S(1)}, f32[384,128]{1,0:T(8,128)S(1)}, u32[]{:S(2)}, u32[]{:S(2)}) collective-permute-start(f32[384,128]{1,0:T(8,128)S(1)} %pad_maximum_fusion.1), channel_id=1, source_target_pairs={{0,2},{1,3},{2,0},{3,1},{4,6},{5,7},{6,4},{7,5},{8,10},{9,11},{10,... | collective-permute-start | bytes 589832 | tf_op jit(solution)/shard_map/ppermute | solution.py:138
  113.2 6.3 %collective-permute-done.9 = f32[384,128]{1,0:T(8,128)S(1)} collective-permute-done((f32[384,128]{1,0:T(8,128)S(1)}, f32[384,128]{1,0:T(8,128)S(1)}, u32[]{:S(2)}, u32[]{:S(2)}) %collective-permute-start.9) | collective-permute-done | bytes 196640 | tf_op jit(solution)/shard_map/ppermute | solution.py:138
  (23 shorter events, 2.9 us)
Async XLA Ops:
  0.6 29.0 %collective-permute-start.2 = (bf16[1024,128]{1,0:T(8,128)(2,1)}, bf16[1024,128]{1,0:T(8,128)(2,1)S(1)}, u32[]{:S(2)}, u32[]{:S(2)}) collective-permute-start(bf16[1024,128]{1,0:T(8,128)(2,1)} %refs_2_.1), channel_id=1, source_target_pairs={{4,0},{8,4},{12,8},{16,12},{20,16},{24,20},{28,24},{32,28},{36,32}... | collective-permute-start | bytes 786440 | tf_op jit(solution)/shard_map/ppermute | solution.py:15
  15.1 21.1 %collective-permute-start.1 = (bf16[1024,128]{1,0:T(8,128)(2,1)}, bf16[1024,128]{1,0:T(8,128)(2,1)S(1)}, u32[]{:S(2)}, u32[]{:S(2)}) collective-permute-start(bf16[1024,128]{1,0:T(8,128)(2,1)} %refs_2_.1), channel_id=1, source_target_pairs={{508,0},{0,4},{4,8},{8,12},{12,16},{16,20},{20,24},{24,28},{28,32}... | collective-permute-start | bytes 786440 | tf_op jit(solution)/shard_map/ppermute | solution.py:15
  17.1 19.2 %collective-permute-start = (bf16[1024,128]{1,0:T(8,128)(2,1)}, bf16[1024,128]{1,0:T(8,128)(2,1)S(1)}, u32[]{:S(2)}, u32[]{:S(2)}) collective-permute-start(bf16[1024,128]{1,0:T(8,128)(2,1)} %refs_2_.1), channel_id=1, source_target_pairs={{504,0},{508,4},{0,8},{4,12},{8,16},{12,20},{16,24},{20,28},{24,32... | collective-permute-start | bytes 786440 | tf_op jit(solution)/shard_map/ppermute | solution.py:15
  19.0 20.0 %collective-permute-start.3 = (bf16[1024,128]{1,0:T(8,128)(2,1)}, bf16[1024,128]{1,0:T(8,128)(2,1)S(1)}, u32[]{:S(2)}, u32[]{:S(2)}) collective-permute-start(bf16[1024,128]{1,0:T(8,128)(2,1)} %refs_2_.1), channel_id=1, source_target_pairs={{8,0},{12,4},{16,8},{20,12},{24,16},{28,20},{32,24},{36,28},{40,32... | collective-permute-start | bytes 786440 | tf_op jit(solution)/shard_map/ppermute | solution.py:15
  39.0 0.9 copy-start
  39.9 0.8 copy-start.1
  40.7 0.8 copy-start.2
  46.3 5.0 %collective-permute-start.4 = (f32[2688,128]{1,0:T(8,128)S(1)}, f32[2688,128]{1,0:T(8,128)S(1)}, u32[]{:S(2)}, u32[]{:S(2)}) collective-permute-start(f32[2688,128]{1,0:T(8,128)S(1)} %pad_maximum_fusion), channel_id=1, source_target_pairs={{0,1},{1,0},{2,3},{3,2},{4,5},{5,4},{6,7},{7,6},{8,9},{9,8},{10,11... | collective-permute-start | bytes 4128776 | tf_op jit(solution)/shard_map/ppermute | solution.py:138
  51.9 32.3 %all-to-all-start = ((f32[128,1,128]{2,1,0:T(1,128)}), f32[128,1,128]{2,1,0:T(1,128)S(1)}, u32[]{:S(2)}, u32[]{:S(2)}) async-start(f32[128,1,128]{2,1,0:T(1,128)} %bitcast.3), calls=%async_computation | async-start | bytes 131072 | tf_op jit(solution)/shard_map/all_to_all | solution.py:146
  63.3 31.9 %collective-permute-start.5 = (bf16[512,128]{1,0:T(8,128)(2,1)S(1)}, bf16[512,128]{1,0:T(8,128)(2,1)S(1)}, u32[]{:S(2)}, u32[]{:S(2)}) collective-permute-start(bf16[512,128]{1,0:T(8,128)(2,1)S(1)} %get-tuple-element.13), channel_id=1, source_target_pairs={{8,0},{12,4},{16,8},{20,12},{24,16},{28,20},{32,24},{36,28},{40,32... | collective-permute-start | bytes 393224 | tf_op jit(solution)/shard_map/ppermute | solution.py:15
  72.2 23.0 %collective-permute-start.8 = (bf16[512,128]{1,0:T(8,128)(2,1)S(1)}, bf16[512,128]{1,0:T(8,128)(2,1)S(1)}, u32[]{:S(2)}, u32[]{:S(2)}) collective-permute-start(bf16[512,128]{1,0:T(8,128)(2,1)S(1)} %get-tuple-element.14), channel_id=1, source_target_pairs={{504,0},{508,4},{0,8},{4,12},{8,16},{12,20},{16,24},{20,28},{24,32... | collective-permute-start | bytes 393224 | tf_op jit(solution)/shard_map/ppermute | solution.py:15
  74.1 21.1 %collective-permute-start.7 = (bf16[512,128]{1,0:T(8,128)(2,1)S(1)}, bf16[512,128]{1,0:T(8,128)(2,1)S(1)}, u32[]{:S(2)}, u32[]{:S(2)}) collective-permute-start(bf16[512,128]{1,0:T(8,128)(2,1)S(1)} %get-tuple-element.15), channel_id=1, source_target_pairs={{508,0},{0,4},{4,8},{8,12},{12,16},{16,20},{20,24},{24,28},{28,32}... | collective-permute-start | bytes 393224 | tf_op jit(solution)/shard_map/ppermute | solution.py:15
  76.6 18.6 %collective-permute-start.6 = (bf16[512,128]{1,0:T(8,128)(2,1)S(1)}, bf16[512,128]{1,0:T(8,128)(2,1)S(1)}, u32[]{:S(2)}, u32[]{:S(2)}) collective-permute-start(bf16[512,128]{1,0:T(8,128)(2,1)S(1)} %get-tuple-element.16), channel_id=1, source_target_pairs={{4,0},{8,4},{12,8},{16,12},{20,16},{24,20},{28,24},{32,28},{36,32}... | collective-permute-start | bytes 393224 | tf_op jit(solution)/shard_map/ppermute | solution.py:15
  85.1 25.4 %all-to-all-start.1 = ((f32[128,1,128]{2,1,0:T(1,128)}), f32[128,1,128]{2,1,0:T(1,128)S(1)}, u32[]{:S(2)}, u32[]{:S(2)}) async-start(f32[128,1,128]{2,1,0:T(1,128)} %broadcast_in_dim.2), calls=%async_computation.1 | async-start | bytes 131072 | tf_op jit(solution)/shard_map/all_to_all | solution.py:149
  110.5 9.1 %collective-permute-start.9 = (f32[384,128]{1,0:T(8,128)S(1)}, f32[384,128]{1,0:T(8,128)S(1)}, u32[]{:S(2)}, u32[]{:S(2)}) collective-permute-start(f32[384,128]{1,0:T(8,128)S(1)} %pad_maximum_fusion.1), channel_id=1, source_target_pairs={{0,2},{1,3},{2,0},{3,1},{4,6},{5,7},{6,4},{7,5},{8,10},{9,11},{10,... | collective-permute-start | bytes 589832 | tf_op jit(solution)/shard_map/ppermute | solution.py:138

commit v5 on v4

--- a/solution.py
+++ b/solution.py
@@ -41,7 +41,7 @@
     return blocks
 
 
-def layer_kernel(coords_ref, counts_ref, *refs, section_count, slot_count, panel_dev, tile_size):
+def layer_kernel(coords_ref, counts_ref, order_ref, *refs, section_count, slot_count, panel_dev, tile_size):
     feature_refs = refs[:section_count]
     tiles_ref, out_grad_ref, weight_ref, act_ref, wgrad_ref, sums_ref = refs[section_count:]
     weight = weight_ref[...]
@@ -58,11 +58,12 @@
     gate_rows = []
     for g in range(panel_dev):
         total = jnp.zeros((tile_size, weight.shape[1]), jnp.float32)
-        for s in range(section_count):
+        for j in range(section_count):
+            s = order_ref[j]
             for k in range(slot_count):
                 column, live = slot_entry(g, s, k)
                 start = pl.multiple_of(column * tile_size, tile_size)
-                picked = feature_refs[s][pl.ds(start, tile_size), :]
+                picked = feature_refs[j][pl.ds(start, tile_size), :]
                 product = jnp.dot(tiles_ref[g, s, k], picked, preferred_element_type=jnp.float32)
                 total = total + jnp.where(live, product, 0.0)
         aggregated = total.astype(jnp.bfloat16)
@@ -86,7 +87,8 @@
         back = lax.dot_general(
             gate_rows[g], weight, (((1,), (1,)), ((), ())), preferred_element_type=jnp.float32
         ).astype(jnp.bfloat16)
-        for s in range(section_count):
+        for j in range(section_count):
+            s = order_ref[j]
             for k in range(slot_count):
                 column, live = slot_entry(g, s, k)
                 start = pl.multiple_of(column * tile_size, tile_size)
@@ -101,7 +103,7 @@
                     sums_ref[s, pl.ds(start, tile_size), :] += contrib
 
 
-def layer_call(source_blocks, tiles, out_grad, weight, coords, counts):
+def layer_call(source_blocks, order, tiles, out_grad, weight, coords, counts):
     panel_dev, section_count, slot_count, tile_size, _ = tiles.shape
     team_rows, feature_width = source_blocks[0].shape
     kernel = functools.partial(
@@ -121,7 +123,7 @@
             jax.ShapeDtypeStruct((feature_width, feature_width), jnp.float32),
             jax.ShapeDtypeStruct((section_count, team_rows, feature_width), jnp.float32),
         ),
-        in_specs=[smem, smem] + [vmem] * (section_count + 3),
+        in_specs=[smem, smem, smem] + [vmem] * (section_count + 3),
         out_specs=(vmem, vmem, vmem),
         compiler_params=pltpu.CompilerParams(vmem_limit_bytes=48 * 1024 * 1024),
         cost_estimate=pl.CostEstimate(
@@ -129,7 +131,7 @@
             transcendentals=panel_dev * tile_size * feature_width,
             bytes_accessed=tiles.size * 2 + section_count * team_rows * feature_width * 6,
         ),
-    )(coords.reshape(-1), counts.reshape(-1), *source_blocks, tiles, out_grad, weight)
+    )(coords.reshape(-1), counts.reshape(-1), order, *source_blocks, tiles, out_grad, weight)
 
 
 def swap_with(block, axis, mask):
@@ -149,18 +151,45 @@
     return lax.all_to_all(copies, "team", 0, 0, tiled=True).reshape(block.shape)
 
 
+def gather_sources(features, reach_size, rep_size):
+    team_size = lax.axis_size("team")
+    if rep_size % 2:
+        blocks = [features] + [
+            from_behind(features, "team", -shift)
+            for shift in range(-reach_size, reach_size + 1)
+            if shift
+        ]
+        shifts = [0] + [shift for shift in range(-reach_size, reach_size + 1) if shift]
+        order = jnp.array([reach_size + shift for shift in shifts], jnp.int32)
+        return blocks, order
+    sign = 1 - 2 * (lax.axis_index("rep") % 2)
+    fetched = []
+    for distance in range(1, reach_size + 1):
+        route = []
+        for team in range(team_size):
+            for rep in range(rep_size):
+                step = distance if rep % 2 == 0 else -distance
+                source = ((team + step) % team_size) * rep_size + rep
+                route.append((source, team * rep_size + rep))
+        fetched.append(lax.ppermute(features, ("team", "rep"), route))
+    swapped = swap_with(jnp.stack(fetched), "rep", 1)
+    blocks = [features] + fetched + [swapped[i] for i in range(reach_size)]
+    distances = jnp.arange(1, reach_size + 1, dtype=jnp.int32)
+    order = jnp.concatenate(
+        [jnp.array([reach_size], jnp.int32), reach_size + sign * distances, reach_size - sign * distances]
+    ).astype(jnp.int32)
+    return blocks, order
+
+
 def body(features, weight, out_grad, tiles, coords, counts):
     panel_dev, section_count, slot_count, tile_size, _ = tiles.shape
     team_rows, feature_width = features.shape
     reach_size = (section_count - 1) // 2
     nodes_total = team_rows * lax.axis_size("team")
     rep_size = lax.axis_size("rep")
-    source_blocks = [
-        features if s == reach_size else from_behind(features, "team", reach_size - s)
-        for s in range(section_count)
-    ]
+    source_blocks, order = gather_sources(features, reach_size, rep_size)
     activated, local_weight_grad, sums = layer_call(
-        source_blocks, tiles, out_grad, weight, coords, counts
+        source_blocks, order, tiles, out_grad, weight, coords, counts
     )
     if rep_size != 4:
         grad_weight = butterfly_sum(local_weight_grad, ("rep", "team"))

time: 122 us -> 109 us (0.89)
  starting transfers between devices: 74 us -> 67.4 us
  waiting for transfers between devices: 34 us -> 30.7 us
  local copies, waits for them, and re-layouts: 5.07 us -> 2.58 us
    ppermute x8 -> x4, starting transfers between devices: 48.3 us -> 20.9 us  [from_behind(): return lax.ppermute(block, axis, route)]
    ppermute x0 -> x2, starting transfers between devices: none -> 18 us  [gather_sources(): fetched.append(lax.ppermute(features, ('team', 'rep'), route))]
    ppermute x8 -> x4, waiting for transfers between devices: 9.37 us -> 0.01 us  [from_behind(): return lax.ppermute(block, axis, route)]
    ppermute x0 -> x2, waiting for transfers between devices: none -> 6.11 us  [gather_sources(): fetched.append(lax.ppermute(features, ('team', 'rep'), route))]
    unnamed x7, local copies, waits for them, and re-layouts: 3.24 us -> 0.7 us
    ppermute x2 -> x3, starting transfers between devices: 4.63 us -> 6.79 us  [swap_with(): return lax.ppermute(block, axis, route)]
    ppermute x2 -> x3, waiting for transfers between devices: 9.44 us -> 9.43 us  [swap_with(): return lax.ppermute(block, axis, route)]
  transfers between devices with their start and end apart: 12 -> 11, of which waited for: 5 -> 6; matrix products, arithmetic and copies ran while one was open for 2% -> 3% of each run, Pallas kernels for 0% -> 0%
where the time goes in v5:
time: 109 us
  starting transfers between devices  67.4 us (62%)
  waiting for transfers between devices  30.7 us (28%)
  Pallas kernels  4.5 us (4%)
  local copies, waits for them, and re-layouts  2.58 us (2%)
  other arithmetic  2.58 us (2%)
    ppermute x4, starting transfers between devices, from_behind(): return lax.ppermute(block, axis, route)  20.9 us
    ppermute x2, starting transfers between devices, gather_sources(): fetched.append(lax.ppermute(features, ('team', 'rep'), route))  18 us
    all_to_all x1, waiting for transfers between devices, team_total_sum(): return lax.all_to_all(copies, 'team', 0, 0, tiled=True).reshape(block.shape)  15.1 us
    all_to_all x1, starting transfers between devices, team_total_sum(): lax.all_to_all(block.reshape(size, rows // size, -1), 'team', 0, 0, tiled...  11.6 us
    all_to_all x1, starting transfers between devices, team_total_sum(): return lax.all_to_all(copies, 'team', 0, 0, tiled=True).reshape(block.shape)  10.2 us
    ppermute x3, waiting for transfers between devices, swap_with(): return lax.ppermute(block, axis, route)  9.43 us
    ppermute x3, starting transfers between devices, swap_with(): return lax.ppermute(block, axis, route)  6.79 us
    ppermute x2, waiting for transfers between devices, gather_sources(): fetched.append(lax.ppermute(features, ('team', 'rep'), route))  6.11 us
  transfers between devices with their start and end apart: 11, of which 6 were waited for; matrix products, arithmetic and copies ran while one was open for 3% of the time, Pallas kernels for 0%

profile of v5, /device:TPU:4, one launch (start us, length us, event | category | flops | bytes accessed | tf_op | source)
XLA Modules:
  0.0 108.7 jit_solution(10153922219585978590)
XLA Ops:
  0.7 14.6 %collective-permute-start = (bf16[1024,128]{1,0:T(8,128)(2,1)}, bf16[1024,128]{1,0:T(8,128)(2,1)S(1)}, u32[]{:S(2)}, u32[]{:S(2)}) collective-permute-start(bf16[1024,128]{1,0:T(8,128)(2,1)} %refs_0_.1), channel_id=1, source_target_pairs={{4,0},{509,1},{6,2},{511,3},{8,4},{1,5},{10,6},{3,7},{12,8},{5,9},... | collective-permute-start | bytes 786440 | tf_op jit(solution)/shard_map/ppermute | solution.py:174
  15.3 3.4 %collective-permute-start.1 = (bf16[1024,128]{1,0:T(8,128)(2,1)}, bf16[1024,128]{1,0:T(8,128)(2,1)S(1)}, u32[]{:S(2)}, u32[]{:S(2)}) collective-permute-start(bf16[1024,128]{1,0:T(8,128)(2,1)} %refs_0_.1), channel_id=1, source_target_pairs={{8,0},{505,1},{10,2},{507,3},{12,4},{509,5},{14,6},{511,7},{16,8},... | collective-permute-start | bytes 786440 | tf_op jit(solution)/shard_map/ppermute | solution.py:174
  18.7 0.8 collective-permute-done.refs_1_
  19.5 5.3 %collective-permute-done.1.refs_2_ = bf16[1024,128]{1,0:T(8,128)(2,1)S(1)} collective-permute-done((bf16[1024,128]{1,0:T(8,128)(2,1)}, bf16[1024,128]{1,0:T(8,128)(2,1)S(1)}, u32[]{:S(2)}, u32[]{:S(2)}) %collective-permute-start.1) | collective-permute-done | bytes 262176 | tf_op jit(solution)/shard_map/ppermute | solution.py:174
  24.8 1.9 %collective-permute-start.2 = (bf16[2,1024,128]{2,1,0:T(8,128)(2,1)S(1)}, bf16[2,1024,128]{2,1,0:T(8,128)(2,1)S(1)}, u32[]{:S(2)}, u32[]{:S(2)}) collective-permute-start(bf16[2,1024,128]{2,1,0:T(8,128)(2,1)S(1)} %pad_maximum_fusion.1), channel_id=1, source_target_pairs={{0,1},{1,0},{2,3},{3,2},{4,5},{5,4},{6,7},{7,6},{8,9},{9,8},{10,11... | collective-permute-start | bytes 1572872 | tf_op jit(solution)/shard_map/ppermute | solution.py:140
  26.8 0.8 reshape.45.counts_ref
  27.5 0.7 copy.12
  28.4 0.2 collective-permute-done.2
  28.7 4.5 %shard_map.94 = (bf16[256,128]{1,0:T(8,128)(2,1)}, f32[128,128]{1,0:T(8,128)S(1)}, f32[5,1024,128]{2,1,0:T(8,128)S(1)}) custom-call(s32[80]{0:T(128)S(1)} %reshape.44.coords_ref, s32[10]{0:T(128)S(1)} %reshape.45.counts_ref, s32[5]{0:T(128)S(1)} %pad_add_fusion.order_ref, bf16[1024,128]{1,0:T(8,128)(2,1)S(1)} %copy-done, ...), custom_call_target="tpu_custom_call" | custom-call | flops 704643072 | bytes 6553600 | tf_op jit(solution)/shard_map/pallas_call | solution.py:119
  33.5 2.2 %collective-permute-start.3 = (f32[2688,128]{1,0:T(8,128)S(1)}, f32[2688,128]{1,0:T(8,128)S(1)}, u32[]{:S(2)}, u32[]{:S(2)}) collective-permute-start(f32[2688,128]{1,0:T(8,128)S(1)} %pad_maximum_fusion), channel_id=1, source_target_pairs={{0,1},{1,0},{2,3},{3,2},{4,5},{5,4},{6,7},{7,6},{8,9},{9,8},{10,11... | collective-permute-start | bytes 4128776 | tf_op jit(solution)/shard_map/ppermute | solution.py:140
  35.7 2.8 %collective-permute-done.3 = f32[2688,128]{1,0:T(8,128)S(1)} collective-permute-done((f32[2688,128]{1,0:T(8,128)S(1)}, f32[2688,128]{1,0:T(8,128)S(1)}, u32[]{:S(2)}, u32[]{:S(2)}) %collective-permute-start.3) | collective-permute-done | bytes 1376288 | tf_op jit(solution)/shard_map/ppermute | solution.py:140
  38.5 0.6 slice_add_fusion.2
  39.1 11.6 %all-to-all-start = ((f32[128,1,128]{2,1,0:T(1,128)}), f32[128,1,128]{2,1,0:T(1,128)S(1)}, u32[]{:S(2)}, u32[]{:S(2)}) async-start(f32[128,1,128]{2,1,0:T(1,128)} %bitcast.7), calls=%async_computation | async-start | bytes 131072 | tf_op jit(solution)/shard_map/all_to_all | solution.py:148
  51.1 8.9 %collective-permute-start.4 = (bf16[512,128]{1,0:T(8,128)(2,1)S(1)}, bf16[512,128]{1,0:T(8,128)(2,1)S(1)}, u32[]{:S(2)}, u32[]{:S(2)}) collective-permute-start(bf16[512,128]{1,0:T(8,128)(2,1)S(1)} %get-tuple-element.13), channel_id=1, source_target_pairs={{8,0},{12,4},{16,8},{20,12},{24,16},{28,20},{32,24},{36,28},{40,32... | collective-permute-start | bytes 393224 | tf_op jit(solution)/shard_map/ppermute | solution.py:15
  60.0 1.9 %collective-permute-start.7 = (bf16[512,128]{1,0:T(8,128)(2,1)S(1)}, bf16[512,128]{1,0:T(8,128)(2,1)S(1)}, u32[]{:S(2)}, u32[]{:S(2)}) collective-permute-start(bf16[512,128]{1,0:T(8,128)(2,1)S(1)} %get-tuple-element.14), channel_id=1, source_target_pairs={{504,0},{508,4},{0,8},{4,12},{8,16},{12,20},{16,24},{20,28},{24,32... | collective-permute-start | bytes 393224 | tf_op jit(solution)/shard_map/ppermute | solution.py:15
  61.9 2.5 %collective-permute-start.6 = (bf16[512,128]{1,0:T(8,128)(2,1)S(1)}, bf16[512,128]{1,0:T(8,128)(2,1)S(1)}, u32[]{:S(2)}, u32[]{:S(2)}) collective-permute-start(bf16[512,128]{1,0:T(8,128)(2,1)S(1)} %get-tuple-element.15), channel_id=1, source_target_pairs={{508,0},{0,4},{4,8},{8,12},{12,16},{16,20},{20,24},{24,28},{28,32}... | collective-permute-start | bytes 393224 | tf_op jit(solution)/shard_map/ppermute | solution.py:15
  64.4 7.6 %collective-permute-start.5 = (bf16[512,128]{1,0:T(8,128)(2,1)S(1)}, bf16[512,128]{1,0:T(8,128)(2,1)S(1)}, u32[]{:S(2)}, u32[]{:S(2)}) collective-permute-start(bf16[512,128]{1,0:T(8,128)(2,1)S(1)} %get-tuple-element.16), channel_id=1, source_target_pairs={{4,0},{8,4},{12,8},{16,12},{20,16},{24,20},{28,24},{32,28},{36,32}... | collective-permute-start | bytes 393224 | tf_op jit(solution)/shard_map/ppermute | solution.py:15
  72.2 0.7 broadcast_in_dim.2
  72.9 10.2 %all-to-all-start.1 = ((f32[128,1,128]{2,1,0:T(1,128)}), f32[128,1,128]{2,1,0:T(1,128)S(1)}, u32[]{:S(2)}, u32[]{:S(2)}) async-start(f32[128,1,128]{2,1,0:T(1,128)} %broadcast_in_dim.2), calls=%async_computation.1 | async-start | bytes 131072 | tf_op jit(solution)/shard_map/all_to_all | solution.py:151
  83.2 15.1 %all-to-all-done.1 = f32[128,1,128]{2,1,0:T(1,128)S(1)} async-done(((f32[128,1,128]{2,1,0:T(1,128)}), f32[128,1,128]{2,1,0:T(1,128)S(1)}, u32[]{:S(2)}, u32[]{:S(2)}) %all-to-all-start.1) | async-done | bytes 65568 | tf_op jit(solution)/shard_map/all_to_all | solution.py:151
  98.3 2.7 %collective-permute-start.8 = (f32[384,128]{1,0:T(8,128)S(1)}, f32[384,128]{1,0:T(8,128)S(1)}, u32[]{:S(2)}, u32[]{:S(2)}) collective-permute-start(f32[384,128]{1,0:T(8,128)S(1)} %pad_maximum_fusion.2), channel_id=1, source_target_pairs={{0,2},{1,3},{2,0},{3,1},{4,6},{5,7},{6,4},{7,5},{8,10},{9,11},{10,... | collective-permute-start | bytes 589832 | tf_op jit(solution)/shard_map/ppermute | solution.py:140
  101.1 6.4 %collective-permute-done.8 = f32[384,128]{1,0:T(8,128)S(1)} collective-permute-done((f32[384,128]{1,0:T(8,128)S(1)}, f32[384,128]{1,0:T(8,128)S(1)}, u32[]{:S(2)}, u32[]{:S(2)}) %collective-permute-start.8) | collective-permute-done | bytes 196640 | tf_op jit(solution)/shard_map/ppermute | solution.py:140
  107.4 0.6 fusion.5
  108.1 0.6 fusion.4
  (25 shorter events, 1.1 us)
Async XLA Ops:
  0.6 28.0 %copy-start = (bf16[1024,128]{1,0:T(8,128)(2,1)S(1)}, bf16[1024,128]{1,0:T(8,128)(2,1)}, u32[]{:S(2)}) copy-start(bf16[1024,128]{1,0:T(8,128)(2,1)} %refs_0_.1) | copy-start | bytes 786436
  0.6 28.0 %copy-start.1 = (bf16[256,128]{1,0:T(8,128)(2,1)S(1)}, bf16[256,128]{1,0:T(8,128)(2,1)}, u32[]{:S(2)}) copy-start(bf16[256,128]{1,0:T(8,128)(2,1)} %refs_6_.1) | copy-start | bytes 196612
  0.7 28.0 %copy-start.2 = (bf16[128,128]{1,0:T(8,128)(2,1)S(1)}, bf16[128,128]{1,0:T(8,128)(2,1)}, u32[]{:S(2)}) copy-start(bf16[128,128]{1,0:T(8,128)(2,1)} %refs_7_.1) | copy-start | bytes 98308
  0.7 18.8 %collective-permute-start = (bf16[1024,128]{1,0:T(8,128)(2,1)}, bf16[1024,128]{1,0:T(8,128)(2,1)S(1)}, u32[]{:S(2)}, u32[]{:S(2)}) collective-permute-start(bf16[1024,128]{1,0:T(8,128)(2,1)} %refs_0_.1), channel_id=1, source_target_pairs={{4,0},{509,1},{6,2},{511,3},{8,4},{1,5},{10,6},{3,7},{12,8},{5,9},... | collective-permute-start | bytes 786440 | tf_op jit(solution)/shard_map/ppermute | solution.py:174
  15.3 9.5 %collective-permute-start.1 = (bf16[1024,128]{1,0:T(8,128)(2,1)}, bf16[1024,128]{1,0:T(8,128)(2,1)S(1)}, u32[]{:S(2)}, u32[]{:S(2)}) collective-permute-start(bf16[1024,128]{1,0:T(8,128)(2,1)} %refs_0_.1), channel_id=1, source_target_pairs={{8,0},{505,1},{10,2},{507,3},{12,4},{509,5},{14,6},{511,7},{16,8},... | collective-permute-start | bytes 786440 | tf_op jit(solution)/shard_map/ppermute | solution.py:174
  24.8 3.8 %collective-permute-start.2 = (bf16[2,1024,128]{2,1,0:T(8,128)(2,1)S(1)}, bf16[2,1024,128]{2,1,0:T(8,128)(2,1)S(1)}, u32[]{:S(2)}, u32[]{:S(2)}) collective-permute-start(bf16[2,1024,128]{2,1,0:T(8,128)(2,1)S(1)} %pad_maximum_fusion.1), channel_id=1, source_target_pairs={{0,1},{1,0},{2,3},{3,2},{4,5},{5,4},{6,7},{7,6},{8,9},{9,8},{10,11... | collective-permute-start | bytes 1572872 | tf_op jit(solution)/shard_map/ppermute | solution.py:140
  33.5 5.0 %collective-permute-start.3 = (f32[2688,128]{1,0:T(8,128)S(1)}, f32[2688,128]{1,0:T(8,128)S(1)}, u32[]{:S(2)}, u32[]{:S(2)}) collective-permute-start(f32[2688,128]{1,0:T(8,128)S(1)} %pad_maximum_fusion), channel_id=1, source_target_pairs={{0,1},{1,0},{2,3},{3,2},{4,5},{5,4},{6,7},{7,6},{8,9},{9,8},{10,11... | collective-permute-start | bytes 4128776 | tf_op jit(solution)/shard_map/ppermute | solution.py:140
  39.1 32.9 %all-to-all-start = ((f32[128,1,128]{2,1,0:T(1,128)}), f32[128,1,128]{2,1,0:T(1,128)S(1)}, u32[]{:S(2)}, u32[]{:S(2)}) async-start(f32[128,1,128]{2,1,0:T(1,128)} %bitcast.7), calls=%async_computation | async-start | bytes 131072 | tf_op jit(solution)/shard_map/all_to_all | solution.py:148
  51.1 31.9 %collective-permute-start.4 = (bf16[512,128]{1,0:T(8,128)(2,1)S(1)}, bf16[512,128]{1,0:T(8,128)(2,1)S(1)}, u32[]{:S(2)}, u32[]{:S(2)}) collective-permute-start(bf16[512,128]{1,0:T(8,128)(2,1)S(1)} %get-tuple-element.13), channel_id=1, source_target_pairs={{8,0},{12,4},{16,8},{20,12},{24,16},{28,20},{32,24},{36,28},{40,32... | collective-permute-start | bytes 393224 | tf_op jit(solution)/shard_map/ppermute | solution.py:15
  60.0 23.0 %collective-permute-start.7 = (bf16[512,128]{1,0:T(8,128)(2,1)S(1)}, bf16[512,128]{1,0:T(8,128)(2,1)S(1)}, u32[]{:S(2)}, u32[]{:S(2)}) collective-permute-start(bf16[512,128]{1,0:T(8,128)(2,1)S(1)} %get-tuple-element.14), channel_id=1, source_target_pairs={{504,0},{508,4},{0,8},{4,12},{8,16},{12,20},{16,24},{20,28},{24,32... | collective-permute-start | bytes 393224 | tf_op jit(solution)/shard_map/ppermute | solution.py:15
  61.9 21.1 %collective-permute-start.6 = (bf16[512,128]{1,0:T(8,128)(2,1)S(1)}, bf16[512,128]{1,0:T(8,128)(2,1)S(1)}, u32[]{:S(2)}, u32[]{:S(2)}) collective-permute-start(bf16[512,128]{1,0:T(8,128)(2,1)S(1)} %get-tuple-element.15), channel_id=1, source_target_pairs={{508,0},{0,4},{4,8},{8,12},{12,16},{16,20},{20,24},{24,28},{28,32}... | collective-permute-start | bytes 393224 | tf_op jit(solution)/shard_map/ppermute | solution.py:15
  64.4 18.6 %collective-permute-start.5 = (bf16[512,128]{1,0:T(8,128)(2,1)S(1)}, bf16[512,128]{1,0:T(8,128)(2,1)S(1)}, u32[]{:S(2)}, u32[]{:S(2)}) collective-permute-start(bf16[512,128]{1,0:T(8,128)(2,1)S(1)} %get-tuple-element.16), channel_id=1, source_target_pairs={{4,0},{8,4},{12,8},{16,12},{20,16},{24,20},{28,24},{32,28},{36,32}... | collective-permute-start | bytes 393224 | tf_op jit(solution)/shard_map/ppermute | solution.py:15
  72.9 25.5 %all-to-all-start.1 = ((f32[128,1,128]{2,1,0:T(1,128)}), f32[128,1,128]{2,1,0:T(1,128)S(1)}, u32[]{:S(2)}, u32[]{:S(2)}) async-start(f32[128,1,128]{2,1,0:T(1,128)} %broadcast_in_dim.2), calls=%async_computation.1 | async-start | bytes 131072 | tf_op jit(solution)/shard_map/all_to_all | solution.py:151
  98.3 9.1 %collective-permute-start.8 = (f32[384,128]{1,0:T(8,128)S(1)}, f32[384,128]{1,0:T(8,128)S(1)}, u32[]{:S(2)}, u32[]{:S(2)}) collective-permute-start(f32[384,128]{1,0:T(8,128)S(1)} %pad_maximum_fusion.2), channel_id=1, source_target_pairs={{0,2},{1,3},{2,0},{3,1},{4,6},{5,7},{6,4},{7,5},{8,10},{9,11},{10,... | collective-permute-start | bytes 589832 | tf_op jit(solution)/shard_map/ppermute | solution.py:140

commit v6 on v5

--- a/solution.py
+++ b/solution.py
@@ -204,29 +204,49 @@
     rep_index = lax.axis_index("rep")
     core_bit = rep_index % 2
     chip_bit = rep_index // 2
+    team_size = lax.axis_size("team")
     quarter = team_rows // 4
     half_rows = 2 * quarter
-    staged = sums.reshape(section_count, 2, 2, quarter, feature_width)
-    kept = lax.dynamic_index_in_dim(staged, core_bit, 2, keepdims=False)
-    sent = lax.dynamic_index_in_dim(staged, 1 - core_bit, 2, keepdims=False)
+
+    given = lax.dynamic_slice_in_dim(sums, core_bit * (reach_size + 1), reach_size, 0)
+    mine = lax.dynamic_slice_in_dim(sums, (1 - core_bit) * (reach_size + 1), reach_size, 0)
+    local = sums[reach_size].reshape(2, 2, quarter, feature_width)
+    local_kept = lax.dynamic_index_in_dim(local, core_bit, 1, keepdims=False)
+    local_given = lax.dynamic_index_in_dim(local, 1 - core_bit, 1, keepdims=False)
     packet = jnp.concatenate(
-        [sent.reshape(section_count * half_rows, feature_width), local_weight_grad], axis=0
+        [
+            given.reshape(reach_size * team_rows, feature_width),
+            local_given.reshape(half_rows, feature_width),
+            local_weight_grad,
+        ],
+        axis=0,
     )
     arrived = swap_with(packet, "rep", 1)
-    kept = kept.reshape(section_count, half_rows, feature_width) + arrived[
-        : section_count * half_rows
-    ].reshape(section_count, half_rows, feature_width)
-    weight_grad = team_total_sum(local_weight_grad + arrived[section_count * half_rows :])
-
-    total = kept[reach_size]
-    for s in range(section_count):
-        if s != reach_size:
-            moved = from_behind(kept[s].astype(jnp.bfloat16), "team", s - reach_size)
-            total = total + moved.astype(jnp.float32)
-
-    staged = total.reshape(2, quarter, feature_width)
-    kept = lax.dynamic_index_in_dim(staged, chip_bit, 0, keepdims=False)
-    sent = lax.dynamic_index_in_dim(staged, 1 - chip_bit, 0, keepdims=False)
+    cut = reach_size * team_rows
+    mine = mine + arrived[:cut].reshape(reach_size, team_rows, feature_width)
+    local_kept = local_kept + arrived[cut : cut + half_rows].reshape(2, quarter, feature_width)
+    weight_grad = team_total_sum(local_weight_grad + arrived[cut + half_rows :])
+
+    incoming = None
+    for index in range(reach_size):
+        distance = index + 1
+        pick = index + core_bit * (reach_size - 1 - 2 * index)
+        block = lax.dynamic_index_in_dim(mine, pick, 0, keepdims=False).astype(jnp.bfloat16)
+        route = []
+        for team in range(team_size):
+            for rep in range(rep_size):
+                step = distance if rep % 2 == 0 else -distance
+                route.append((team * rep_size + rep, ((team + step) % team_size) * rep_size + rep))
+        moved = lax.ppermute(block, ("team", "rep"), route).astype(jnp.float32)
+        incoming = moved if incoming is None else incoming + moved
+
+    staged = incoming.reshape(2, 2, quarter, feature_width)
+    kept = lax.dynamic_index_in_dim(staged, core_bit, 1, keepdims=False)
+    sent = lax.dynamic_index_in_dim(staged, 1 - core_bit, 1, keepdims=False)
+    total = kept + local_kept + swap_with(sent, "rep", 1)
+
+    kept = lax.dynamic_index_in_dim(total, chip_bit, 0, keepdims=False)
+    sent = lax.dynamic_index_in_dim(total, 1 - chip_bit, 0, keepdims=False)
     arrived = swap_with(jnp.concatenate([sent, weight_grad], axis=0), "rep", 2)
     gradient_share = (kept + arrived[:quarter]).astype(jnp.bfloat16)
     grad_weight = (weight_grad + arrived[quarter:]) * (1.0 / math.sqrt(nodes_total))

time: 109 us -> 123 us (1.13)
  waiting for transfers between devices: 30.7 us -> 60.8 us
  starting transfers between devices: 67.4 us -> 46.1 us
  local copies, waits for them, and re-layouts: 2.58 us -> 5.49 us
  other arithmetic: 2.58 us -> 4.47 us
    ppermute x4 -> x2, waiting for transfers between devices: 0.01 us -> 15.5 us  [body(): moved = lax.ppermute(block, ('team', 'rep'), route).astype(jnp.float32)]
    ppermute x4 -> x2, starting transfers between devices: 20.9 us -> 5.75 us  [body(): moved = lax.ppermute(block, ('team', 'rep'), route).astype(jnp.float32)]
    all_to_all x1, waiting for transfers between devices: 0.01 us -> 14.4 us  [team_total_sum(): lax.all_to_all(block.reshape(size, rows // size, -1), 'team', 0, 0, tiled...]
    all_to_all x1, starting transfers between devices: 11.6 us -> 7.47 us  [team_total_sum(): lax.all_to_all(block.reshape(size, rows // size, -1), 'team', 0, 0, tiled...]
    all_to_all x1, starting transfers between devices: 10.2 us -> 6.15 us  [team_total_sum(): return lax.all_to_all(copies, 'team', 0, 0, tiled=True).reshape(block.shape)]
    slice x1 -> x3, local copies, waits for them, and re-layouts: 0.09 us -> 2.3 us  [the longest x1 1.29 us: body(): mine = mine + arrived[:cut].reshape(reach_size, team_rows, feature_width)]
    ppermute x3 -> x4, starting transfers between devices: 6.79 us -> 8.72 us  [swap_with(): return lax.ppermute(block, axis, route)]
    ppermute x3 -> x4, waiting for transfers between devices: 9.43 us -> 9.73 us  [swap_with(): return lax.ppermute(block, axis, route)]
  transfers between devices with their start and end apart: 11 -> 10, of which waited for: 6 -> 9; matrix products, arithmetic and copies ran while one was open for 3% -> 4% of each run, Pallas kernels for 0% -> 0%
where the time goes in v6:
time: 123 us; the launch traced here: 122 us
  waiting for transfers between devices  60.8 us (49%)
  starting transfers between devices  46.1 us (37%)
  local copies, waits for them, and re-layouts  5.49 us (4%)
  Pallas kernels  4.48 us (4%)
  other arithmetic  4.47 us (4%)
    ppermute x2, starting transfers between devices, gather_sources(): fetched.append(lax.ppermute(features, ('team', 'rep'), route))  18 us
    ppermute x2, waiting for transfers between devices, body(): moved = lax.ppermute(block, ('team', 'rep'), route).astype(jnp.float32)  15.5 us
    all_to_all x1, waiting for transfers between devices, team_total_sum(): return lax.all_to_all(copies, 'team', 0, 0, tiled=True).reshape(block.shape)  15.2 us
    all_to_all x1, waiting for transfers between devices, team_total_sum(): lax.all_to_all(block.reshape(size, rows // size, -1), 'team', 0, 0, tiled...  14.4 us
    ppermute x4, waiting for transfers between devices, swap_with(): return lax.ppermute(block, axis, route)  9.73 us
    ppermute x4, starting transfers between devices, swap_with(): return lax.ppermute(block, axis, route)  8.72 us
    all_to_all x1, starting transfers between devices, team_total_sum(): lax.all_to_all(block.reshape(size, rows // size, -1), 'team', 0, 0, tiled...  7.47 us
    all_to_all x1, starting transfers between devices, team_total_sum(): return lax.all_to_all(copies, 'team', 0, 0, tiled=True).reshape(block.shape)  6.15 us
  transfers between devices with their start and end apart: 10, of which 9 were waited for; matrix products, arithmetic and copies ran while one was open for 4% of the time, Pallas kernels for 0%

profile of v6, /device:TPU:4, one launch (start us, length us, event | category | flops | bytes accessed | tf_op | source)
XLA Modules:
  0.0 122.3 jit_solution(9499205676808661431)
XLA Ops:
  0.6 14.6 %collective-permute-start = (bf16[1024,128]{1,0:T(8,128)(2,1)}, bf16[1024,128]{1,0:T(8,128)(2,1)S(1)}, u32[]{:S(2)}, u32[]{:S(2)}) collective-permute-start(bf16[1024,128]{1,0:T(8,128)(2,1)} %refs_0_.1), channel_id=1, source_target_pairs={{4,0},{509,1},{6,2},{511,3},{8,4},{1,5},{10,6},{3,7},{12,8},{5,9},... | collective-permute-start | bytes 786440 | tf_op jit(solution)/shard_map/ppermute | solution.py:174
  15.3 3.4 %collective-permute-start.1 = (bf16[1024,128]{1,0:T(8,128)(2,1)}, bf16[1024,128]{1,0:T(8,128)(2,1)S(1)}, u32[]{:S(2)}, u32[]{:S(2)}) collective-permute-start(bf16[1024,128]{1,0:T(8,128)(2,1)} %refs_0_.1), channel_id=1, source_target_pairs={{8,0},{505,1},{10,2},{507,3},{12,4},{509,5},{14,6},{511,7},{16,8},... | collective-permute-start | bytes 786440 | tf_op jit(solution)/shard_map/ppermute | solution.py:174
  18.6 0.8 collective-permute-done.refs_1_
  19.5 5.3 %collective-permute-done.1.refs_2_ = bf16[1024,128]{1,0:T(8,128)(2,1)S(1)} collective-permute-done((bf16[1024,128]{1,0:T(8,128)(2,1)}, bf16[1024,128]{1,0:T(8,128)(2,1)S(1)}, u32[]{:S(2)}, u32[]{:S(2)}) %collective-permute-start.1) | collective-permute-done | bytes 262176 | tf_op jit(solution)/shard_map/ppermute | solution.py:174
  24.8 1.9 %collective-permute-start.2 = (bf16[2,1024,128]{2,1,0:T(8,128)(2,1)S(1)}, bf16[2,1024,128]{2,1,0:T(8,128)(2,1)S(1)}, u32[]{:S(2)}, u32[]{:S(2)}) collective-permute-start(bf16[2,1024,128]{2,1,0:T(8,128)(2,1)S(1)} %pad_maximum_fusion.1), channel_id=1, source_target_pairs={{0,1},{1,0},{2,3},{3,2},{4,5},{5,4},{6,7},{7,6},{8,9},{9,8},{10,11... | collective-permute-start | bytes 1572872 | tf_op jit(solution)/shard_map/ppermute | solution.py:140
  26.8 0.8 reshape.42.counts_ref
  29.4 4.5 %shard_map.94 = (bf16[256,128]{1,0:T(8,128)(2,1)}, f32[128,128]{1,0:T(8,128)S(1)}, f32[5,1024,128]{2,1,0:T(8,128)S(1)}) custom-call(s32[80]{0:T(128)S(1)} %reshape.41.coords_ref, s32[10]{0:T(128)S(1)} %reshape.42.counts_ref, s32[5]{0:T(128)S(1)} %pad_add_fusion.order_ref, bf16[1024,128]{1,0:T(8,128)(2,1)S(1)} %copy-done, ...), custom_call_target="tpu_custom_call" | custom-call | flops 704643072 | bytes 6553600 | tf_op jit(solution)/shard_map/pallas_call | solution.py:119
  34.1 1.2 pad_maximum_fusion
  35.3 2.2 %collective-permute-start.3 = (f32[2688,128]{1,0:T(8,128)}, f32[2688,128]{1,0:T(8,128)}, u32[]{:S(2)}, u32[]{:S(2)}) collective-permute-start(f32[2688,128]{1,0:T(8,128)} %pad_maximum_fusion), channel_id=1, source_target_pairs={{0,1},{1,0},{2,3},{3,2},{4,5},{5,4},{6,7},{7,6},{8,9},{9,8},{10,11... | collective-permute-start | bytes 4128776 | tf_op jit(solution)/shard_map/ppermute | solution.py:140
  37.5 3.2 %collective-permute-done.3 = f32[2688,128]{1,0:T(8,128)} collective-permute-done((f32[2688,128]{1,0:T(8,128)}, f32[2688,128]{1,0:T(8,128)}, u32[]{:S(2)}, u32[]{:S(2)}) %collective-permute-start.3) | collective-permute-done | bytes 1376288 | tf_op jit(solution)/shard_map/ppermute | solution.py:140
  40.6 1.3 %slice.35 = f32[2048,128]{1,0:T(8,128)S(1)} slice(f32[2688,128]{1,0:T(8,128)} %collective-permute-done.3), slice={[0:2048], [0:128]} | slice | bytes 2097152 | tf_op jit(solution)/shard_map/slice | solution.py:226
  42.1 3.8 %collective-permute-start.4 = (bf16[1024,128]{1,0:T(8,128)(2,1)S(1)}, bf16[1024,128]{1,0:T(8,128)(2,1)S(1)}, u32[]{:S(2)}, u32[]{:S(2)}) collective-permute-start(bf16[1024,128]{1,0:T(8,128)(2,1)S(1)} %get-tuple-element.9), channel_id=1, source_target_pairs={{0,4},{1,509},{2,6},{3,511},{4,8},{5,1},{6,10},{7,3},{8,12},{9,5},... | collective-permute-start | bytes 786440 | tf_op jit(solution)/shard_map/ppermute | solution.py:240
  45.9 1.9 %collective-permute-start.5 = (bf16[1024,128]{1,0:T(8,128)(2,1)S(1)}, bf16[1024,128]{1,0:T(8,128)(2,1)S(1)}, u32[]{:S(2)}, u32[]{:S(2)}) collective-permute-start(bf16[1024,128]{1,0:T(8,128)(2,1)S(1)} %get-tuple-element.10), channel_id=1, source_target_pairs={{0,8},{1,505},{2,10},{3,507},{4,12},{5,509},{6,14},{7,511},{8,16},... | collective-permute-start | bytes 786440 | tf_op jit(solution)/shard_map/ppermute | solution.py:240
  47.8 8.4 %collective-permute-done.4 = bf16[1024,128]{1,0:T(8,128)(2,1)S(1)} collective-permute-done((bf16[1024,128]{1,0:T(8,128)(2,1)S(1)}, bf16[1024,128]{1,0:T(8,128)(2,1)S(1)}, u32[]{:S(2)}, u32[]{:S(2)}) %collective-permute-start.4) | collective-permute-done | bytes 262176 | tf_op jit(solution)/shard_map/ppermute | solution.py:240
  56.3 7.1 %collective-permute-done.5 = bf16[1024,128]{1,0:T(8,128)(2,1)S(1)} collective-permute-done((bf16[1024,128]{1,0:T(8,128)(2,1)S(1)}, bf16[1024,128]{1,0:T(8,128)(2,1)S(1)}, u32[]{:S(2)}, u32[]{:S(2)}) %collective-permute-start.5) | collective-permute-done | bytes 262176 | tf_op jit(solution)/shard_map/ppermute | solution.py:240
  63.4 1.9 %collective-permute-start.6 = (f32[2,256,128]{2,1,0:T(8,128)S(1)}, f32[2,256,128]{2,1,0:T(8,128)S(1)}, u32[]{:S(2)}, u32[]{:S(2)}) collective-permute-start(f32[2,256,128]{2,1,0:T(8,128)S(1)} %dynamic-slice_bitcast_fusion), channel_id=1, source_target_pairs={{0,1},{1,0},{2,3},{3,2},{4,5},{5,4},{6,7},{7,6},{8,9},{9,8},{10,11... | collective-permute-start | bytes 786440 | tf_op jit(solution)/shard_map/ppermute | solution.py:140
  65.4 1.5 %slice_add_fusion.2 = f32[128,128]{1,0:T(8,128)} fusion(f32[128,128]{1,0:T(8,128)S(1)} %get-tuple-element.7, f32[2688,128]{1,0:T(8,128)} %collective-permute-done.3), kind=kLoop, calls=%fused_computation.20 | loop fusion | flops 16384 | bytes 196608 | tf_op jit(solution)/shard_map/add | solution.py:228
  66.8 7.5 %all-to-all-start = ((f32[128,1,128]{2,1,0:T(1,128)}), f32[128,1,128]{2,1,0:T(1,128)S(1)}, u32[]{:S(2)}, u32[]{:S(2)}) async-start(f32[128,1,128]{2,1,0:T(1,128)} %bitcast.8), calls=%async_computation | async-start | bytes 131072 | tf_op jit(solution)/shard_map/all_to_all | solution.py:148
  74.3 1.0 slice.36
  75.3 14.4 %all-to-all-done = f32[128,1,128]{2,1,0:T(1,128)S(1)} async-done(((f32[128,1,128]{2,1,0:T(1,128)}), f32[128,1,128]{2,1,0:T(1,128)S(1)}, u32[]{:S(2)}, u32[]{:S(2)}) %all-to-all-start) | async-done | bytes 65568 | tf_op jit(solution)/shard_map/all_to_all | solution.py:148
  90.5 6.1 %all-to-all-start.1 = ((f32[128,1,128]{2,1,0:T(1,128)}), f32[128,1,128]{2,1,0:T(1,128)S(1)}, u32[]{:S(2)}, u32[]{:S(2)}) async-start(f32[128,1,128]{2,1,0:T(1,128)} %broadcast_in_dim.2), calls=%async_computation.1 | async-start | bytes 131072 | tf_op jit(solution)/shard_map/all_to_all | solution.py:151
  96.7 15.2 %all-to-all-done.1 = f32[128,1,128]{2,1,0:T(1,128)S(1)} async-done(((f32[128,1,128]{2,1,0:T(1,128)}), f32[128,1,128]{2,1,0:T(1,128)S(1)}, u32[]{:S(2)}, u32[]{:S(2)}) %all-to-all-start.1) | async-done | bytes 65568 | tf_op jit(solution)/shard_map/all_to_all | solution.py:151
  111.9 2.7 %collective-permute-start.7 = (f32[384,128]{1,0:T(8,128)S(1)}, f32[384,128]{1,0:T(8,128)S(1)}, u32[]{:S(2)}, u32[]{:S(2)}) collective-permute-start(f32[384,128]{1,0:T(8,128)S(1)} %pad_maximum_fusion.2), channel_id=1, source_target_pairs={{0,2},{1,3},{2,0},{3,1},{4,6},{5,7},{6,4},{7,5},{8,10},{9,11},{10,... | collective-permute-start | bytes 589832 | tf_op jit(solution)/shard_map/ppermute | solution.py:140
  114.6 6.3 %collective-permute-done.7 = f32[384,128]{1,0:T(8,128)S(1)} collective-permute-done((f32[384,128]{1,0:T(8,128)S(1)}, f32[384,128]{1,0:T(8,128)S(1)}, u32[]{:S(2)}, u32[]{:S(2)}) %collective-permute-start.7) | collective-permute-done | bytes 196640 | tf_op jit(solution)/shard_map/ppermute | solution.py:140
  (28 shorter events, 4.5 us)
Async XLA Ops:
  0.6 28.0 %copy-start = (bf16[1024,128]{1,0:T(8,128)(2,1)S(1)}, bf16[1024,128]{1,0:T(8,128)(2,1)}, u32[]{:S(2)}) copy-start(bf16[1024,128]{1,0:T(8,128)(2,1)} %refs_0_.1) | copy-start | bytes 786436
  0.6 28.0 %copy-start.1 = (bf16[256,128]{1,0:T(8,128)(2,1)S(1)}, bf16[256,128]{1,0:T(8,128)(2,1)}, u32[]{:S(2)}) copy-start(bf16[256,128]{1,0:T(8,128)(2,1)} %refs_6_.1) | copy-start | bytes 196612
  0.6 18.8 %collective-permute-start = (bf16[1024,128]{1,0:T(8,128)(2,1)}, bf16[1024,128]{1,0:T(8,128)(2,1)S(1)}, u32[]{:S(2)}, u32[]{:S(2)}) collective-permute-start(bf16[1024,128]{1,0:T(8,128)(2,1)} %refs_0_.1), channel_id=1, source_target_pairs={{4,0},{509,1},{6,2},{511,3},{8,4},{1,5},{10,6},{3,7},{12,8},{5,9},... | collective-permute-start | bytes 786440 | tf_op jit(solution)/shard_map/ppermute | solution.py:174
  15.3 9.5 %collective-permute-start.1 = (bf16[1024,128]{1,0:T(8,128)(2,1)}, bf16[1024,128]{1,0:T(8,128)(2,1)S(1)}, u32[]{:S(2)}, u32[]{:S(2)}) collective-permute-start(bf16[1024,128]{1,0:T(8,128)(2,1)} %refs_0_.1), channel_id=1, source_target_pairs={{8,0},{505,1},{10,2},{507,3},{12,4},{509,5},{14,6},{511,7},{16,8},... | collective-permute-start | bytes 786440 | tf_op jit(solution)/shard_map/ppermute | solution.py:174
  24.8 3.8 %collective-permute-start.2 = (bf16[2,1024,128]{2,1,0:T(8,128)(2,1)S(1)}, bf16[2,1024,128]{2,1,0:T(8,128)(2,1)S(1)}, u32[]{:S(2)}, u32[]{:S(2)}) collective-permute-start(bf16[2,1024,128]{2,1,0:T(8,128)(2,1)S(1)} %pad_maximum_fusion.1), channel_id=1, source_target_pairs={{0,1},{1,0},{2,3},{3,2},{4,5},{5,4},{6,7},{7,6},{8,9},{9,8},{10,11... | collective-permute-start | bytes 1572872 | tf_op jit(solution)/shard_map/ppermute | solution.py:140
  28.7 0.8 copy-start.2
  35.3 5.4 %collective-permute-start.3 = (f32[2688,128]{1,0:T(8,128)}, f32[2688,128]{1,0:T(8,128)}, u32[]{:S(2)}, u32[]{:S(2)}) collective-permute-start(f32[2688,128]{1,0:T(8,128)} %pad_maximum_fusion), channel_id=1, source_target_pairs={{0,1},{1,0},{2,3},{3,2},{4,5},{5,4},{6,7},{7,6},{8,9},{9,8},{10,11... | collective-permute-start | bytes 4128776 | tf_op jit(solution)/shard_map/ppermute | solution.py:140
  42.1 14.2 %collective-permute-start.4 = (bf16[1024,128]{1,0:T(8,128)(2,1)S(1)}, bf16[1024,128]{1,0:T(8,128)(2,1)S(1)}, u32[]{:S(2)}, u32[]{:S(2)}) collective-permute-start(bf16[1024,128]{1,0:T(8,128)(2,1)S(1)} %get-tuple-element.9), channel_id=1, source_target_pairs={{0,4},{1,509},{2,6},{3,511},{4,8},{5,1},{6,10},{7,3},{8,12},{9,5},... | collective-permute-start | bytes 786440 | tf_op jit(solution)/shard_map/ppermute | solution.py:240
  45.9 17.4 %collective-permute-start.5 = (bf16[1024,128]{1,0:T(8,128)(2,1)S(1)}, bf16[1024,128]{1,0:T(8,128)(2,1)S(1)}, u32[]{:S(2)}, u32[]{:S(2)}) collective-permute-start(bf16[1024,128]{1,0:T(8,128)(2,1)S(1)} %get-tuple-element.10), channel_id=1, source_target_pairs={{0,8},{1,505},{2,10},{3,507},{4,12},{5,509},{6,14},{7,511},{8,16},... | collective-permute-start | bytes 786440 | tf_op jit(solution)/shard_map/ppermute | solution.py:240
  63.4 33.2 %collective-permute-start.6 = (f32[2,256,128]{2,1,0:T(8,128)S(1)}, f32[2,256,128]{2,1,0:T(8,128)S(1)}, u32[]{:S(2)}, u32[]{:S(2)}) collective-permute-start(f32[2,256,128]{2,1,0:T(8,128)S(1)} %dynamic-slice_bitcast_fusion), channel_id=1, source_target_pairs={{0,1},{1,0},{2,3},{3,2},{4,5},{5,4},{6,7},{7,6},{8,9},{9,8},{10,11... | collective-permute-start | bytes 786440 | tf_op jit(solution)/shard_map/ppermute | solution.py:140
  66.8 22.8 %all-to-all-start = ((f32[128,1,128]{2,1,0:T(1,128)}), f32[128,1,128]{2,1,0:T(1,128)S(1)}, u32[]{:S(2)}, u32[]{:S(2)}) async-start(f32[128,1,128]{2,1,0:T(1,128)} %bitcast.8), calls=%async_computation | async-start | bytes 131072 | tf_op jit(solution)/shard_map/all_to_all | solution.py:148
  90.5 21.4 %all-to-all-start.1 = ((f32[128,1,128]{2,1,0:T(1,128)}), f32[128,1,128]{2,1,0:T(1,128)S(1)}, u32[]{:S(2)}, u32[]{:S(2)}) async-start(f32[128,1,128]{2,1,0:T(1,128)} %broadcast_in_dim.2), calls=%async_computation.1 | async-start | bytes 131072 | tf_op jit(solution)/shard_map/all_to_all | solution.py:151
  111.9 9.1 %collective-permute-start.7 = (f32[384,128]{1,0:T(8,128)S(1)}, f32[384,128]{1,0:T(8,128)S(1)}, u32[]{:S(2)}, u32[]{:S(2)}) collective-permute-start(f32[384,128]{1,0:T(8,128)S(1)} %pad_maximum_fusion.2), channel_id=1, source_target_pairs={{0,2},{1,3},{2,0},{3,1},{4,6},{5,7},{6,4},{7,5},{8,10},{9,11},{10,... | collective-permute-start | bytes 589832 | tf_op jit(solution)/shard_map/ppermute | solution.py:140

commit v7 on v5

--- a/solution.py
+++ b/solution.py
@@ -140,15 +140,18 @@
     return lax.ppermute(block, axis, route)
 
 
-def team_total_sum(block):
+def team_scatter_sum(block):
     size = lax.axis_size("team")
     rows = block.shape[0]
-    if rows % size:
-        return butterfly_sum(block, ("team",))
     pieces = lax.all_to_all(block.reshape(size, rows // size, -1), "team", 0, 0, tiled=True)
-    own = jnp.sum(pieces, axis=0)
-    copies = jnp.broadcast_to(own[None], (size,) + own.shape)
-    return lax.all_to_all(copies, "team", 0, 0, tiled=True).reshape(block.shape)
+    return jnp.sum(pieces, axis=0)
+
+
+def team_gather(piece):
+    size = lax.axis_size("team")
+    copies = jnp.broadcast_to(piece[None], (size,) + piece.shape)
+    gathered = lax.all_to_all(copies, "team", 0, 0, tiled=True)
+    return gathered.reshape(size * piece.shape[0], -1)
 
 
 def gather_sources(features, reach_size, rep_size):
@@ -216,7 +219,7 @@
     kept = kept.reshape(section_count, half_rows, feature_width) + arrived[
         : section_count * half_rows
     ].reshape(section_count, half_rows, feature_width)
-    weight_grad = team_total_sum(local_weight_grad + arrived[section_count * half_rows :])
+    weight_grad = team_scatter_sum(local_weight_grad + arrived[section_count * half_rows :])
 
     total = kept[reach_size]
     for s in range(section_count):
@@ -229,7 +232,7 @@
     sent = lax.dynamic_index_in_dim(staged, 1 - chip_bit, 0, keepdims=False)
     arrived = swap_with(jnp.concatenate([sent, weight_grad], axis=0), "rep", 2)
     gradient_share = (kept + arrived[:quarter]).astype(jnp.bfloat16)
-    grad_weight = (weight_grad + arrived[quarter:]) * (1.0 / math.sqrt(nodes_total))
+    grad_weight = team_gather(weight_grad + arrived[quarter:]) * (1.0 / math.sqrt(nodes_total))
     return (activated, grad_weight, gradient_share)
 
 

time: 109 us -> 119 us (1.092)
  waiting for transfers between devices: 30.7 us -> 44.8 us
  starting transfers between devices: 67.4 us -> 59.8 us
  other arithmetic: 2.58 us -> 4.57 us
    all_to_all x2, waiting for transfers between devices: 15.1 us -> 29.7 us  [the longest x1 15.1 us: team_scatter_sum(): lax.all_to_all(block.reshape(size, rows // size, -1), 'team', 0, 0, tiled...]
    all_to_all x2, starting transfers between devices: 21.8 us -> 12.3 us  [the longest x1 6.15 us: team_scatter_sum(): lax.all_to_all(block.reshape(size, rows // size, -1), 'team', 0, 0, tiled...]
    ppermute x4, starting transfers between devices: 20.9 us -> 22.7 us  [from_behind(): return lax.ppermute(block, axis, route)]
  transfers between devices with their start and end apart: 11 -> 11, of which waited for: 6 -> 7; matrix products, arithmetic and copies ran while one was open for 3% -> 3% of each run, Pallas kernels for 0% -> 0%
where the time goes in v7:
time: 119 us; the launch traced here: 118 us
  starting transfers between devices  59.8 us (50%)
  waiting for transfers between devices  44.8 us (38%)
  other arithmetic  4.57 us (4%)
  Pallas kernels  4.5 us (4%)
  local copies, waits for them, and re-layouts  3.61 us (3%)
    ppermute x4, starting transfers between devices, from_behind(): return lax.ppermute(block, axis, route)  22.7 us
    ppermute x2, starting transfers between devices, gather_sources(): fetched.append(lax.ppermute(features, ('team', 'rep'), route))  18 us
    all_to_all x1, waiting for transfers between devices, team_scatter_sum(): lax.all_to_all(block.reshape(size, rows // size, -1), 'team', 0, 0, tiled...  15.1 us
    all_to_all x1, waiting for transfers between devices, team_gather(): gathered = lax.all_to_all(copies, 'team', 0, 0, tiled=True)  14.6 us
    ppermute x3, waiting for transfers between devices, swap_with(): return lax.ppermute(block, axis, route)  8.98 us
    ppermute x3, starting transfers between devices, swap_with(): return lax.ppermute(block, axis, route)  6.77 us
    all_to_all x1, starting transfers between devices, team_scatter_sum(): lax.all_to_all(block.reshape(size, rows // size, -1), 'team', 0, 0, tiled...  6.15 us
    all_to_all x1, starting transfers between devices, team_gather(): gathered = lax.all_to_all(copies, 'team', 0, 0, tiled=True)  6.15 us
  transfers between devices with their start and end apart: 11, of which 7 were waited for; matrix products, arithmetic and copies ran while one was open for 3% of the time, Pallas kernels for 0%

profile of v7, /device:TPU:4, one launch (start us, length us, event | category | flops | bytes accessed | tf_op | source)
XLA Modules:
  0.0 118.1 jit_solution(8614638647991846610)
XLA Ops:
  0.7 14.6 %collective-permute-start = (bf16[1024,128]{1,0:T(8,128)(2,1)}, bf16[1024,128]{1,0:T(8,128)(2,1)S(1)}, u32[]{:S(2)}, u32[]{:S(2)}) collective-permute-start(bf16[1024,128]{1,0:T(8,128)(2,1)} %refs_0_.1), channel_id=1, source_target_pairs={{4,0},{509,1},{6,2},{511,3},{8,4},{1,5},{10,6},{3,7},{12,8},{5,9},... | collective-permute-start | bytes 786440 | tf_op jit(solution)/shard_map/ppermute | solution.py:177
  15.3 3.4 %collective-permute-start.1 = (bf16[1024,128]{1,0:T(8,128)(2,1)}, bf16[1024,128]{1,0:T(8,128)(2,1)S(1)}, u32[]{:S(2)}, u32[]{:S(2)}) collective-permute-start(bf16[1024,128]{1,0:T(8,128)(2,1)} %refs_0_.1), channel_id=1, source_target_pairs={{8,0},{505,1},{10,2},{507,3},{12,4},{509,5},{14,6},{511,7},{16,8},... | collective-permute-start | bytes 786440 | tf_op jit(solution)/shard_map/ppermute | solution.py:177
  18.7 0.8 collective-permute-done.refs_1_
  19.5 5.3 %collective-permute-done.1.refs_2_ = bf16[1024,128]{1,0:T(8,128)(2,1)S(1)} collective-permute-done((bf16[1024,128]{1,0:T(8,128)(2,1)}, bf16[1024,128]{1,0:T(8,128)(2,1)S(1)}, u32[]{:S(2)}, u32[]{:S(2)}) %collective-permute-start.1) | collective-permute-done | bytes 262176 | tf_op jit(solution)/shard_map/ppermute | solution.py:177
  24.8 1.9 %collective-permute-start.2 = (bf16[2,1024,128]{2,1,0:T(8,128)(2,1)S(1)}, bf16[2,1024,128]{2,1,0:T(8,128)(2,1)S(1)}, u32[]{:S(2)}, u32[]{:S(2)}) collective-permute-start(bf16[2,1024,128]{2,1,0:T(8,128)(2,1)S(1)} %pad_maximum_fusion.1), channel_id=1, source_target_pairs={{0,1},{1,0},{2,3},{3,2},{4,5},{5,4},{6,7},{7,6},{8,9},{9,8},{10,11... | collective-permute-start | bytes 1572872 | tf_op jit(solution)/shard_map/ppermute | solution.py:140
  26.8 0.8 reshape.44.counts_ref
  27.5 0.7 copy.12
  28.7 4.5 %shard_map.94 = (bf16[256,128]{1,0:T(8,128)(2,1)}, f32[128,128]{1,0:T(8,128)S(1)}, f32[5,1024,128]{2,1,0:T(8,128)S(1)}) custom-call(s32[80]{0:T(128)S(1)} %reshape.43.coords_ref, s32[10]{0:T(128)S(1)} %reshape.44.counts_ref, s32[5]{0:T(128)S(1)} %pad_add_fusion.order_ref, bf16[1024,128]{1,0:T(8,128)(2,1)S(1)} %copy-done, ...), custom_call_target="tpu_custom_call" | custom-call | flops 704643072 | bytes 6553600 | tf_op jit(solution)/shard_map/pallas_call | solution.py:119
  33.4 1.2 pad_maximum_fusion
  34.6 2.2 %collective-permute-start.3 = (f32[2688,128]{1,0:T(8,128)}, f32[2688,128]{1,0:T(8,128)S(1)}, u32[]{:S(2)}, u32[]{:S(2)}) collective-permute-start(f32[2688,128]{1,0:T(8,128)} %pad_maximum_fusion), channel_id=1, source_target_pairs={{0,1},{1,0},{2,3},{3,2},{4,5},{5,4},{6,7},{7,6},{8,9},{9,8},{10,11... | collective-permute-start | bytes 4128776 | tf_op jit(solution)/shard_map/ppermute | solution.py:140
  36.8 3.0 %collective-permute-done.3 = f32[2688,128]{1,0:T(8,128)S(1)} collective-permute-done((f32[2688,128]{1,0:T(8,128)}, f32[2688,128]{1,0:T(8,128)S(1)}, u32[]{:S(2)}, u32[]{:S(2)}) %collective-permute-start.3) | collective-permute-done | bytes 1376288 | tf_op jit(solution)/shard_map/ppermute | solution.py:140
  39.9 1.0 copy-done.3
  41.1 8.0 %collective-permute-start.4 = (bf16[512,128]{1,0:T(8,128)(2,1)S(1)}, bf16[512,128]{1,0:T(8,128)(2,1)S(1)}, u32[]{:S(2)}, u32[]{:S(2)}) collective-permute-start(bf16[512,128]{1,0:T(8,128)(2,1)S(1)} %get-tuple-element.13), channel_id=1, source_target_pairs={{8,0},{12,4},{16,8},{20,12},{24,16},{28,20},{32,24},{36,28},{40,32... | collective-permute-start | bytes 393224 | tf_op jit(solution)/shard_map/ppermute | solution.py:15
  49.2 1.9 %collective-permute-start.7 = (bf16[512,128]{1,0:T(8,128)(2,1)S(1)}, bf16[512,128]{1,0:T(8,128)(2,1)S(1)}, u32[]{:S(2)}, u32[]{:S(2)}) collective-permute-start(bf16[512,128]{1,0:T(8,128)(2,1)S(1)} %get-tuple-element.14), channel_id=1, source_target_pairs={{504,0},{508,4},{0,8},{4,12},{8,16},{12,20},{16,24},{20,28},{24,32... | collective-permute-start | bytes 393224 | tf_op jit(solution)/shard_map/ppermute | solution.py:15
  51.1 5.2 %collective-permute-start.6 = (bf16[512,128]{1,0:T(8,128)(2,1)S(1)}, bf16[512,128]{1,0:T(8,128)(2,1)S(1)}, u32[]{:S(2)}, u32[]{:S(2)}) collective-permute-start(bf16[512,128]{1,0:T(8,128)(2,1)S(1)} %get-tuple-element.15), channel_id=1, source_target_pairs={{508,0},{0,4},{4,8},{8,12},{12,16},{16,20},{20,24},{24,28},{28,32}... | collective-permute-start | bytes 393224 | tf_op jit(solution)/shard_map/ppermute | solution.py:15
  56.3 7.6 %collective-permute-start.5 = (bf16[512,128]{1,0:T(8,128)(2,1)S(1)}, bf16[512,128]{1,0:T(8,128)(2,1)S(1)}, u32[]{:S(2)}, u32[]{:S(2)}) collective-permute-start(bf16[512,128]{1,0:T(8,128)(2,1)S(1)} %get-tuple-element.16), channel_id=1, source_target_pairs={{4,0},{8,4},{12,8},{16,12},{20,16},{24,20},{28,24},{32,28},{36,32}... | collective-permute-start | bytes 393224 | tf_op jit(solution)/shard_map/ppermute | solution.py:15
  63.9 1.5 %slice_add_fusion.1 = f32[128,128]{1,0:T(8,128)} fusion(f32[128,128]{1,0:T(8,128)S(1)} %get-tuple-element.7, f32[2688,128]{1,0:T(8,128)} %copy-done.3), kind=kLoop, calls=%fused_computation.18 | loop fusion | flops 16384 | bytes 196608 | tf_op jit(solution)/shard_map/add | solution.py:222
  65.4 6.1 %all-to-all-start = ((f32[128,1,128]{2,1,0:T(1,128)}), f32[128,1,128]{2,1,0:T(1,128)S(1)}, u32[]{:S(2)}, u32[]{:S(2)}) async-start(f32[128,1,128]{2,1,0:T(1,128)} %bitcast.7), calls=%async_computation | async-start | bytes 131072 | tf_op jit(solution)/shard_map/all_to_all | solution.py:146
  71.7 15.1 %all-to-all-done = f32[128,1,128]{2,1,0:T(1,128)S(1)} async-done(((f32[128,1,128]{2,1,0:T(1,128)}), f32[128,1,128]{2,1,0:T(1,128)S(1)}, u32[]{:S(2)}, u32[]{:S(2)}) %all-to-all-start) | async-done | bytes 65568 | tf_op jit(solution)/shard_map/all_to_all | solution.py:146
  86.9 2.7 %collective-permute-start.8 = (f32[257,128]{1,0:T(8,128)S(1)}, f32[257,128]{1,0:T(8,128)S(1)}, u32[]{:S(2)}, u32[]{:S(2)}) collective-permute-start(f32[257,128]{1,0:T(8,128)S(1)} %pad_maximum_fusion.2), channel_id=1, source_target_pairs={{0,2},{1,3},{2,0},{3,1},{4,6},{5,7},{6,4},{7,5},{8,10},{9,11},{10,... | collective-permute-start | bytes 394760 | tf_op jit(solution)/shard_map/ppermute | solution.py:140
  89.6 5.7 %collective-permute-done.8 = f32[257,128]{1,0:T(8,128)S(1)} collective-permute-done((f32[257,128]{1,0:T(8,128)S(1)}, f32[257,128]{1,0:T(8,128)S(1)}, u32[]{:S(2)}, u32[]{:S(2)}) %collective-permute-start.8) | collective-permute-done | bytes 131616 | tf_op jit(solution)/shard_map/ppermute | solution.py:140
  96.0 6.1 %all-to-all-start.1 = ((f32[128,1,128]{2,1,0:T(1,128)}), f32[128,1,128]{2,1,0:T(1,128)S(1)}, u32[]{:S(2)}, u32[]{:S(2)}) async-start(f32[128,1,128]{2,1,0:T(1,128)} %broadcast_in_dim.9), calls=%async_computation.1 | async-start | bytes 131072 | tf_op jit(solution)/shard_map/all_to_all | solution.py:153
  102.8 14.6 %all-to-all-done.1 = f32[128,1,128]{2,1,0:T(1,128)S(1)} async-done(((f32[128,1,128]{2,1,0:T(1,128)}), f32[128,1,128]{2,1,0:T(1,128)S(1)}, u32[]{:S(2)}, u32[]{:S(2)}) %all-to-all-start.1) | async-done | bytes 65568 | tf_op jit(solution)/shard_map/all_to_all | solution.py:153
  117.4 0.7 broadcast_multiply_fusion
  (28 shorter events, 2.6 us)
Async XLA Ops:
  0.6 28.0 %copy-start = (bf16[1024,128]{1,0:T(8,128)(2,1)S(1)}, bf16[1024,128]{1,0:T(8,128)(2,1)}, u32[]{:S(2)}) copy-start(bf16[1024,128]{1,0:T(8,128)(2,1)} %refs_0_.1) | copy-start | bytes 786436
  0.6 28.0 %copy-start.1 = (bf16[256,128]{1,0:T(8,128)(2,1)S(1)}, bf16[256,128]{1,0:T(8,128)(2,1)}, u32[]{:S(2)}) copy-start(bf16[256,128]{1,0:T(8,128)(2,1)} %refs_6_.1) | copy-start | bytes 196612
  0.7 28.0 %copy-start.2 = (bf16[128,128]{1,0:T(8,128)(2,1)S(1)}, bf16[128,128]{1,0:T(8,128)(2,1)}, u32[]{:S(2)}) copy-start(bf16[128,128]{1,0:T(8,128)(2,1)} %refs_7_.1) | copy-start | bytes 98308
  0.7 18.8 %collective-permute-start = (bf16[1024,128]{1,0:T(8,128)(2,1)}, bf16[1024,128]{1,0:T(8,128)(2,1)S(1)}, u32[]{:S(2)}, u32[]{:S(2)}) collective-permute-start(bf16[1024,128]{1,0:T(8,128)(2,1)} %refs_0_.1), channel_id=1, source_target_pairs={{4,0},{509,1},{6,2},{511,3},{8,4},{1,5},{10,6},{3,7},{12,8},{5,9},... | collective-permute-start | bytes 786440 | tf_op jit(solution)/shard_map/ppermute | solution.py:177
  15.3 9.5 %collective-permute-start.1 = (bf16[1024,128]{1,0:T(8,128)(2,1)}, bf16[1024,128]{1,0:T(8,128)(2,1)S(1)}, u32[]{:S(2)}, u32[]{:S(2)}) collective-permute-start(bf16[1024,128]{1,0:T(8,128)(2,1)} %refs_0_.1), channel_id=1, source_target_pairs={{8,0},{505,1},{10,2},{507,3},{12,4},{509,5},{14,6},{511,7},{16,8},... | collective-permute-start | bytes 786440 | tf_op jit(solution)/shard_map/ppermute | solution.py:177
  24.8 3.8 %collective-permute-start.2 = (bf16[2,1024,128]{2,1,0:T(8,128)(2,1)S(1)}, bf16[2,1024,128]{2,1,0:T(8,128)(2,1)S(1)}, u32[]{:S(2)}, u32[]{:S(2)}) collective-permute-start(bf16[2,1024,128]{2,1,0:T(8,128)(2,1)S(1)} %pad_maximum_fusion.1), channel_id=1, source_target_pairs={{0,1},{1,0},{2,3},{3,2},{4,5},{5,4},{6,7},{7,6},{8,9},{9,8},{10,11... | collective-permute-start | bytes 1572872 | tf_op jit(solution)/shard_map/ppermute | solution.py:140
  34.6 5.2 %collective-permute-start.3 = (f32[2688,128]{1,0:T(8,128)}, f32[2688,128]{1,0:T(8,128)S(1)}, u32[]{:S(2)}, u32[]{:S(2)}) collective-permute-start(f32[2688,128]{1,0:T(8,128)} %pad_maximum_fusion), channel_id=1, source_target_pairs={{0,1},{1,0},{2,3},{3,2},{4,5},{5,4},{6,7},{7,6},{8,9},{9,8},{10,11... | collective-permute-start | bytes 4128776 | tf_op jit(solution)/shard_map/ppermute | solution.py:140
  39.8 1.1 copy-start.3
  41.1 30.4 %collective-permute-start.4 = (bf16[512,128]{1,0:T(8,128)(2,1)S(1)}, bf16[512,128]{1,0:T(8,128)(2,1)S(1)}, u32[]{:S(2)}, u32[]{:S(2)}) collective-permute-start(bf16[512,128]{1,0:T(8,128)(2,1)S(1)} %get-tuple-element.13), channel_id=1, source_target_pairs={{8,0},{12,4},{16,8},{20,12},{24,16},{28,20},{32,24},{36,28},{40,32... | collective-permute-start | bytes 393224 | tf_op jit(solution)/shard_map/ppermute | solution.py:15
  49.2 22.4 %collective-permute-start.7 = (bf16[512,128]{1,0:T(8,128)(2,1)S(1)}, bf16[512,128]{1,0:T(8,128)(2,1)S(1)}, u32[]{:S(2)}, u32[]{:S(2)}) collective-permute-start(bf16[512,128]{1,0:T(8,128)(2,1)S(1)} %get-tuple-element.14), channel_id=1, source_target_pairs={{504,0},{508,4},{0,8},{4,12},{8,16},{12,20},{16,24},{20,28},{24,32... | collective-permute-start | bytes 393224 | tf_op jit(solution)/shard_map/ppermute | solution.py:15
  51.1 20.4 %collective-permute-start.6 = (bf16[512,128]{1,0:T(8,128)(2,1)S(1)}, bf16[512,128]{1,0:T(8,128)(2,1)S(1)}, u32[]{:S(2)}, u32[]{:S(2)}) collective-permute-start(bf16[512,128]{1,0:T(8,128)(2,1)S(1)} %get-tuple-element.15), channel_id=1, source_target_pairs={{508,0},{0,4},{4,8},{8,12},{12,16},{16,20},{20,24},{24,28},{28,32}... | collective-permute-start | bytes 393224 | tf_op jit(solution)/shard_map/ppermute | solution.py:15
  56.3 15.3 %collective-permute-start.5 = (bf16[512,128]{1,0:T(8,128)(2,1)S(1)}, bf16[512,128]{1,0:T(8,128)(2,1)S(1)}, u32[]{:S(2)}, u32[]{:S(2)}) collective-permute-start(bf16[512,128]{1,0:T(8,128)(2,1)S(1)} %get-tuple-element.16), channel_id=1, source_target_pairs={{4,0},{8,4},{12,8},{16,12},{20,16},{24,20},{28,24},{32,28},{36,32}... | collective-permute-start | bytes 393224 | tf_op jit(solution)/shard_map/ppermute | solution.py:15
  65.4 21.4 %all-to-all-start = ((f32[128,1,128]{2,1,0:T(1,128)}), f32[128,1,128]{2,1,0:T(1,128)S(1)}, u32[]{:S(2)}, u32[]{:S(2)}) async-start(f32[128,1,128]{2,1,0:T(1,128)} %bitcast.7), calls=%async_computation | async-start | bytes 131072 | tf_op jit(solution)/shard_map/all_to_all | solution.py:146
  86.9 8.4 %collective-permute-start.8 = (f32[257,128]{1,0:T(8,128)S(1)}, f32[257,128]{1,0:T(8,128)S(1)}, u32[]{:S(2)}, u32[]{:S(2)}) collective-permute-start(f32[257,128]{1,0:T(8,128)S(1)} %pad_maximum_fusion.2), channel_id=1, source_target_pairs={{0,2},{1,3},{2,0},{3,1},{4,6},{5,7},{6,4},{7,5},{8,10},{9,11},{10,... | collective-permute-start | bytes 394760 | tf_op jit(solution)/shard_map/ppermute | solution.py:140
  96.0 21.4 %all-to-all-start.1 = ((f32[128,1,128]{2,1,0:T(1,128)}), f32[128,1,128]{2,1,0:T(1,128)S(1)}, u32[]{:S(2)}, u32[]{:S(2)}) async-start(f32[128,1,128]{2,1,0:T(1,128)} %broadcast_in_dim.9), calls=%async_computation.1 | async-start | bytes 131072 | tf_op jit(solution)/shard_map/all_to_all | solution.py:153

commit v8 on v7

--- a/solution.py
+++ b/solution.py
@@ -27,18 +27,6 @@
             block = block + lax.ppermute(block, axis, route)
             distance *= 2
     return block
-
-
-def neighbour_blocks(features, reach_size):
-    blocks = {0: features}
-    ahead_block = features
-    behind_block = features
-    for offset in range(1, reach_size + 1):
-        ahead_block = from_behind(ahead_block, "team", -1)
-        behind_block = from_behind(behind_block, "team", 1)
-        blocks[offset] = ahead_block
-        blocks[-offset] = behind_block
-    return blocks
 
 
 def layer_kernel(coords_ref, counts_ref, order_ref, *refs, section_count, slot_count, panel_dev, tile_size):
@@ -185,7 +173,7 @@
 
 
 def body(features, weight, out_grad, tiles, coords, counts):
-    panel_dev, section_count, slot_count, tile_size, _ = tiles.shape
+    _, section_count, _, _, _ = tiles.shape
     team_rows, feature_width = features.shape
     reach_size = (section_count - 1) // 2
     nodes_total = team_rows * lax.axis_size("team")
@@ -245,6 +233,7 @@
         P(("team", "rep"), None, None),
         P(("team", "rep"), None),
     )
+
     return jax.shard_map(
         body,
         mesh=mesh,

time: 119 us -> 119 us (level)
  no operation moved by 1% of the time
where the time goes in v8:
time: 119 us; the launch traced here: 118 us
  starting transfers between devices  59.8 us (50%)
  waiting for transfers between devices  44.8 us (38%)
  other arithmetic  4.57 us (4%)
  Pallas kernels  4.5 us (4%)
  local copies, waits for them, and re-layouts  3.61 us (3%)
    ppermute x4, starting transfers between devices, from_behind(): return lax.ppermute(block, axis, route)  22.7 us
    ppermute x2, starting transfers between devices, gather_sources(): fetched.append(lax.ppermute(features, ('team', 'rep'), route))  18 us
    all_to_all x1, waiting for transfers between devices, team_scatter_sum(): lax.all_to_all(block.reshape(size, rows // size, -1), 'team', 0, 0, tiled...  15.1 us
    all_to_all x1, waiting for transfers between devices, team_gather(): gathered = lax.all_to_all(copies, 'team', 0, 0, tiled=True)  14.6 us
    ppermute x3, waiting for transfers between devices, swap_with(): return lax.ppermute(block, axis, route)  8.98 us
    ppermute x3, starting transfers between devices, swap_with(): return lax.ppermute(block, axis, route)  6.77 us
    all_to_all x1, starting transfers between devices, team_scatter_sum(): lax.all_to_all(block.reshape(size, rows // size, -1), 'team', 0, 0, tiled...  6.15 us
    all_to_all x1, starting transfers between devices, team_gather(): gathered = lax.all_to_all(copies, 'team', 0, 0, tiled=True)  6.15 us
  transfers between devices with their start and end apart: 11, of which 7 were waited for; matrix products, arithmetic and copies ran while one was open for 3% of the time, Pallas kernels for 0%

profile of v8, /device:TPU:4, one launch (start us, length us, event | category | flops | bytes accessed | tf_op | source)
XLA Modules:
  0.0 118.1 jit_solution(8614638647991846610)
XLA Ops:
  0.7 14.6 %collective-permute-start = (bf16[1024,128]{1,0:T(8,128)(2,1)}, bf16[1024,128]{1,0:T(8,128)(2,1)S(1)}, u32[]{:S(2)}, u32[]{:S(2)}) collective-permute-start(bf16[1024,128]{1,0:T(8,128)(2,1)} %refs_0_.1), channel_id=1, source_target_pairs={{4,0},{509,1},{6,2},{511,3},{8,4},{1,5},{10,6},{3,7},{12,8},{5,9},... | collective-permute-start | bytes 786440 | tf_op jit(solution)/shard_map/ppermute | solution.py:165
  15.3 3.4 %collective-permute-start.1 = (bf16[1024,128]{1,0:T(8,128)(2,1)}, bf16[1024,128]{1,0:T(8,128)(2,1)S(1)}, u32[]{:S(2)}, u32[]{:S(2)}) collective-permute-start(bf16[1024,128]{1,0:T(8,128)(2,1)} %refs_0_.1), channel_id=1, source_target_pairs={{8,0},{505,1},{10,2},{507,3},{12,4},{509,5},{14,6},{511,7},{16,8},... | collective-permute-start | bytes 786440 | tf_op jit(solution)/shard_map/ppermute | solution.py:165
  18.7 0.8 collective-permute-done.refs_1_
  19.5 5.3 %collective-permute-done.1.refs_2_ = bf16[1024,128]{1,0:T(8,128)(2,1)S(1)} collective-permute-done((bf16[1024,128]{1,0:T(8,128)(2,1)}, bf16[1024,128]{1,0:T(8,128)(2,1)S(1)}, u32[]{:S(2)}, u32[]{:S(2)}) %collective-permute-start.1) | collective-permute-done | bytes 262176 | tf_op jit(solution)/shard_map/ppermute | solution.py:165
  24.8 1.9 %collective-permute-start.2 = (bf16[2,1024,128]{2,1,0:T(8,128)(2,1)S(1)}, bf16[2,1024,128]{2,1,0:T(8,128)(2,1)S(1)}, u32[]{:S(2)}, u32[]{:S(2)}) collective-permute-start(bf16[2,1024,128]{2,1,0:T(8,128)(2,1)S(1)} %pad_maximum_fusion.1), channel_id=1, source_target_pairs={{0,1},{1,0},{2,3},{3,2},{4,5},{5,4},{6,7},{7,6},{8,9},{9,8},{10,11... | collective-permute-start | bytes 1572872 | tf_op jit(solution)/shard_map/ppermute | solution.py:128
  26.8 0.8 reshape.44.counts_ref
  27.5 0.7 copy.12
  28.7 4.5 %shard_map.94 = (bf16[256,128]{1,0:T(8,128)(2,1)}, f32[128,128]{1,0:T(8,128)S(1)}, f32[5,1024,128]{2,1,0:T(8,128)S(1)}) custom-call(s32[80]{0:T(128)S(1)} %reshape.43.coords_ref, s32[10]{0:T(128)S(1)} %reshape.44.counts_ref, s32[5]{0:T(128)S(1)} %pad_add_fusion.order_ref, bf16[1024,128]{1,0:T(8,128)(2,1)S(1)} %copy-done, ...), custom_call_target="tpu_custom_call" | custom-call | flops 704643072 | bytes 6553600 | tf_op jit(solution)/shard_map/pallas_call | solution.py:107
  33.4 1.2 pad_maximum_fusion
  34.6 2.2 %collective-permute-start.3 = (f32[2688,128]{1,0:T(8,128)}, f32[2688,128]{1,0:T(8,128)S(1)}, u32[]{:S(2)}, u32[]{:S(2)}) collective-permute-start(f32[2688,128]{1,0:T(8,128)} %pad_maximum_fusion), channel_id=1, source_target_pairs={{0,1},{1,0},{2,3},{3,2},{4,5},{5,4},{6,7},{7,6},{8,9},{9,8},{10,11... | collective-permute-start | bytes 4128776 | tf_op jit(solution)/shard_map/ppermute | solution.py:128
  36.8 3.0 %collective-permute-done.3 = f32[2688,128]{1,0:T(8,128)S(1)} collective-permute-done((f32[2688,128]{1,0:T(8,128)}, f32[2688,128]{1,0:T(8,128)S(1)}, u32[]{:S(2)}, u32[]{:S(2)}) %collective-permute-start.3) | collective-permute-done | bytes 1376288 | tf_op jit(solution)/shard_map/ppermute | solution.py:128
  39.9 1.0 copy-done.3
  41.1 8.0 %collective-permute-start.4 = (bf16[512,128]{1,0:T(8,128)(2,1)S(1)}, bf16[512,128]{1,0:T(8,128)(2,1)S(1)}, u32[]{:S(2)}, u32[]{:S(2)}) collective-permute-start(bf16[512,128]{1,0:T(8,128)(2,1)S(1)} %get-tuple-element.13), channel_id=1, source_target_pairs={{8,0},{12,4},{16,8},{20,12},{24,16},{28,20},{32,24},{36,28},{40,32... | collective-permute-start | bytes 393224 | tf_op jit(solution)/shard_map/ppermute | solution.py:15
  49.2 1.9 %collective-permute-start.7 = (bf16[512,128]{1,0:T(8,128)(2,1)S(1)}, bf16[512,128]{1,0:T(8,128)(2,1)S(1)}, u32[]{:S(2)}, u32[]{:S(2)}) collective-permute-start(bf16[512,128]{1,0:T(8,128)(2,1)S(1)} %get-tuple-element.14), channel_id=1, source_target_pairs={{504,0},{508,4},{0,8},{4,12},{8,16},{12,20},{16,24},{20,28},{24,32... | collective-permute-start | bytes 393224 | tf_op jit(solution)/shard_map/ppermute | solution.py:15
  51.1 5.2 %collective-permute-start.6 = (bf16[512,128]{1,0:T(8,128)(2,1)S(1)}, bf16[512,128]{1,0:T(8,128)(2,1)S(1)}, u32[]{:S(2)}, u32[]{:S(2)}) collective-permute-start(bf16[512,128]{1,0:T(8,128)(2,1)S(1)} %get-tuple-element.15), channel_id=1, source_target_pairs={{508,0},{0,4},{4,8},{8,12},{12,16},{16,20},{20,24},{24,28},{28,32}... | collective-permute-start | bytes 393224 | tf_op jit(solution)/shard_map/ppermute | solution.py:15
  56.3 7.6 %collective-permute-start.5 = (bf16[512,128]{1,0:T(8,128)(2,1)S(1)}, bf16[512,128]{1,0:T(8,128)(2,1)S(1)}, u32[]{:S(2)}, u32[]{:S(2)}) collective-permute-start(bf16[512,128]{1,0:T(8,128)(2,1)S(1)} %get-tuple-element.16), channel_id=1, source_target_pairs={{4,0},{8,4},{12,8},{16,12},{20,16},{24,20},{28,24},{32,28},{36,32}... | collective-permute-start | bytes 393224 | tf_op jit(solution)/shard_map/ppermute | solution.py:15
  63.9 1.5 %slice_add_fusion.1 = f32[128,128]{1,0:T(8,128)} fusion(f32[128,128]{1,0:T(8,128)S(1)} %get-tuple-element.7, f32[2688,128]{1,0:T(8,128)} %copy-done.3), kind=kLoop, calls=%fused_computation.18 | loop fusion | flops 16384 | bytes 196608 | tf_op jit(solution)/shard_map/add | solution.py:210
  65.4 6.1 %all-to-all-start = ((f32[128,1,128]{2,1,0:T(1,128)}), f32[128,1,128]{2,1,0:T(1,128)S(1)}, u32[]{:S(2)}, u32[]{:S(2)}) async-start(f32[128,1,128]{2,1,0:T(1,128)} %bitcast.7), calls=%async_computation | async-start | bytes 131072 | tf_op jit(solution)/shard_map/all_to_all | solution.py:134
  71.7 15.1 %all-to-all-done = f32[128,1,128]{2,1,0:T(1,128)S(1)} async-done(((f32[128,1,128]{2,1,0:T(1,128)}), f32[128,1,128]{2,1,0:T(1,128)S(1)}, u32[]{:S(2)}, u32[]{:S(2)}) %all-to-all-start) | async-done | bytes 65568 | tf_op jit(solution)/shard_map/all_to_all | solution.py:134
  86.9 2.7 %collective-permute-start.8 = (f32[257,128]{1,0:T(8,128)S(1)}, f32[257,128]{1,0:T(8,128)S(1)}, u32[]{:S(2)}, u32[]{:S(2)}) collective-permute-start(f32[257,128]{1,0:T(8,128)S(1)} %pad_maximum_fusion.2), channel_id=1, source_target_pairs={{0,2},{1,3},{2,0},{3,1},{4,6},{5,7},{6,4},{7,5},{8,10},{9,11},{10,... | collective-permute-start | bytes 394760 | tf_op jit(solution)/shard_map/ppermute | solution.py:128
  89.6 5.7 %collective-permute-done.8 = f32[257,128]{1,0:T(8,128)S(1)} collective-permute-done((f32[257,128]{1,0:T(8,128)S(1)}, f32[257,128]{1,0:T(8,128)S(1)}, u32[]{:S(2)}, u32[]{:S(2)}) %collective-permute-start.8) | collective-permute-done | bytes 131616 | tf_op jit(solution)/shard_map/ppermute | solution.py:128
  96.0 6.1 %all-to-all-start.1 = ((f32[128,1,128]{2,1,0:T(1,128)}), f32[128,1,128]{2,1,0:T(1,128)S(1)}, u32[]{:S(2)}, u32[]{:S(2)}) async-start(f32[128,1,128]{2,1,0:T(1,128)} %broadcast_in_dim.9), calls=%async_computation.1 | async-start | bytes 131072 | tf_op jit(solution)/shard_map/all_to_all | solution.py:141
  102.8 14.6 %all-to-all-done.1 = f32[128,1,128]{2,1,0:T(1,128)S(1)} async-done(((f32[128,1,128]{2,1,0:T(1,128)}), f32[128,1,128]{2,1,0:T(1,128)S(1)}, u32[]{:S(2)}, u32[]{:S(2)}) %all-to-all-start.1) | async-done | bytes 65568 | tf_op jit(solution)/shard_map/all_to_all | solution.py:141
  117.4 0.7 broadcast_multiply_fusion
  (28 shorter events, 2.6 us)
Async XLA Ops:
  0.6 28.0 %copy-start = (bf16[1024,128]{1,0:T(8,128)(2,1)S(1)}, bf16[1024,128]{1,0:T(8,128)(2,1)}, u32[]{:S(2)}) copy-start(bf16[1024,128]{1,0:T(8,128)(2,1)} %refs_0_.1) | copy-start | bytes 786436
  0.6 28.0 %copy-start.1 = (bf16[256,128]{1,0:T(8,128)(2,1)S(1)}, bf16[256,128]{1,0:T(8,128)(2,1)}, u32[]{:S(2)}) copy-start(bf16[256,128]{1,0:T(8,128)(2,1)} %refs_6_.1) | copy-start | bytes 196612
  0.7 28.0 %copy-start.2 = (bf16[128,128]{1,0:T(8,128)(2,1)S(1)}, bf16[128,128]{1,0:T(8,128)(2,1)}, u32[]{:S(2)}) copy-start(bf16[128,128]{1,0:T(8,128)(2,1)} %refs_7_.1) | copy-start | bytes 98308
  0.7 18.8 %collective-permute-start = (bf16[1024,128]{1,0:T(8,128)(2,1)}, bf16[1024,128]{1,0:T(8,128)(2,1)S(1)}, u32[]{:S(2)}, u32[]{:S(2)}) collective-permute-start(bf16[1024,128]{1,0:T(8,128)(2,1)} %refs_0_.1), channel_id=1, source_target_pairs={{4,0},{509,1},{6,2},{511,3},{8,4},{1,5},{10,6},{3,7},{12,8},{5,9},... | collective-permute-start | bytes 786440 | tf_op jit(solution)/shard_map/ppermute | solution.py:165
  15.3 9.5 %collective-permute-start.1 = (bf16[1024,128]{1,0:T(8,128)(2,1)}, bf16[1024,128]{1,0:T(8,128)(2,1)S(1)}, u32[]{:S(2)}, u32[]{:S(2)}) collective-permute-start(bf16[1024,128]{1,0:T(8,128)(2,1)} %refs_0_.1), channel_id=1, source_target_pairs={{8,0},{505,1},{10,2},{507,3},{12,4},{509,5},{14,6},{511,7},{16,8},... | collective-permute-start | bytes 786440 | tf_op jit(solution)/shard_map/ppermute | solution.py:165
  24.8 3.8 %collective-permute-start.2 = (bf16[2,1024,128]{2,1,0:T(8,128)(2,1)S(1)}, bf16[2,1024,128]{2,1,0:T(8,128)(2,1)S(1)}, u32[]{:S(2)}, u32[]{:S(2)}) collective-permute-start(bf16[2,1024,128]{2,1,0:T(8,128)(2,1)S(1)} %pad_maximum_fusion.1), channel_id=1, source_target_pairs={{0,1},{1,0},{2,3},{3,2},{4,5},{5,4},{6,7},{7,6},{8,9},{9,8},{10,11... | collective-permute-start | bytes 1572872 | tf_op jit(solution)/shard_map/ppermute | solution.py:128
  34.6 5.2 %collective-permute-start.3 = (f32[2688,128]{1,0:T(8,128)}, f32[2688,128]{1,0:T(8,128)S(1)}, u32[]{:S(2)}, u32[]{:S(2)}) collective-permute-start(f32[2688,128]{1,0:T(8,128)} %pad_maximum_fusion), channel_id=1, source_target_pairs={{0,1},{1,0},{2,3},{3,2},{4,5},{5,4},{6,7},{7,6},{8,9},{9,8},{10,11... | collective-permute-start | bytes 4128776 | tf_op jit(solution)/shard_map/ppermute | solution.py:128
  39.8 1.1 copy-start.3
  41.1 30.4 %collective-permute-start.4 = (bf16[512,128]{1,0:T(8,128)(2,1)S(1)}, bf16[512,128]{1,0:T(8,128)(2,1)S(1)}, u32[]{:S(2)}, u32[]{:S(2)}) collective-permute-start(bf16[512,128]{1,0:T(8,128)(2,1)S(1)} %get-tuple-element.13), channel_id=1, source_target_pairs={{8,0},{12,4},{16,8},{20,12},{24,16},{28,20},{32,24},{36,28},{40,32... | collective-permute-start | bytes 393224 | tf_op jit(solution)/shard_map/ppermute | solution.py:15
  49.2 22.4 %collective-permute-start.7 = (bf16[512,128]{1,0:T(8,128)(2,1)S(1)}, bf16[512,128]{1,0:T(8,128)(2,1)S(1)}, u32[]{:S(2)}, u32[]{:S(2)}) collective-permute-start(bf16[512,128]{1,0:T(8,128)(2,1)S(1)} %get-tuple-element.14), channel_id=1, source_target_pairs={{504,0},{508,4},{0,8},{4,12},{8,16},{12,20},{16,24},{20,28},{24,32... | collective-permute-start | bytes 393224 | tf_op jit(solution)/shard_map/ppermute | solution.py:15
  51.1 20.4 %collective-permute-start.6 = (bf16[512,128]{1,0:T(8,128)(2,1)S(1)}, bf16[512,128]{1,0:T(8,128)(2,1)S(1)}, u32[]{:S(2)}, u32[]{:S(2)}) collective-permute-start(bf16[512,128]{1,0:T(8,128)(2,1)S(1)} %get-tuple-element.15), channel_id=1, source_target_pairs={{508,0},{0,4},{4,8},{8,12},{12,16},{16,20},{20,24},{24,28},{28,32}... | collective-permute-start | bytes 393224 | tf_op jit(solution)/shard_map/ppermute | solution.py:15
  56.3 15.3 %collective-permute-start.5 = (bf16[512,128]{1,0:T(8,128)(2,1)S(1)}, bf16[512,128]{1,0:T(8,128)(2,1)S(1)}, u32[]{:S(2)}, u32[]{:S(2)}) collective-permute-start(bf16[512,128]{1,0:T(8,128)(2,1)S(1)} %get-tuple-element.16), channel_id=1, source_target_pairs={{4,0},{8,4},{12,8},{16,12},{20,16},{24,20},{28,24},{32,28},{36,32}... | collective-permute-start | bytes 393224 | tf_op jit(solution)/shard_map/ppermute | solution.py:15
  65.4 21.4 %all-to-all-start = ((f32[128,1,128]{2,1,0:T(1,128)}), f32[128,1,128]{2,1,0:T(1,128)S(1)}, u32[]{:S(2)}, u32[]{:S(2)}) async-start(f32[128,1,128]{2,1,0:T(1,128)} %bitcast.7), calls=%async_computation | async-start | bytes 131072 | tf_op jit(solution)/shard_map/all_to_all | solution.py:134
  86.9 8.4 %collective-permute-start.8 = (f32[257,128]{1,0:T(8,128)S(1)}, f32[257,128]{1,0:T(8,128)S(1)}, u32[]{:S(2)}, u32[]{:S(2)}) collective-permute-start(f32[257,128]{1,0:T(8,128)S(1)} %pad_maximum_fusion.2), channel_id=1, source_target_pairs={{0,2},{1,3},{2,0},{3,1},{4,6},{5,7},{6,4},{7,5},{8,10},{9,11},{10,... | collective-permute-start | bytes 394760 | tf_op jit(solution)/shard_map/ppermute | solution.py:128
  96.0 21.4 %all-to-all-start.1 = ((f32[128,1,128]{2,1,0:T(1,128)}), f32[128,1,128]{2,1,0:T(1,128)S(1)}, u32[]{:S(2)}, u32[]{:S(2)}) async-start(f32[128,1,128]{2,1,0:T(1,128)} %broadcast_in_dim.9), calls=%async_computation.1 | async-start | bytes 131072 | tf_op jit(solution)/shard_map/all_to_all | solution.py:141

commit v9 on v8

--- a/solution.py
+++ b/solution.py
@@ -208,9 +208,10 @@
         : section_count * half_rows
     ].reshape(section_count, half_rows, feature_width)
     weight_grad = team_scatter_sum(local_weight_grad + arrived[section_count * half_rows :])
+    weight_grad = team_gather(weight_grad)
 
     total = kept[reach_size]
-    for s in range(section_count):
+    for s in sorted(range(section_count), key=lambda s: -abs(s - reach_size)):
         if s != reach_size:
             moved = from_behind(kept[s].astype(jnp.bfloat16), "team", s - reach_size)
             total = total + moved.astype(jnp.float32)
@@ -220,7 +221,7 @@
     sent = lax.dynamic_index_in_dim(staged, 1 - chip_bit, 0, keepdims=False)
     arrived = swap_with(jnp.concatenate([sent, weight_grad], axis=0), "rep", 2)
     gradient_share = (kept + arrived[:quarter]).astype(jnp.bfloat16)
-    grad_weight = team_gather(weight_grad + arrived[quarter:]) * (1.0 / math.sqrt(nodes_total))
+    grad_weight = (weight_grad + arrived[quarter:]) * (1.0 / math.sqrt(nodes_total))
     return (activated, grad_weight, gradient_share)
 
 

time: 119 us -> 110 us (0.924)
  waiting for transfers between devices: 44.8 us -> 30.7 us
  starting transfers between devices: 59.8 us -> 67.9 us
  other arithmetic: 4.57 us -> 2.58 us
    all_to_all x1, waiting for transfers between devices: 15.1 us -> 0.01 us  [team_scatter_sum(): lax.all_to_all(block.reshape(size, rows // size, -1), 'team', 0, 0, tiled...]
    all_to_all x1, starting transfers between devices: 6.15 us -> 11.6 us  [team_scatter_sum(): lax.all_to_all(block.reshape(size, rows // size, -1), 'team', 0, 0, tiled...]
    all_to_all x1, starting transfers between devices: 6.15 us -> 10.6 us  [team_gather(): gathered = lax.all_to_all(copies, 'team', 0, 0, tiled=True)]
    ppermute x4, starting transfers between devices: 22.7 us -> 20.9 us  [from_behind(): return lax.ppermute(block, axis, route)]
  transfers between devices with their start and end apart: 11 -> 11, of which waited for: 7 -> 6; matrix products, arithmetic and copies ran while one was open for 3% -> 3% of each run, Pallas kernels for 0% -> 0%
where the time goes in v9:
time: 110 us; the launch traced here: 109 us
  starting transfers between devices  67.9 us (62%)
  waiting for transfers between devices  30.7 us (28%)
  Pallas kernels  4.5 us (4%)
  local copies, waits for them, and re-layouts  2.58 us (2%)
  other arithmetic  2.58 us (2%)
    ppermute x4, starting transfers between devices, from_behind(): return lax.ppermute(block, axis, route)  20.9 us
    ppermute x2, starting transfers between devices, gather_sources(): fetched.append(lax.ppermute(features, ('team', 'rep'), route))  18 us
    all_to_all x1, waiting for transfers between devices, team_gather(): gathered = lax.all_to_all(copies, 'team', 0, 0, tiled=True)  15.1 us
    all_to_all x1, starting transfers between devices, team_scatter_sum(): lax.all_to_all(block.reshape(size, rows // size, -1), 'team', 0, 0, tiled...  11.6 us
    all_to_all x1, starting transfers between devices, team_gather(): gathered = lax.all_to_all(copies, 'team', 0, 0, tiled=True)  10.6 us
    ppermute x3, waiting for transfers between devices, swap_with(): return lax.ppermute(block, axis, route)  9.43 us
    ppermute x3, starting transfers between devices, swap_with(): return lax.ppermute(block, axis, route)  6.79 us
    ppermute x2, waiting for transfers between devices, gather_sources(): fetched.append(lax.ppermute(features, ('team', 'rep'), route))  6.11 us
  transfers between devices with their start and end apart: 11, of which 6 were waited for; matrix products, arithmetic and copies ran while one was open for 3% of the time, Pallas kernels for 0%

profile of v9, /device:TPU:4, one launch (start us, length us, event | category | flops | bytes accessed | tf_op | source)
XLA Modules:
  0.0 109.2 jit_solution(13206683700365405100)
XLA Ops:
  0.7 14.6 %collective-permute-start = (bf16[1024,128]{1,0:T(8,128)(2,1)}, bf16[1024,128]{1,0:T(8,128)(2,1)S(1)}, u32[]{:S(2)}, u32[]{:S(2)}) collective-permute-start(bf16[1024,128]{1,0:T(8,128)(2,1)} %refs_0_.1), channel_id=1, source_target_pairs={{4,0},{509,1},{6,2},{511,3},{8,4},{1,5},{10,6},{3,7},{12,8},{5,9},... | collective-permute-start | bytes 786440 | tf_op jit(solution)/shard_map/ppermute | solution.py:165
  15.3 3.4 %collective-permute-start.1 = (bf16[1024,128]{1,0:T(8,128)(2,1)}, bf16[1024,128]{1,0:T(8,128)(2,1)S(1)}, u32[]{:S(2)}, u32[]{:S(2)}) collective-permute-start(bf16[1024,128]{1,0:T(8,128)(2,1)} %refs_0_.1), channel_id=1, source_target_pairs={{8,0},{505,1},{10,2},{507,3},{12,4},{509,5},{14,6},{511,7},{16,8},... | collective-permute-start | bytes 786440 | tf_op jit(solution)/shard_map/ppermute | solution.py:165
  18.7 0.8 collective-permute-done.refs_1_
  19.5 5.3 %collective-permute-done.1.refs_2_ = bf16[1024,128]{1,0:T(8,128)(2,1)S(1)} collective-permute-done((bf16[1024,128]{1,0:T(8,128)(2,1)}, bf16[1024,128]{1,0:T(8,128)(2,1)S(1)}, u32[]{:S(2)}, u32[]{:S(2)}) %collective-permute-start.1) | collective-permute-done | bytes 262176 | tf_op jit(solution)/shard_map/ppermute | solution.py:165
  24.8 1.9 %collective-permute-start.2 = (bf16[2,1024,128]{2,1,0:T(8,128)(2,1)S(1)}, bf16[2,1024,128]{2,1,0:T(8,128)(2,1)S(1)}, u32[]{:S(2)}, u32[]{:S(2)}) collective-permute-start(bf16[2,1024,128]{2,1,0:T(8,128)(2,1)S(1)} %pad_maximum_fusion.1), channel_id=1, source_target_pairs={{0,1},{1,0},{2,3},{3,2},{4,5},{5,4},{6,7},{7,6},{8,9},{9,8},{10,11... | collective-permute-start | bytes 1572872 | tf_op jit(solution)/shard_map/ppermute | solution.py:128
  26.8 0.8 reshape.45.counts_ref
  27.5 0.7 copy.12
  28.4 0.2 collective-permute-done.2
  28.7 4.5 %shard_map.94 = (bf16[256,128]{1,0:T(8,128)(2,1)}, f32[128,128]{1,0:T(8,128)S(1)}, f32[5,1024,128]{2,1,0:T(8,128)S(1)}) custom-call(s32[80]{0:T(128)S(1)} %reshape.44.coords_ref, s32[10]{0:T(128)S(1)} %reshape.45.counts_ref, s32[5]{0:T(128)S(1)} %pad_add_fusion.order_ref, bf16[1024,128]{1,0:T(8,128)(2,1)S(1)} %copy-done, ...), custom_call_target="tpu_custom_call" | custom-call | flops 704643072 | bytes 6553600 | tf_op jit(solution)/shard_map/pallas_call | solution.py:107
  33.5 2.2 %collective-permute-start.3 = (f32[2688,128]{1,0:T(8,128)S(1)}, f32[2688,128]{1,0:T(8,128)S(1)}, u32[]{:S(2)}, u32[]{:S(2)}) collective-permute-start(f32[2688,128]{1,0:T(8,128)S(1)} %pad_maximum_fusion), channel_id=1, source_target_pairs={{0,1},{1,0},{2,3},{3,2},{4,5},{5,4},{6,7},{7,6},{8,9},{9,8},{10,11... | collective-permute-start | bytes 4128776 | tf_op jit(solution)/shard_map/ppermute | solution.py:128
  35.7 2.8 %collective-permute-done.3 = f32[2688,128]{1,0:T(8,128)S(1)} collective-permute-done((f32[2688,128]{1,0:T(8,128)S(1)}, f32[2688,128]{1,0:T(8,128)S(1)}, u32[]{:S(2)}, u32[]{:S(2)}) %collective-permute-start.3) | collective-permute-done | bytes 1376288 | tf_op jit(solution)/shard_map/ppermute | solution.py:128
  38.5 0.6 slice_add_fusion.2
  39.1 11.6 %all-to-all-start = ((f32[128,1,128]{2,1,0:T(1,128)}), f32[128,1,128]{2,1,0:T(1,128)S(1)}, u32[]{:S(2)}, u32[]{:S(2)}) async-start(f32[128,1,128]{2,1,0:T(1,128)} %bitcast.7), calls=%async_computation | async-start | bytes 131072 | tf_op jit(solution)/shard_map/all_to_all | solution.py:134
  51.1 8.9 %collective-permute-start.4 = (bf16[512,128]{1,0:T(8,128)(2,1)S(1)}, bf16[512,128]{1,0:T(8,128)(2,1)S(1)}, u32[]{:S(2)}, u32[]{:S(2)}) collective-permute-start(bf16[512,128]{1,0:T(8,128)(2,1)S(1)} %get-tuple-element.13), channel_id=1, source_target_pairs={{8,0},{12,4},{16,8},{20,12},{24,16},{28,20},{32,24},{36,28},{40,32... | collective-permute-start | bytes 393224 | tf_op jit(solution)/shard_map/ppermute | solution.py:15
  60.0 2.5 %collective-permute-start.7 = (bf16[512,128]{1,0:T(8,128)(2,1)S(1)}, bf16[512,128]{1,0:T(8,128)(2,1)S(1)}, u32[]{:S(2)}, u32[]{:S(2)}) collective-permute-start(bf16[512,128]{1,0:T(8,128)(2,1)S(1)} %get-tuple-element.14), channel_id=1, source_target_pairs={{508,0},{0,4},{4,8},{8,12},{12,16},{16,20},{20,24},{24,28},{28,32}... | collective-permute-start | bytes 393224 | tf_op jit(solution)/shard_map/ppermute | solution.py:15
  62.5 7.6 %collective-permute-start.6 = (bf16[512,128]{1,0:T(8,128)(2,1)S(1)}, bf16[512,128]{1,0:T(8,128)(2,1)S(1)}, u32[]{:S(2)}, u32[]{:S(2)}) collective-permute-start(bf16[512,128]{1,0:T(8,128)(2,1)S(1)} %get-tuple-element.15), channel_id=1, source_target_pairs={{4,0},{8,4},{12,8},{16,12},{20,16},{24,20},{28,24},{32,28},{36,32}... | collective-permute-start | bytes 393224 | tf_op jit(solution)/shard_map/ppermute | solution.py:15
  70.1 1.9 %collective-permute-start.5 = (bf16[512,128]{1,0:T(8,128)(2,1)S(1)}, bf16[512,128]{1,0:T(8,128)(2,1)S(1)}, u32[]{:S(2)}, u32[]{:S(2)}) collective-permute-start(bf16[512,128]{1,0:T(8,128)(2,1)S(1)} %get-tuple-element.16), channel_id=1, source_target_pairs={{504,0},{508,4},{0,8},{4,12},{8,16},{12,20},{16,24},{20,28},{24,32... | collective-permute-start | bytes 393224 | tf_op jit(solution)/shard_map/ppermute | solution.py:15
  72.2 0.7 broadcast_in_dim.2
  72.9 10.6 %all-to-all-start.1 = ((f32[128,1,128]{2,1,0:T(1,128)}), f32[128,1,128]{2,1,0:T(1,128)S(1)}, u32[]{:S(2)}, u32[]{:S(2)}) async-start(f32[128,1,128]{2,1,0:T(1,128)} %broadcast_in_dim.2), calls=%async_computation.1 | async-start | bytes 131072 | tf_op jit(solution)/shard_map/all_to_all | solution.py:141
  83.7 15.1 %all-to-all-done.1 = f32[128,1,128]{2,1,0:T(1,128)S(1)} async-done(((f32[128,1,128]{2,1,0:T(1,128)}), f32[128,1,128]{2,1,0:T(1,128)S(1)}, u32[]{:S(2)}, u32[]{:S(2)}) %all-to-all-start.1) | async-done | bytes 65568 | tf_op jit(solution)/shard_map/all_to_all | solution.py:141
  98.8 2.7 %collective-permute-start.8 = (f32[384,128]{1,0:T(8,128)S(1)}, f32[384,128]{1,0:T(8,128)S(1)}, u32[]{:S(2)}, u32[]{:S(2)}) collective-permute-start(f32[384,128]{1,0:T(8,128)S(1)} %pad_maximum_fusion.2), channel_id=1, source_target_pairs={{0,2},{1,3},{2,0},{3,1},{4,6},{5,7},{6,4},{7,5},{8,10},{9,11},{10,... | collective-permute-start | bytes 589832 | tf_op jit(solution)/shard_map/ppermute | solution.py:128
  101.5 6.4 %collective-permute-done.8 = f32[384,128]{1,0:T(8,128)S(1)} collective-permute-done((f32[384,128]{1,0:T(8,128)S(1)}, f32[384,128]{1,0:T(8,128)S(1)}, u32[]{:S(2)}, u32[]{:S(2)}) %collective-permute-start.8) | collective-permute-done | bytes 196640 | tf_op jit(solution)/shard_map/ppermute | solution.py:128
  107.9 0.6 fusion.5
  108.5 0.6 fusion.4
  (25 shorter events, 1.1 us)
Async XLA Ops:
  0.6 28.0 %copy-start = (bf16[1024,128]{1,0:T(8,128)(2,1)S(1)}, bf16[1024,128]{1,0:T(8,128)(2,1)}, u32[]{:S(2)}) copy-start(bf16[1024,128]{1,0:T(8,128)(2,1)} %refs_0_.1) | copy-start | bytes 786436
  0.6 28.0 %copy-start.1 = (bf16[256,128]{1,0:T(8,128)(2,1)S(1)}, bf16[256,128]{1,0:T(8,128)(2,1)}, u32[]{:S(2)}) copy-start(bf16[256,128]{1,0:T(8,128)(2,1)} %refs_6_.1) | copy-start | bytes 196612
  0.7 28.0 %copy-start.2 = (bf16[128,128]{1,0:T(8,128)(2,1)S(1)}, bf16[128,128]{1,0:T(8,128)(2,1)}, u32[]{:S(2)}) copy-start(bf16[128,128]{1,0:T(8,128)(2,1)} %refs_7_.1) | copy-start | bytes 98308
  0.7 18.8 %collective-permute-start = (bf16[1024,128]{1,0:T(8,128)(2,1)}, bf16[1024,128]{1,0:T(8,128)(2,1)S(1)}, u32[]{:S(2)}, u32[]{:S(2)}) collective-permute-start(bf16[1024,128]{1,0:T(8,128)(2,1)} %refs_0_.1), channel_id=1, source_target_pairs={{4,0},{509,1},{6,2},{511,3},{8,4},{1,5},{10,6},{3,7},{12,8},{5,9},... | collective-permute-start | bytes 786440 | tf_op jit(solution)/shard_map/ppermute | solution.py:165
  15.3 9.5 %collective-permute-start.1 = (bf16[1024,128]{1,0:T(8,128)(2,1)}, bf16[1024,128]{1,0:T(8,128)(2,1)S(1)}, u32[]{:S(2)}, u32[]{:S(2)}) collective-permute-start(bf16[1024,128]{1,0:T(8,128)(2,1)} %refs_0_.1), channel_id=1, source_target_pairs={{8,0},{505,1},{10,2},{507,3},{12,4},{509,5},{14,6},{511,7},{16,8},... | collective-permute-start | bytes 786440 | tf_op jit(solution)/shard_map/ppermute | solution.py:165
  24.8 3.8 %collective-permute-start.2 = (bf16[2,1024,128]{2,1,0:T(8,128)(2,1)S(1)}, bf16[2,1024,128]{2,1,0:T(8,128)(2,1)S(1)}, u32[]{:S(2)}, u32[]{:S(2)}) collective-permute-start(bf16[2,1024,128]{2,1,0:T(8,128)(2,1)S(1)} %pad_maximum_fusion.1), channel_id=1, source_target_pairs={{0,1},{1,0},{2,3},{3,2},{4,5},{5,4},{6,7},{7,6},{8,9},{9,8},{10,11... | collective-permute-start | bytes 1572872 | tf_op jit(solution)/shard_map/ppermute | solution.py:128
  33.5 5.0 %collective-permute-start.3 = (f32[2688,128]{1,0:T(8,128)S(1)}, f32[2688,128]{1,0:T(8,128)S(1)}, u32[]{:S(2)}, u32[]{:S(2)}) collective-permute-start(f32[2688,128]{1,0:T(8,128)S(1)} %pad_maximum_fusion), channel_id=1, source_target_pairs={{0,1},{1,0},{2,3},{3,2},{4,5},{5,4},{6,7},{7,6},{8,9},{9,8},{10,11... | collective-permute-start | bytes 4128776 | tf_op jit(solution)/shard_map/ppermute | solution.py:128
  39.1 32.9 %all-to-all-start = ((f32[128,1,128]{2,1,0:T(1,128)}), f32[128,1,128]{2,1,0:T(1,128)S(1)}, u32[]{:S(2)}, u32[]{:S(2)}) async-start(f32[128,1,128]{2,1,0:T(1,128)} %bitcast.7), calls=%async_computation | async-start | bytes 131072 | tf_op jit(solution)/shard_map/all_to_all | solution.py:134
  51.1 32.4 %collective-permute-start.4 = (bf16[512,128]{1,0:T(8,128)(2,1)S(1)}, bf16[512,128]{1,0:T(8,128)(2,1)S(1)}, u32[]{:S(2)}, u32[]{:S(2)}) collective-permute-start(bf16[512,128]{1,0:T(8,128)(2,1)S(1)} %get-tuple-element.13), channel_id=1, source_target_pairs={{8,0},{12,4},{16,8},{20,12},{24,16},{28,20},{32,24},{36,28},{40,32... | collective-permute-start | bytes 393224 | tf_op jit(solution)/shard_map/ppermute | solution.py:15
  60.0 23.5 %collective-permute-start.7 = (bf16[512,128]{1,0:T(8,128)(2,1)S(1)}, bf16[512,128]{1,0:T(8,128)(2,1)S(1)}, u32[]{:S(2)}, u32[]{:S(2)}) collective-permute-start(bf16[512,128]{1,0:T(8,128)(2,1)S(1)} %get-tuple-element.14), channel_id=1, source_target_pairs={{508,0},{0,4},{4,8},{8,12},{12,16},{16,20},{20,24},{24,28},{28,32}... | collective-permute-start | bytes 393224 | tf_op jit(solution)/shard_map/ppermute | solution.py:15
  62.5 21.0 %collective-permute-start.6 = (bf16[512,128]{1,0:T(8,128)(2,1)S(1)}, bf16[512,128]{1,0:T(8,128)(2,1)S(1)}, u32[]{:S(2)}, u32[]{:S(2)}) collective-permute-start(bf16[512,128]{1,0:T(8,128)(2,1)S(1)} %get-tuple-element.15), channel_id=1, source_target_pairs={{4,0},{8,4},{12,8},{16,12},{20,16},{24,20},{28,24},{32,28},{36,32}... | collective-permute-start | bytes 393224 | tf_op jit(solution)/shard_map/ppermute | solution.py:15
  70.1 13.5 %collective-permute-start.5 = (bf16[512,128]{1,0:T(8,128)(2,1)S(1)}, bf16[512,128]{1,0:T(8,128)(2,1)S(1)}, u32[]{:S(2)}, u32[]{:S(2)}) collective-permute-start(bf16[512,128]{1,0:T(8,128)(2,1)S(1)} %get-tuple-element.16), channel_id=1, source_target_pairs={{504,0},{508,4},{0,8},{4,12},{8,16},{12,20},{16,24},{20,28},{24,32... | collective-permute-start | bytes 393224 | tf_op jit(solution)/shard_map/ppermute | solution.py:15
  72.9 25.9 %all-to-all-start.1 = ((f32[128,1,128]{2,1,0:T(1,128)}), f32[128,1,128]{2,1,0:T(1,128)S(1)}, u32[]{:S(2)}, u32[]{:S(2)}) async-start(f32[128,1,128]{2,1,0:T(1,128)} %broadcast_in_dim.2), calls=%async_computation.1 | async-start | bytes 131072 | tf_op jit(solution)/shard_map/all_to_all | solution.py:141
  98.8 9.1 %collective-permute-start.8 = (f32[384,128]{1,0:T(8,128)S(1)}, f32[384,128]{1,0:T(8,128)S(1)}, u32[]{:S(2)}, u32[]{:S(2)}) collective-permute-start(f32[384,128]{1,0:T(8,128)S(1)} %pad_maximum_fusion.2), channel_id=1, source_target_pairs={{0,2},{1,3},{2,0},{3,1},{4,6},{5,7},{6,4},{7,5},{8,10},{9,11},{10,... | collective-permute-start | bytes 589832 | tf_op jit(solution)/shard_map/ppermute | solution.py:128
